TPU v7x, 32 devices: a whole 2x2x4 slice. The times are simulated.
32 devices in a mesh: trait: 4 (over y, x), tile: 8 (over z, core).
Axes of the slice: x: 2, y: 2, z: 4, core: 2. Of those that a mesh axis runs over, the one named last changes fastest.
Arguments:
- probe_signs: int32 [4, 16, 64, 2048], P(None, 'trait', 'tile'), may hold values from 0 to 1
- land_mask: int32 [64, 2048], P('tile'), may hold values from 0 to 1
- kappa_sq: float32 [64, 2048], P('tile'), may hold values from 0.2 to 4.5
- trait_covariance: float32 [16, 16], replicated, may hold values from -0.025 to 3, as said below
Outputs:
- alphas: float32 [4, 3], replicated
- betas: float32 [4, 3], replicated
- last_vector: float32 [4, 16, 64, 2048], P(None, 'trait', 'tile')
Inputs may be any that keep to these rules, and one draw needn't show every extreme that they name: `trait_covariance`: symmetric.
All inputs are finite; a program needn't handle non-finite values.
Results may differ from a plain program's by a relative error of at most 0.0003.
Values may be sent and summed in bfloat16 or wider, within the bound.
No kernel may reach another device: no remote copies, remote signals or barrier semaphores. Data moves between devices by JAX's collectives and lax.ppermute only.
A program may use at most 64 MiB of HBM per device.

v0:
```python
import jax
import jax.numpy as jnp
from jax import lax
from jax.sharding import PartitionSpec as P

PROBES = 4
ITERS = 3


along_cols = 0.25
along_rows = 0.15
cross_term = 0.1
epsilon = 1e-06


def extended(block, sides, width):
    for axis, dim in sides:
        count = lax.axis_size(axis)
        forward = [(i, i + 1) for i in range(count - 1)]
        backward = [(target, source) for source, target in forward]
        low = lax.ppermute(
            lax.slice_in_dim(block, block.shape[dim] - width, None, axis=dim), axis, forward
        )
        high = lax.ppermute(lax.slice_in_dim(block, 0, width, axis=dim), axis, backward)
        block = jnp.concatenate([low, block, high], axis=dim)
    return block


def nine_point(padded, kappa_rows):
    center = padded[..., 1:-1, 1:-1]
    sideways = padded[..., 1:-1, :-2] + padded[..., 1:-1, 2:]
    vertical = padded[..., :-2, 1:-1] + padded[..., 2:, 1:-1]
    diag_main = padded[..., 2:, 2:] + padded[..., :-2, :-2]
    diag_anti = padded[..., 2:, :-2] + padded[..., :-2, 2:]
    return (
        (kappa_rows + 2.0 * along_cols + 2.0 * along_rows) * center
        - along_cols * sideways
        - along_rows * vertical
        - 0.5 * cross_term * (diag_main - diag_anti)
    )


def pad_cols(field):
    return jnp.pad(field, [(0, 0)] * (field.ndim - 1) + [(1, 1)])


def local_sum(left, right):
    return jnp.sum(left * right, axis=(1, 2, 3))


def shards(probe_signs, land_mask, kappa_sq, trait_covariance):
    land = land_mask.astype(jnp.float32)
    signed_field = land * (2 * probe_signs - 1).astype(jnp.float32)
    variances = jnp.diagonal(trait_covariance)
    trait_pos = lax.axis_index("trait")
    exchanged = lax.all_to_all(
        signed_field.astype(jnp.bfloat16), "trait", split_axis=0, concat_axis=1, tiled=True
    ).astype(jnp.float32)
    field = exchanged * variances[None, :, None, None]
    probe_count = field.shape[0]
    offset = trait_pos * probe_count

    def spread(local):
        return lax.dynamic_update_slice(jnp.zeros((PROBES,), jnp.float32), local, (offset,))

    def own_part(full):
        return lax.dynamic_slice(full, (offset,), (probe_count,))

    def edge_rows(current):
        return extended(current, (("tile", 2),), 1)

    total = lax.psum(spread(local_sum(field, field)), ("trait", "tile"))
    norm_own = own_part(jnp.sqrt(total + epsilon))
    current = field / norm_own[:, None, None, None]
    previous = jnp.zeros_like(current)
    beta_prev = jnp.zeros_like(norm_own)
    alpha_list = []
    beta_list = []
    for step in range(ITERS):
        first = land * nine_point(
            pad_cols(
                edge_rows(
                    jnp.einsum(
                        "ts,psrc->ptrc", trait_covariance, current, precision=lax.Precision.HIGHEST
                    )
                )
            ),
            kappa_sq,
        )
        image = (
            land * nine_point(pad_cols(edge_rows(first)), kappa_sq)
            - beta_prev[:, None, None, None] * previous
        )
        alpha_full = lax.psum(spread(local_sum(image, current)), ("trait", "tile"))
        residual = image - own_part(alpha_full)[:, None, None, None] * current
        beta_full = jnp.sqrt(
            lax.psum(spread(local_sum(residual, residual)), ("trait", "tile")) + epsilon
        )
        beta_own = own_part(beta_full)
        previous = current
        current = residual / beta_own[:, None, None, None]
        beta_prev = beta_own
        alpha_list.append(alpha_full)
        beta_list.append(beta_full)
    last_vector = current * norm_own[:, None, None, None]
    last_vector = lax.all_to_all(last_vector, "trait", split_axis=1, concat_axis=0, tiled=True)
    return (jnp.stack(alpha_list, axis=1), jnp.stack(beta_list, axis=1), last_vector)


def solution(mesh):
    in_specs = (P(None, "trait", "tile", None), P("tile", None), P("tile", None), P())
    out_specs = (P(), P(), P(None, "trait", "tile", None))
    return jax.shard_map(shards, mesh=mesh, in_specs=in_specs, out_specs=out_specs, check_vma=False)
```

profile of v0, /device:TPU:0, one launch (start us, length us, event | category | flops | bytes accessed | tf_op | source)
XLA Modules:
  0.0 405.6 jit_solution(9260228566444692212)
XLA Ops:
  1.5 2.2 multiply_convert_fusion
  3.7 5.2 %all-to-all-start = ((bf16[4,4,8,2048]{3,2,1,0:T(8,128)(2,1)}), bf16[4,4,8,2048]{3,2,1,0:T(8,128)(2,1)S(1)}, u32[]{:S(2)}, u32[]{:S(2)}) async-start(bf16[4,4,8,2048]{3,2,1,0:T(8,128)(2,1)} %multiply_convert_fusion), calls=%async_computation | async-start | bytes 1048576 | tf_op jit(solution)/shard_map/all_to_all | solution.py:56
  9.6 7.3 %all-to-all-done = bf16[4,4,8,2048]{3,2,1,0:T(8,128)(2,1)S(1)} async-done(((bf16[4,4,8,2048]{3,2,1,0:T(8,128)(2,1)}), bf16[4,4,8,2048]{3,2,1,0:T(8,128)(2,1)S(1)}, u32[]{:S(2)}, u32[]{:S(2)}) %all-to-all-start) | async-done | bytes 524320 | tf_op jit(solution)/shard_map/all_to_all | solution.py:56
  18.6 39.5 %psum.49 = f32[4]{0:T(128)S(1)} all-reduce(f32[4]{0:T(128)S(1)} %dynamic_update_slice.21), channel_id=1, replica_groups=mesh['trait'=4,'tile'=8] {'trait','tile'}, use_global_device_ids=true, to_apply=%region_1.2 | all-reduce | flops 4 | bytes 32 | tf_op jit(solution)/shard_map/psum | solution.py:72
  58.8 2.3 convolution_bitcast_fusion.2
  63.8 3.6 collective-permute-done.1
  68.8 5.5 %collective-permute-start.2 = (f32[1,16,1,2048]{3,1,2,0:T(8,128)S(1)}, f32[1,16,1,2048]{3,1,2,0:T(8,128)S(1)}, u32[]{:S(2)}, u32[]{:S(2)}) collective-permute-start(f32[1,16,1,2048]{3,1,2,0:T(8,128)S(1)} %get-tuple-element.26), channel_id=1, source_target_pairs={{0,1},{1,2},{2,3},{3,4},{4,5},{5,6},{6,7},{8,9},{9,10},{10,11},{11... | collective-permute-start | bytes 393224 | tf_op jit(solution)/shard_map/ppermute | solution.py:21
  75.6 1.9 collective-permute-done.3
  77.9 2.4 multiply_reduce_fusion.5
  81.0 42.3 %psum.50 = f32[4]{0:T(128)S(1)} all-reduce(f32[4]{0:T(128)S(1)} %dynamic_update_slice.22), channel_id=1, replica_groups=mesh['trait'=4,'tile'=8] {'trait','tile'}, use_global_device_ids=true, to_apply=%region_3.4 | all-reduce | flops 4 | bytes 32 | tf_op jit(solution)/shard_map/psum | solution.py:94
  123.9 2.6 multiply_reduce_fusion.4
  127.3 40.0 %psum.51 = f32[4]{0:T(128)S(1)} all-reduce(f32[4]{0:T(128)S(1)} %dynamic_update_slice.23), channel_id=1, replica_groups=mesh['trait'=4,'tile'=8] {'trait','tile'}, use_global_device_ids=true, to_apply=%region_5.6 | all-reduce | flops 4 | bytes 32 | tf_op jit(solution)/shard_map/psum | solution.py:97
  167.8 2.6 broadcast_divide_fusion.1
  172.8 1.5 collective-permute-start.5
  174.3 3.5 collective-permute-done.5
  179.2 5.5 %collective-permute-start.6 = (f32[1,16,1,2048]{3,1,2,0:T(8,128)S(1)}, f32[1,16,1,2048]{3,1,2,0:T(8,128)S(1)}, u32[]{:S(2)}, u32[]{:S(2)}) collective-permute-start(f32[1,16,1,2048]{3,1,2,0:T(8,128)S(1)} %get-tuple-element.22), channel_id=1, source_target_pairs={{0,1},{1,2},{2,3},{3,4},{4,5},{5,6},{6,7},{8,9},{9,10},{10,11},{11... | collective-permute-start | bytes 393224 | tf_op jit(solution)/shard_map/ppermute | solution.py:21
  185.9 1.9 collective-permute-done.7
  188.3 3.1 multiply_reduce_fusion.3
  192.1 41.6 %psum.52 = f32[4]{0:T(128)S(1)} all-reduce(f32[4]{0:T(128)S(1)} %dynamic_update_slice.24), channel_id=1, replica_groups=mesh['trait'=4,'tile'=8] {'trait','tile'}, use_global_device_ids=true, to_apply=%region_7.8 | all-reduce | flops 4 | bytes 32 | tf_op jit(solution)/shard_map/psum | solution.py:94
  234.3 1.5 multiply_reduce_fusion.2
  236.6 39.8 %psum.53 = f32[4]{0:T(128)S(1)} all-reduce(f32[4]{0:T(128)S(1)} %dynamic_update_slice.25), channel_id=1, replica_groups=mesh['trait'=4,'tile'=8] {'trait','tile'}, use_global_device_ids=true, to_apply=%region_9.10 | all-reduce | flops 4 | bytes 32 | tf_op jit(solution)/shard_map/psum | solution.py:97
  282.1 3.4 collective-permute-done.9
  286.9 5.5 %collective-permute-start.10 = (f32[1,16,1,2048]{3,1,2,0:T(8,128)S(1)}, f32[1,16,1,2048]{3,1,2,0:T(8,128)S(1)}, u32[]{:S(2)}, u32[]{:S(2)}) collective-permute-start(f32[1,16,1,2048]{3,1,2,0:T(8,128)S(1)} %get-tuple-element.18), channel_id=1, source_target_pairs={{0,1},{1,2},{2,3},{3,4},{4,5},{5,6},{6,7},{8,9},{9,10},{10,11},{11... | collective-permute-start | bytes 393224 | tf_op jit(solution)/shard_map/ppermute | solution.py:21
  293.7 1.9 collective-permute-done.11
  296.0 2.2 multiply_reduce_fusion.1
  299.0 41.6 %psum.54 = f32[4]{0:T(128)S(1)} all-reduce(f32[4]{0:T(128)S(1)} %dynamic_update_slice.26), channel_id=1, replica_groups=mesh['trait'=4,'tile'=8] {'trait','tile'}, use_global_device_ids=true, to_apply=%region_11.12 | all-reduce | flops 4 | bytes 32 | tf_op jit(solution)/shard_map/psum | solution.py:94
  341.2 1.5 multiply_reduce_fusion
  343.4 40.1 %psum.55 = f32[4]{0:T(128)S(1)} all-reduce(f32[4]{0:T(128)S(1)} %dynamic_update_slice.27), channel_id=1, replica_groups=mesh['trait'=4,'tile'=8] {'trait','tile'}, use_global_device_ids=true, to_apply=%region_13.14 | all-reduce | flops 4 | bytes 32 | tf_op jit(solution)/shard_map/psum | solution.py:97
  384.2 2.1 divide_multiply_fusion
  386.3 1.6 copy.19
  387.9 4.1 %all-to-all-start.1 = ((f32[1,16,8,2048]{3,2,0,1:T(8,128)}), f32[1,16,8,2048]{3,2,0,1:T(8,128)S(1)}, u32[]{:S(2)}, u32[]{:S(2)}) async-start(f32[1,16,8,2048]{3,2,0,1:T(8,128)} %copy.19), calls=%async_computation.1 | async-start | bytes 2097152 | tf_op jit(solution)/shard_map/all_to_all | solution.py:106
  393.4 11.3 %all-to-all-done.1 = f32[1,16,8,2048]{3,2,0,1:T(8,128)S(1)} async-done(((f32[1,16,8,2048]{3,2,0,1:T(8,128)}), f32[1,16,8,2048]{3,2,0,1:T(8,128)S(1)}, u32[]{:S(2)}, u32[]{:S(2)}) %all-to-all-start.1) | async-done | bytes 1048608 | tf_op jit(solution)/shard_map/all_to_all | solution.py:106
  (73 shorter events, 33.7 us)
Async XLA Ops:
  0.6 8.3 %copy-start = (f32[16,16]{1,0:T(8,128)S(1)}, f32[16,16]{1,0:T(8,128)}, u32[]{:S(2)}) copy-start(f32[16,16]{1,0:T(8,128)} %param.7) | copy-start | bytes 3076
  3.7 13.2 %all-to-all-start = ((bf16[4,4,8,2048]{3,2,1,0:T(8,128)(2,1)}), bf16[4,4,8,2048]{3,2,1,0:T(8,128)(2,1)S(1)}, u32[]{:S(2)}, u32[]{:S(2)}) async-start(bf16[4,4,8,2048]{3,2,1,0:T(8,128)(2,1)} %multiply_convert_fusion), calls=%async_computation | async-start | bytes 1048576 | tf_op jit(solution)/shard_map/all_to_all | solution.py:56
  58.8 4.9 %copy-start.1 = (f32[8,2048]{1,0:T(8,128)S(1)}, f32[8,2048]{1,0:T(8,128)}, u32[]{:S(2)}) copy-start(f32[8,2048]{1,0:T(8,128)} %param.6) | copy-start | bytes 196612
  61.1 2.6 collective-permute-start
  62.4 5.0 %collective-permute-start.1 = (f32[1,16,1,2048]{3,1,2,0:T(8,128)S(1)}, f32[1,16,1,2048]{3,1,2,0:T(8,128)S(1)}, u32[]{:S(2)}, u32[]{:S(2)}) collective-permute-start(f32[1,16,1,2048]{3,1,2,0:T(8,128)S(1)} %get-tuple-element.29), channel_id=1, source_target_pairs={{1,0},{2,1},{3,2},{4,3},{5,4},{6,5},{7,6},{9,8},{10,9},{11,10},{12... | collective-permute-start | bytes 393224 | tf_op jit(solution)/shard_map/ppermute | solution.py:24
  68.8 6.8 %collective-permute-start.2 = (f32[1,16,1,2048]{3,1,2,0:T(8,128)S(1)}, f32[1,16,1,2048]{3,1,2,0:T(8,128)S(1)}, u32[]{:S(2)}, u32[]{:S(2)}) collective-permute-start(f32[1,16,1,2048]{3,1,2,0:T(8,128)S(1)} %get-tuple-element.26), channel_id=1, source_target_pairs={{0,1},{1,2},{2,3},{3,4},{4,5},{5,6},{6,7},{8,9},{9,10},{10,11},{11... | collective-permute-start | bytes 393224 | tf_op jit(solution)/shard_map/ppermute | solution.py:21
  74.2 3.2 collective-permute-start.3
  171.5 2.8 collective-permute-start.4
  172.8 5.0 %collective-permute-start.5 = (f32[1,16,1,2048]{3,1,2,0:T(8,128)S(1)}, f32[1,16,1,2048]{3,1,2,0:T(8,128)S(1)}, u32[]{:S(2)}, u32[]{:S(2)}) collective-permute-start(f32[1,16,1,2048]{3,1,2,0:T(8,128)S(1)} %get-tuple-element.25), channel_id=1, source_target_pairs={{1,0},{2,1},{3,2},{4,3},{5,4},{6,5},{7,6},{9,8},{10,9},{11,10},{12... | collective-permute-start | bytes 393224 | tf_op jit(solution)/shard_map/ppermute | solution.py:24
  179.2 6.8 %collective-permute-start.6 = (f32[1,16,1,2048]{3,1,2,0:T(8,128)S(1)}, f32[1,16,1,2048]{3,1,2,0:T(8,128)S(1)}, u32[]{:S(2)}, u32[]{:S(2)}) collective-permute-start(f32[1,16,1,2048]{3,1,2,0:T(8,128)S(1)} %get-tuple-element.22), channel_id=1, source_target_pairs={{0,1},{1,2},{2,3},{3,4},{4,5},{5,6},{6,7},{8,9},{9,10},{10,11},{11... | collective-permute-start | bytes 393224 | tf_op jit(solution)/shard_map/ppermute | solution.py:21
  184.6 3.2 collective-permute-start.7
  279.5 2.6 collective-permute-start.8
  280.8 4.7 %collective-permute-start.9 = (f32[1,16,1,2048]{3,1,2,0:T(8,128)S(1)}, f32[1,16,1,2048]{3,1,2,0:T(8,128)S(1)}, u32[]{:S(2)}, u32[]{:S(2)}) collective-permute-start(f32[1,16,1,2048]{3,1,2,0:T(8,128)S(1)} %get-tuple-element.21), channel_id=1, source_target_pairs={{1,0},{2,1},{3,2},{4,3},{5,4},{6,5},{7,6},{9,8},{10,9},{11,10},{12... | collective-permute-start | bytes 393224 | tf_op jit(solution)/shard_map/ppermute | solution.py:24
  286.9 6.8 %collective-permute-start.10 = (f32[1,16,1,2048]{3,1,2,0:T(8,128)S(1)}, f32[1,16,1,2048]{3,1,2,0:T(8,128)S(1)}, u32[]{:S(2)}, u32[]{:S(2)}) collective-permute-start(f32[1,16,1,2048]{3,1,2,0:T(8,128)S(1)} %get-tuple-element.18), channel_id=1, source_target_pairs={{0,1},{1,2},{2,3},{3,4},{4,5},{5,6},{6,7},{8,9},{9,10},{10,11},{11... | collective-permute-start | bytes 393224 | tf_op jit(solution)/shard_map/ppermute | solution.py:21
  292.3 3.2 collective-permute-start.11
  387.9 16.8 %all-to-all-start.1 = ((f32[1,16,8,2048]{3,2,0,1:T(8,128)}), f32[1,16,8,2048]{3,2,0,1:T(8,128)S(1)}, u32[]{:S(2)}, u32[]{:S(2)}) async-start(f32[1,16,8,2048]{3,2,0,1:T(8,128)} %copy.19), calls=%async_computation.1 | async-start | bytes 2097152 | tf_op jit(solution)/shard_map/all_to_all | solution.py:106
where the time goes:
time: 407 us; the launch traced here: 406 us
  blocking collectives  285 us (70%)
  starting transfers between devices  37.5 us (9%)
  waiting for transfers between devices  34.9 us (9%)
  other arithmetic  28.9 us (7%)
  local copies, waits for them, and re-layouts  14.2 us (3%)
  matrix products  4.35 us (1%)
    psum x3, blocking collectives, shards(): alpha_full = lax.psum(spread(local_sum(image, current)), ('trait', 'tile'))  125 us
    psum x3, blocking collectives, shards(): lax.psum(spread(local_sum(residual, residual)), ('trait', 'tile')) + epsilon  120 us
    psum x1, blocking collectives, shards(): total = lax.psum(spread(local_sum(field, field)), ('trait', 'tile'))  39.5 us
    ppermute x6, starting transfers between devices, extended(): lax.ppermute(lax.slice_in_dim(block, block.shape[dim] - width, None, axis...  20.3 us
    ppermute x6, waiting for transfers between devices, extended(): lax.ppermute(lax.slice_in_dim(block, 0, width, axis=dim), axis, backward)  16.3 us
    reduce_sum x7, other arithmetic, local_sum(): return jnp.sum(left * right, axis=(1, 2, 3))  14.3 us
    all_to_all x1, waiting for transfers between devices, shards(): lax.all_to_all(last_vector, 'trait', split_axis=1, concat_axis=0, tiled=T...  11.3 us
  transfers between devices with their start and end apart: 14, of which 8 were waited for; matrix products, arithmetic and copies ran while one was open for 1% of the time, Pallas kernels for 0%

commit v1 on v0

v1 whole, which is shorter than its diff:
```python
import jax
import jax.numpy as jnp
from jax import lax
from jax.sharding import PartitionSpec as P


along_cols = 0.25
along_rows = 0.15
cross_term = 0.1
epsilon = 1e-06

HALO = 6


def nine_valid(x, kappa_rows):
    padded = jnp.pad(x, [(0, 0)] * (x.ndim - 1) + [(1, 1)])
    center = padded[..., 1:-1, 1:-1]
    sideways = padded[..., 1:-1, :-2] + padded[..., 1:-1, 2:]
    vertical = padded[..., :-2, 1:-1] + padded[..., 2:, 1:-1]
    diag_main = padded[..., 2:, 2:] + padded[..., :-2, :-2]
    diag_anti = padded[..., 2:, :-2] + padded[..., :-2, 2:]
    return (
        (kappa_rows + 2.0 * along_cols + 2.0 * along_rows) * center
        - along_cols * sideways
        - along_rows * vertical
        - 0.5 * cross_term * (diag_main - diag_anti)
    )


def tile_sum(v):
    n = lax.axis_size("tile")
    if n & (n - 1):
        return lax.psum(v, "tile")
    s = 1
    while s < n:
        v = v + lax.ppermute(v, "tile", [(i, i ^ s) for i in range(n)])
        s *= 2
    return v


def halo_rows(block, width):
    n = lax.axis_size("tile")
    dim = block.ndim - 2
    rows = block.shape[dim]
    assert rows >= width
    forward = [(i, i + 1) for i in range(n - 1)]
    backward = [(i + 1, i) for i in range(n - 1)]
    low = lax.ppermute(lax.slice_in_dim(block, rows - width, rows, axis=dim), "tile", forward)
    high = lax.ppermute(lax.slice_in_dim(block, 0, width, axis=dim), "tile", backward)
    return jnp.concatenate([low, block, high], axis=dim)


def shards(probe_signs, land_mask, kappa_sq, trait_covariance):
    rows = land_mask.shape[0]
    h = HALO
    signed = (land_mask[None, None] * (2 * probe_signs - 1)).astype(jnp.bfloat16)
    exchanged = lax.all_to_all(signed, "trait", split_axis=0, concat_axis=1, tiled=True)
    field_ext = halo_rows(exchanged, h).astype(jnp.float32)
    kappa_ext = halo_rows(kappa_sq, h)
    land_ext = field_ext[0, 0] * field_ext[0, 0]
    variances = jnp.diagonal(trait_covariance)
    z = field_ext * variances[None, :, None, None]

    def apply_a(x, off):
        r = x.shape[2]
        mixed = jnp.einsum("ts,psrc->ptrc", trait_covariance, x, precision=lax.Precision.HIGHEST)
        first = land_ext[off + 1 : off + r - 1] * nine_valid(mixed, kappa_ext[off + 1 : off + r - 1])
        return land_ext[off + 2 : off + r - 2] * nine_valid(first, kappa_ext[off + 2 : off + r - 2])

    def own(x, off):
        return x[:, :, h - off : h - off + rows]

    def dot(a, b, off):
        return jnp.sum(own(a, off) * own(b, off), axis=(1, 2, 3))

    def crop(x, k):
        return x[:, :, k : x.shape[2] - k]

    az = apply_a(z, 0)
    z2 = crop(z, 2)
    sums = tile_sum(jnp.stack([dot(z2, z2, 2), dot(az, z2, 2)], axis=-1))
    norm = jnp.sqrt(sums[:, 0] + epsilon)
    alpha = sums[:, 1] / (norm * norm)
    q = z2 / norm[:, None, None, None]
    v = az / norm[:, None, None, None]
    w = v - alpha[:, None, None, None] * q
    off = 2
    alphas = [alpha]
    betas = []
    iters = 3
    for step in range(1, iters):
        aw = apply_a(w, off)
        w2 = crop(w, 2)
        q2 = crop(q, 2)
        off += 2
        sums = tile_sum(
            jnp.stack([dot(w2, w2, off), dot(aw, w2, off), dot(q2, w2, off)], axis=-1)
        )
        beta = jnp.sqrt(sums[:, 0] + epsilon)
        alpha = sums[:, 1] / (beta * beta) - sums[:, 2]
        q_next = w2 / beta[:, None, None, None]
        v = aw / beta[:, None, None, None] - beta[:, None, None, None] * q2
        w = v - alpha[:, None, None, None] * q_next
        q = q_next
        betas.append(beta)
        alphas.append(alpha)
    w_own = own(w, off)
    sums = tile_sum(jnp.sum(w_own * w_own, axis=(1, 2, 3)))
    beta = jnp.sqrt(sums + epsilon)
    betas.append(beta)
    last = (w_own / beta[:, None, None, None]) * norm[:, None, None, None]
    last = lax.all_to_all(last, "trait", split_axis=1, concat_axis=0, tiled=True)
    scalars = jnp.concatenate([jnp.stack(alphas, axis=1), jnp.stack(betas, axis=1)], axis=1)
    scalars = lax.all_gather(scalars, "trait", axis=0, tiled=True)
    return scalars[:, :iters], scalars[:, iters:], last


def solution(mesh):
    in_specs = (P(None, "trait", "tile", None), P("tile", None), P("tile", None), P())
    out_specs = (P(), P(), P(None, "trait", "tile", None))
    return jax.shard_map(shards, mesh=mesh, in_specs=in_specs, out_specs=out_specs, check_vma=False)
```

time: 407 us -> 149 us (0.37)
  blocking collectives: 285 us -> 12.8 us
  other arithmetic: 28.9 us -> 48.3 us
  waiting for transfers between devices: 34.9 us -> 23.8 us
  between operations: 0.96 us -> 8.73 us
  local copies, waits for them, and re-layouts: 14.2 us -> 6.77 us
  starting transfers between devices: 37.5 us -> 41.6 us
    psum x7 -> x0, blocking collectives: 285 us -> none  [the longest x3 125 us: shards(): alpha_full = lax.psum(spread(local_sum(image, current)), ('trait', 'tile'))]
    all_to_all x2, waiting for transfers between devices: 18.6 us -> 1.59 us  [the longest x1 1.59 us: shards(): lax.all_to_all(signed, 'trait', split_axis=0, concat_axis=1, tiled=True)]
    all_gather x0 -> x1, blocking collectives: none -> 12.8 us  [shards(): scalars = lax.all_gather(scalars, 'trait', axis=0, tiled=True)]
    mul x4 -> x8, other arithmetic: 4.86 us -> 17.3 us  [the longest x3 10.3 us: apply_a(): land_ext[off + 1:off + r - 1]]
    add x1 -> x15, other arithmetic: 0.01 us -> 10.9 us  [the longest x9 10.7 us: tile_sum(): v = v + lax.ppermute(v, 'tile', [(i, i ^ s) for i in range(n)])]
    reduce_sum x7 -> x4, other arithmetic: 14.3 us -> 5.32 us  [the longest x3 4.44 us: dot(): return jnp.sum(own(a, off) * own(b, off), axis=(1, 2, 3))]
    ppermute x12 -> x16, waiting for transfers between devices: 16.4 us -> 22.2 us  [the longest x12 17.5 us: tile_sum(): v = v + lax.ppermute(v, 'tile', [(i, i ^ s) for i in range(n)])]
    another operation x4 -> x3, other arithmetic: 0.03 us -> 5.36 us  [the longest x2 3.99 us: shards(): jnp.stack([dot(w2, w2, off), dot(aw, w2, off), dot(q2, w2, off)], axis=-1)]
  transfers between devices with their start and end apart: 14 -> 18, of which waited for: 8 -> 15; matrix products, arithmetic and copies ran while one was open for 1% -> 1% of each run, Pallas kernels for 0% -> 0%
where the time goes in v1:
time: 149 us; the launch traced here: 148 us
  other arithmetic  48.3 us (32%)
  starting transfers between devices  41.6 us (28%)
  waiting for transfers between devices  23.8 us (16%)
  blocking collectives  12.8 us (9%)
  between operations  8.73 us (6%)
  local copies, waits for them, and re-layouts  6.77 us (5%)
  matrix products  6.47 us (4%)
    ppermute x12, starting transfers between devices, tile_sum(): v = v + lax.ppermute(v, 'tile', [(i, i ^ s) for i in range(n)])  25.2 us
    ppermute x12, waiting for transfers between devices, tile_sum(): v = v + lax.ppermute(v, 'tile', [(i, i ^ s) for i in range(n)])  17.5 us
    all_gather x1, blocking collectives, shards(): scalars = lax.all_gather(scalars, 'trait', axis=0, tiled=True)  12.8 us
    add x9, other arithmetic, tile_sum(): v = v + lax.ppermute(v, 'tile', [(i, i ^ s) for i in range(n)])  10.7 us
    mul x3, other arithmetic, apply_a(): land_ext[off + 1:off + r - 1]  10.3 us
    dot_general x3, matrix products, apply_a(): jnp.einsum('ts,psrc->ptrc', trait_covariance, x, precision=lax.Precision....  6.47 us
    mul x2, other arithmetic, apply_a(): land_ext[off + 2:off + r - 2]  6.43 us
    all_to_all x1, starting transfers between devices, shards(): lax.all_to_all(signed, 'trait', split_axis=0, concat_axis=1, tiled=True)  5.19 us
  transfers between devices with their start and end apart: 18, of which 15 were waited for; matrix products, arithmetic and copies ran while one was open for 1% of the time, Pallas kernels for 0%

profile of v1, /device:TPU:0, one launch (start us, length us, event | category | flops | bytes accessed | tf_op | source)
XLA Modules:
  0.0 148.5 jit_solution(6242069277461077655)
XLA Ops:
  0.7 2.2 %multiply_convert_fusion = bf16[4,4,8,2048]{3,2,1,0:T(8,128)(2,1)} fusion(s32[4,4,8,2048]{3,2,1,0:T(8,128)} %param.4, s32[8,2048]{1,0:T(8,128)} %param.5), kind=kLoop, calls=%fused_computation.150 | loop fusion | flops 1048576 | bytes 1638400 | tf_op jit(solution)/shard_map/convert_element_type | solution.py:56
  2.9 5.2 %all-to-all-start = ((bf16[4,4,8,2048]{3,2,1,0:T(8,128)(2,1)}), bf16[4,4,8,2048]{3,2,1,0:T(8,128)(2,1)S(1)}, u32[]{:S(2)}, u32[]{:S(2)}) async-start(bf16[4,4,8,2048]{3,2,1,0:T(8,128)(2,1)} %multiply_convert_fusion), calls=%async_computation | async-start | bytes 1048576 | tf_op jit(solution)/shard_map/all_to_all | solution.py:57
  11.6 2.8 %collective-permute-done.3 = f32[6,2048]{1,0:T(8,128)S(1)} collective-permute-done((f32[6,2048]{1,0:T(8,128)S(1)}, f32[6,2048]{1,0:T(8,128)S(1)}, u32[]{:S(2)}, u32[]{:S(2)}) %collective-permute-start.3) | collective-permute-done | bytes 49184 | tf_op jit(solution)/shard_map/ppermute | solution.py:49
  16.5 3.3 %collective-permute-start = (bf16[1,16,6,2048]{3,1,2,0:T(8,128)(2,1)S(1)}, bf16[1,16,6,2048]{3,1,2,0:T(8,128)(2,1)S(1)}, u32[]{:S(2)}, u32[]{:S(2)}) collective-permute-start(bf16[1,16,6,2048]{3,1,2,0:T(8,128)(2,1)S(1)} %get-tuple-element.24), channel_id=1, source_target_pairs={{0,1},{1,2},{2,3},{3,4},{4,5},{5,6},{6,7},{8,9},{9,10},{10,11},{11... | collective-permute-start | bytes 1179656 | tf_op jit(solution)/shard_map/ppermute | solution.py:48
  21.4 2.0 %collective-permute-done.1 = bf16[1,16,6,2048]{3,1,2,0:T(8,128)(2,1)S(1)} collective-permute-done((bf16[1,16,6,2048]{3,1,2,0:T(8,128)(2,1)S(1)}, bf16[1,16,6,2048]{3,1,2,0:T(8,128)(2,1)S(1)}, u32[]{:S(2)}, u32[]{:S(2)}) %collective-permute-start.1) | collective-permute-done | bytes 393248 | tf_op jit(solution)/shard_map/ppermute | solution.py:49
  23.8 3.0 %convolution_bitcast_fusion = f32[1,16,20,2048]{3,1,2,0:T(8,128)S(1)} fusion(bf16[16,6,2048]{2,0,1:T(8,128)(2,1)S(1)} %bitcast.73, bf16[16,8,2048]{2,0,1:T(8,128)(2,1)S(1)} %copy.14, bf16[16,6,2048]{2,0,1:T(8,128)(2,1)S(1)} %bitcast.72, f32[16]{0:T(128)S(1)} %gather_fusion, f32[16,16]{1,0:T(8,128)S(1)} %copy-done), kind=kOutput, calls=%fused_computation.1 | convolution fusion | flops 128450560 | bytes 3933248 | tf_op jit(solution)/shard_map/ts,psrc->ptrc/dot_general | solution.py:66
  26.8 4.6 %fusion.7 = f32[1,16,18,2048]{3,1,2,0:T(8,128)S(1)} fusion(f32[1,16,20,2048]{3,1,2,0:T(8,128)S(1)} %convolution_bitcast_fusion, f32[18,2048]{1,0:T(8,128)S(1)} %slice_add_fusion.6, f32[18,2048]{1,0:T(8,128)S(1)} %bitcast.78), kind=kLoop, calls=%fused_computation.17 | loop fusion | flops 7667712 | bytes 12451840 | tf_op jit(solution)/shard_map/mul | solution.py:67
  31.4 3.9 %fusion.18 = f32[1,16,16,2048]{3,1,2,0:T(8,128)S(1)} fusion(f32[1,16,18,2048]{3,1,2,0:T(8,128)S(1)} %fusion.7, f32[16,2048]{1,0:T(8,128)S(1)} %slice_add_fusion.10, f32[16,2048]{1,0:T(8,128)S(1)} %bitcast.74), kind=kLoop, calls=%fused_computation.36 | loop fusion | flops 6815744 | bytes 11010048 | tf_op jit(solution)/shard_map/mul | solution.py:68
  38.1 5.8 %collective-permute-start.4 = (f32[1,2]{1,0:T(1,128)S(1)}, f32[1,2]{1,0:T(1,128)S(1)}, u32[]{:S(2)}, u32[]{:S(2)}) collective-permute-start(f32[1,2]{1,0:T(1,128)S(1)} %pad_maximum_fusion.1), channel_id=1, source_target_pairs={{0,1},{1,0},{2,3},{3,2},{4,5},{5,4},{6,7},{7,6},{8,9},{9,8},{10,11... | collective-permute-start | bytes 32 | tf_op jit(solution)/shard_map/ppermute | solution.py:36
  47.7 2.0 %collective-permute-done.5 = f32[1,2]{1,0:T(1,128)S(1)} collective-permute-done((f32[1,2]{1,0:T(1,128)S(1)}, f32[1,2]{1,0:T(1,128)S(1)}, u32[]{:S(2)}, u32[]{:S(2)}) %collective-permute-start.5) | collective-permute-done | bytes 40 | tf_op jit(solution)/shard_map/ppermute | solution.py:36
  51.0 2.6 %collective-permute-start.6 = (f32[1,2]{1,0:T(1,128)S(1)}, f32[1,2]{1,0:T(1,128)S(1)}, u32[]{:S(2)}, u32[]{:S(2)}) collective-permute-start(f32[1,2]{1,0:T(1,128)S(1)} %fusion.97), channel_id=1, source_target_pairs={{0,4},{1,5},{2,6},{3,7},{4,0},{5,1},{6,2},{7,3},{8,12},{9,13},{10,... | collective-permute-start | bytes 32 | tf_op jit(solution)/shard_map/ppermute | solution.py:36
  57.4 4.0 %slice_divide_fusion = (f32[1,16,16,2048]{3,1,2,0:T(8,128)S(1)}, f32[1,16,16,2048]{3,1,2,0:T(8,128)S(1)}) fusion(f32[1,16,20,2048]{3,1,2,0:T(8,128)S(1)} %broadcast_multiply_fusion, f32[]{:T(128)} %bitcast.11, f32[]{:T(128)} %bitcast.12, f32[1,16,18,2048]{3,1,2,0:T(8,128)S(1)} %fusion.7, f32[16,2048]{1,0:T(8,128)S(1)} %slice_add_fusion.10, ...), kind=kLoop, calls=%fused_computation.41 | loop fusion | flops 8912896 | bytes 15204360 | tf_op jit(solution)/shard_map/div | solution.py:84
  61.4 2.0 %convolution_bitcast_fusion.1 = f32[1,16,16,2048]{3,1,2,0:T(8,128)S(1)} fusion(f32[1,16,16,2048]{3,1,2,0:T(8,128)S(1)} %get-tuple-element.21, f32[16,16]{1,0:T(8,128)S(1)} %copy-done), kind=kOutput, calls=%fused_computation.2 | convolution fusion | flops 100663296 | bytes 4195328 | tf_op jit(solution)/shard_map/ts,psrc->ptrc/dot_general | solution.py:66
  63.4 3.7 %fusion.30 = f32[1,16,14,2048]{3,1,2,0:T(8,128)S(1)} fusion(f32[1,16,16,2048]{3,1,2,0:T(8,128)S(1)} %convolution_bitcast_fusion.1, f32[14,2048]{1,0:T(8,128)S(1)} %slice_add_fusion.8, f32[14,2048]{1,0:T(8,128)S(1)} %bitcast.80), kind=kLoop, calls=%fused_computation.58 | loop fusion | flops 5963776 | bytes 9699328 | tf_op jit(solution)/shard_map/mul | solution.py:67
  67.0 2.5 %fusion.41 = f32[1,16,12,2048]{3,1,2,0:T(8,128)S(1)} fusion(f32[1,16,14,2048]{3,1,2,0:T(8,128)S(1)} %fusion.30, f32[12,2048]{1,0:T(8,128)S(1)} %slice_add_fusion.9, f32[12,2048]{1,0:T(8,128)S(1)} %bitcast.76), kind=kLoop, calls=%fused_computation.77 | loop fusion | flops 5111808 | bytes 8388608 | tf_op jit(solution)/shard_map/mul | solution.py:68
  70.6 1.9 %pad_maximum_fusion.2 = f32[1,3]{1,0:T(1,128)S(1)} fusion(f32[1,1]{1,0:T(1,128)} %bitcast.19, f32[1,1]{1,0:T(1,128)} %bitcast.18, f32[1,1]{1,0:T(1,128)} %bitcast.13), kind=kLoop, calls=%fused_computation.169 | loop fusion | flops 6 | bytes 24 | tf_op jit(solution)/shard_map/stack | solution.py:97
  73.7 1.9 %fusion.93 = f32[1,3]{1,0:T(1,128)S(1)} fusion(f32[1,3]{1,0:T(1,128)S(1)} %collective-permute-done.7, f32[1,1]{1,0:T(1,128)} %bitcast.19, f32[1,1]{1,0:T(1,128)} %bitcast.18, f32[1,1]{1,0:T(1,128)} %bitcast.13), kind=kLoop, calls=%fused_computation.180 | loop fusion | flops 9 | bytes 36 | tf_op jit(solution)/shard_map/add | solution.py:36
  77.2 2.0 %collective-permute-done.8 = f32[1,3]{1,0:T(1,128)S(1)} collective-permute-done((f32[1,3]{1,0:T(1,128)S(1)}, f32[1,3]{1,0:T(1,128)S(1)}, u32[]{:S(2)}, u32[]{:S(2)}) %collective-permute-start.8) | collective-permute-done | bytes 44 | tf_op jit(solution)/shard_map/ppermute | solution.py:36
  79.2 1.9 %fusion.96 = f32[1,3]{1,0:T(1,128)S(1)} fusion(f32[1,3]{1,0:T(1,128)S(1)} %collective-permute-done.8, f32[1,3]{1,0:T(1,128)S(1)} %collective-permute-done.7, f32[1,1]{1,0:T(1,128)} %bitcast.19, f32[1,1]{1,0:T(1,128)} %bitcast.18, f32[1,1]{1,0:T(1,128)} %bitcast.13), kind=kLoop, calls=%fused_computation.183 | loop fusion | flops 12 | bytes 48 | tf_op jit(solution)/shard_map/add | solution.py:36
  81.1 2.6 %collective-permute-start.9 = (f32[1,3]{1,0:T(1,128)S(1)}, f32[1,3]{1,0:T(1,128)S(1)}, u32[]{:S(2)}, u32[]{:S(2)}) collective-permute-start(f32[1,3]{1,0:T(1,128)S(1)} %fusion.96), channel_id=1, source_target_pairs={{0,4},{1,5},{2,6},{3,7},{4,0},{5,1},{6,2},{7,3},{8,12},{9,13},{10,... | collective-permute-start | bytes 44 | tf_op jit(solution)/shard_map/ppermute | solution.py:36
  88.0 3.0 %slice_divide_fusion.1 = (f32[1,16,12,2048]{3,1,2,0:T(8,128)S(1)}, f32[1,16,12,2048]{3,1,2,0:T(8,128)S(1)}) fusion(f32[1,16,16,2048]{3,1,2,0:T(8,128)S(1)} %get-tuple-element.21, f32[]{:T(128)} %bitcast.20, f32[]{:T(128)} %bitcast.21, f32[1,16,16,2048]{3,1,2,0:T(8,128)S(1)} %get-tuple-element.20, f32[1,16,14,2048]{3,1,2,0:T(8,128)S(1)} %fusion.30, ...), kind=kLoop, calls=%fused_computation.82 | loop fusion | flops 7471104 | bytes 13107208 | tf_op jit(solution)/shard_map/div | solution.py:101
  92.5 2.1 %fusion.55 = f32[1,16,10,2048]{3,1,2,0:T(8,128)S(1)} fusion(f32[1,16,12,2048]{3,1,2,0:T(8,128)S(1)} %convolution_bitcast_fusion.2, f32[10,2048]{1,0:T(8,128)S(1)} %slice_add_fusion.7, f32[10,2048]{1,0:T(8,128)S(1)} %bitcast.79), kind=kLoop, calls=%fused_computation.101 | loop fusion | flops 4259840 | bytes 7077888 | tf_op jit(solution)/shard_map/mul | solution.py:67
  94.7 2.4 %multiply_reduce_fusion.3 = (f32[]{:T(128)}, f32[]{:T(128)}, f32[]{:T(128)}, f32[1,16,8,2048]{3,1,2,0:T(8,128)S(1)}) fusion(f32[1,16,12,2048]{3,1,2,0:T(8,128)S(1)} %get-tuple-element.23, f32[1,16,12,2048]{3,1,2,0:T(8,128)S(1)} %get-tuple-element.22, f32[1,16,10,2048]{3,1,2,0:T(8,128)S(1)} %fusion.55, f32[8,2048]{1,0:T(8,128)S(1)} %broadcast_add_fusion, ...), kind=kLoop, calls=%fused_computation.147 | loop fusion | flops 4980733 | bytes 7733260 | tf_op jit(solution)/shard_map/reduce_sum | solution.py:74
  97.1 2.1 %pad_maximum_fusion.3 = f32[1,3]{1,0:T(1,128)S(1)} fusion(f32[1,1]{1,0:T(1,128)} %bitcast.28, f32[1,1]{1,0:T(1,128)} %bitcast.27, f32[1,1]{1,0:T(1,128)} %bitcast.22), kind=kLoop, calls=%fused_computation.170 | loop fusion | flops 6 | bytes 24 | tf_op jit(solution)/shard_map/stack | solution.py:97
  100.3 2.1 %fusion.92 = f32[1,3]{1,0:T(1,128)S(1)} fusion(f32[1,3]{1,0:T(1,128)S(1)} %collective-permute-done.10, f32[1,1]{1,0:T(1,128)} %bitcast.28, f32[1,1]{1,0:T(1,128)} %bitcast.27, f32[1,1]{1,0:T(1,128)} %bitcast.22), kind=kLoop, calls=%fused_computation.179 | loop fusion | flops 9 | bytes 36 | tf_op jit(solution)/shard_map/add | solution.py:36
  104.0 2.0 %collective-permute-done.11 = f32[1,3]{1,0:T(1,128)S(1)} collective-permute-done((f32[1,3]{1,0:T(1,128)S(1)}, f32[1,3]{1,0:T(1,128)S(1)}, u32[]{:S(2)}, u32[]{:S(2)}) %collective-permute-start.11) | collective-permute-done | bytes 44 | tf_op jit(solution)/shard_map/ppermute | solution.py:36
  106.0 2.1 %fusion.95 = f32[1,3]{1,0:T(1,128)S(1)} fusion(f32[1,3]{1,0:T(1,128)S(1)} %collective-permute-done.11, f32[1,3]{1,0:T(1,128)S(1)} %collective-permute-done.10, f32[1,1]{1,0:T(1,128)} %bitcast.28, f32[1,1]{1,0:T(1,128)} %bitcast.27, f32[1,1]{1,0:T(1,128)} %bitcast.22), kind=kLoop, calls=%fused_computation.182 | loop fusion | flops 12 | bytes 48 | tf_op jit(solution)/shard_map/add | solution.py:36
  108.1 2.6 %collective-permute-start.12 = (f32[1,3]{1,0:T(1,128)S(1)}, f32[1,3]{1,0:T(1,128)S(1)}, u32[]{:S(2)}, u32[]{:S(2)}) collective-permute-start(f32[1,3]{1,0:T(1,128)S(1)} %fusion.95), channel_id=1, source_target_pairs={{0,4},{1,5},{2,6},{3,7},{4,0},{5,1},{6,2},{7,3},{8,12},{9,13},{10,... | collective-permute-start | bytes 44 | tf_op jit(solution)/shard_map/ppermute | solution.py:36
  118.8 2.9 %collective-permute-start.14 = (f32[1]{0:T(128)}, f32[1]{0:T(128)}, u32[]{:S(2)}, u32[]{:S(2)}) collective-permute-start(f32[1]{0:T(128)} %add.248), channel_id=1, source_target_pairs={{0,2},{1,3},{2,0},{3,1},{4,6},{5,7},{6,4},{7,5},{8,10},{9,11},{10,... | collective-permute-start | bytes 20 | tf_op jit(solution)/shard_map/ppermute | solution.py:36
  123.1 3.9 %collective-permute-start.15 = (f32[1]{0:T(128)}, f32[1]{0:T(128)}, u32[]{:S(2)}, u32[]{:S(2)}) collective-permute-start(f32[1]{0:T(128)} %add.249), channel_id=1, source_target_pairs={{0,4},{1,5},{2,6},{3,7},{4,0},{5,1},{6,2},{7,3},{8,12},{9,13},{10,... | collective-permute-start | bytes 20 | tf_op jit(solution)/shard_map/ppermute | solution.py:36
  130.1 3.9 %all-to-all-start.1 = ((f32[1,16,8,2048]{3,2,0,1:T(8,128)}), f32[1,16,8,2048]{3,2,0,1:T(8,128)S(1)}, u32[]{:S(2)}, u32[]{:S(2)}) async-start(f32[1,16,8,2048]{3,2,0,1:T(8,128)} %copy.15), calls=%async_computation.1 | async-start | bytes 2097152 | tf_op jit(solution)/shard_map/all_to_all | solution.py:112
  134.1 12.8 %all-gather = f32[4,1,6]{2,1,0:T(1,128)S(1)} all-gather(f32[1,1,6]{2,1,0:T(1,128)S(1)} %bitcast.83), channel_id=1, replica_groups=mesh['trait'=4,'tile'=8] {'trait'}, dimensions={0}, use_global_device_ids=true | all-gather | bytes 120 | tf_op jit(solution)/shard_map/all_gather | solution.py:114
  (78 shorter events, 38.1 us)
Async XLA Ops:
  0.6 10.3 %copy-start = (f32[16,16]{1,0:T(8,128)S(1)}, f32[16,16]{1,0:T(8,128)}, u32[]{:S(2)}) copy-start(f32[16,16]{1,0:T(8,128)} %param.7) | copy-start | bytes 3076
  0.6 7.4 %copy-start.2 = (f32[8,2048]{1,0:T(8,128)S(1)}, f32[8,2048]{1,0:T(8,128)}, u32[]{:S(2)}) copy-start(f32[8,2048]{1,0:T(8,128)} %param.6) | copy-start | bytes 196612
  2.9 13.2 %all-to-all-start = ((bf16[4,4,8,2048]{3,2,1,0:T(8,128)(2,1)}), bf16[4,4,8,2048]{3,2,1,0:T(8,128)(2,1)S(1)}, u32[]{:S(2)}, u32[]{:S(2)}) async-start(bf16[4,4,8,2048]{3,2,1,0:T(8,128)(2,1)} %multiply_convert_fusion), calls=%async_computation | async-start | bytes 1048576 | tf_op jit(solution)/shard_map/all_to_all | solution.py:57
  8.1 3.5 %collective-permute-start.2 = (f32[6,2048]{1,0:T(8,128)S(1)}, f32[6,2048]{1,0:T(8,128)S(1)}, u32[]{:S(2)}, u32[]{:S(2)}) collective-permute-start(f32[6,2048]{1,0:T(8,128)S(1)} %get-tuple-element.26), channel_id=1, source_target_pairs={{0,1},{1,2},{2,3},{3,4},{4,5},{5,6},{6,7},{8,9},{9,10},{10,11},{11... | collective-permute-start | bytes 147464 | tf_op jit(solution)/shard_map/ppermute | solution.py:48
  9.6 4.8 %collective-permute-start.3 = (f32[6,2048]{1,0:T(8,128)S(1)}, f32[6,2048]{1,0:T(8,128)S(1)}, u32[]{:S(2)}, u32[]{:S(2)}) collective-permute-start(f32[6,2048]{1,0:T(8,128)S(1)} %get-tuple-element.27), channel_id=1, source_target_pairs={{1,0},{2,1},{3,2},{4,3},{5,4},{6,5},{7,6},{9,8},{10,9},{11,10},{12... | collective-permute-start | bytes 147464 | tf_op jit(solution)/shard_map/ppermute | solution.py:49
  16.5 4.9 %collective-permute-start = (bf16[1,16,6,2048]{3,1,2,0:T(8,128)(2,1)S(1)}, bf16[1,16,6,2048]{3,1,2,0:T(8,128)(2,1)S(1)}, u32[]{:S(2)}, u32[]{:S(2)}) collective-permute-start(bf16[1,16,6,2048]{3,1,2,0:T(8,128)(2,1)S(1)} %get-tuple-element.24), channel_id=1, source_target_pairs={{0,1},{1,2},{2,3},{3,4},{4,5},{5,6},{6,7},{8,9},{9,10},{10,11},{11... | collective-permute-start | bytes 1179656 | tf_op jit(solution)/shard_map/ppermute | solution.py:48
  19.8 3.6 %collective-permute-start.1 = (bf16[1,16,6,2048]{3,1,2,0:T(8,128)(2,1)S(1)}, bf16[1,16,6,2048]{3,1,2,0:T(8,128)(2,1)S(1)}, u32[]{:S(2)}, u32[]{:S(2)}) collective-permute-start(bf16[1,16,6,2048]{3,1,2,0:T(8,128)(2,1)S(1)} %get-tuple-element.25), channel_id=1, source_target_pairs={{1,0},{2,1},{3,2},{4,3},{5,4},{6,5},{7,6},{9,8},{10,9},{11,10},{12... | collective-permute-start | bytes 1179656 | tf_op jit(solution)/shard_map/ppermute | solution.py:49
  23.7 3.2 %copy-start.1 = (f32[1,1,20,2048]{3,1,2,0:T(1,128)}, f32[1,1,20,2048]{3,1,2,0:T(1,128)S(1)}, u32[]{:S(2)}) copy-start(f32[1,1,20,2048]{3,1,2,0:T(1,128)S(1)} %slice_multiply_fusion.10) | copy-start | bytes 491524
  35.7 8.2 %slice-start = ((f32[1,1,20,2048]{3,1,2,0:T(1,128)}), f32[1,1,14,2048]{3,1,2,0:T(1,128)S(1)}, s32[]{:S(2)}) async-start(f32[1,1,20,2048]{3,1,2,0:T(1,128)} %copy-done.1), calls=%async_computation.2 | async-start | bytes 229376 | tf_op jit(solution)/shard_map/slice | solution.py:67
  35.7 8.2 %slice-start.1 = ((f32[1,1,20,2048]{3,1,2,0:T(1,128)}), f32[1,1,12,2048]{3,1,2,0:T(1,128)S(1)}, s32[]{:S(2)}) async-start(f32[1,1,20,2048]{3,1,2,0:T(1,128)} %copy-done.1), calls=%async_computation.3 | async-start | bytes 196608 | tf_op jit(solution)/shard_map/slice | solution.py:68
  35.7 8.3 %slice-start.2 = ((f32[1,1,20,2048]{3,1,2,0:T(1,128)}), f32[1,1,10,2048]{3,1,2,0:T(1,128)S(1)}, s32[]{:S(2)}) async-start(f32[1,1,20,2048]{3,1,2,0:T(1,128)} %copy-done.1), calls=%async_computation.4 | async-start | bytes 163840 | tf_op jit(solution)/shard_map/slice | solution.py:67
  35.7 8.3 %slice-start.3 = ((f32[1,1,20,2048]{3,1,2,0:T(1,128)}), f32[1,1,8,2048]{3,1,2,0:T(1,128)S(1)}, s32[]{:S(2)}) async-start(f32[1,1,20,2048]{3,1,2,0:T(1,128)} %copy-done.1), calls=%async_computation.5 | async-start | bytes 131072 | tf_op jit(solution)/shard_map/slice | solution.py:68
  38.1 6.6 %collective-permute-start.4 = (f32[1,2]{1,0:T(1,128)S(1)}, f32[1,2]{1,0:T(1,128)S(1)}, u32[]{:S(2)}, u32[]{:S(2)}) collective-permute-start(f32[1,2]{1,0:T(1,128)S(1)} %pad_maximum_fusion.1), channel_id=1, source_target_pairs={{0,1},{1,0},{2,3},{3,2},{4,5},{5,4},{6,7},{7,6},{8,9},{9,8},{10,11... | collective-permute-start | bytes 32 | tf_op jit(solution)/shard_map/ppermute | solution.py:36
  46.1 3.6 %collective-permute-start.5 = (f32[1,2]{1,0:T(1,128)S(1)}, f32[1,2]{1,0:T(1,128)S(1)}, u32[]{:S(2)}, u32[]{:S(2)}) collective-permute-start(f32[1,2]{1,0:T(1,128)S(1)} %fusion.94), channel_id=1, source_target_pairs={{0,2},{1,3},{2,0},{3,1},{4,6},{5,7},{6,4},{7,5},{8,10},{9,11},{10,... | collective-permute-start | bytes 32 | tf_op jit(solution)/shard_map/ppermute | solution.py:36
  51.0 4.5 %collective-permute-start.6 = (f32[1,2]{1,0:T(1,128)S(1)}, f32[1,2]{1,0:T(1,128)S(1)}, u32[]{:S(2)}, u32[]{:S(2)}) collective-permute-start(f32[1,2]{1,0:T(1,128)S(1)} %fusion.97), channel_id=1, source_target_pairs={{0,4},{1,5},{2,6},{3,7},{4,0},{5,1},{6,2},{7,3},{8,12},{9,13},{10,... | collective-permute-start | bytes 32 | tf_op jit(solution)/shard_map/ppermute | solution.py:36
  72.5 1.2 collective-permute-start.7
  75.6 3.6 %collective-permute-start.8 = (f32[1,3]{1,0:T(1,128)S(1)}, f32[1,3]{1,0:T(1,128)S(1)}, u32[]{:S(2)}, u32[]{:S(2)}) collective-permute-start(f32[1,3]{1,0:T(1,128)S(1)} %fusion.93), channel_id=1, source_target_pairs={{0,2},{1,3},{2,0},{3,1},{4,6},{5,7},{6,4},{7,5},{8,10},{9,11},{10,... | collective-permute-start | bytes 44 | tf_op jit(solution)/shard_map/ppermute | solution.py:36
  81.1 4.5 %collective-permute-start.9 = (f32[1,3]{1,0:T(1,128)S(1)}, f32[1,3]{1,0:T(1,128)S(1)}, u32[]{:S(2)}, u32[]{:S(2)}) collective-permute-start(f32[1,3]{1,0:T(1,128)S(1)} %fusion.96), channel_id=1, source_target_pairs={{0,4},{1,5},{2,6},{3,7},{4,0},{5,1},{6,2},{7,3},{8,12},{9,13},{10,... | collective-permute-start | bytes 44 | tf_op jit(solution)/shard_map/ppermute | solution.py:36
  99.1 1.2 collective-permute-start.10
  102.4 3.6 %collective-permute-start.11 = (f32[1,3]{1,0:T(1,128)S(1)}, f32[1,3]{1,0:T(1,128)S(1)}, u32[]{:S(2)}, u32[]{:S(2)}) collective-permute-start(f32[1,3]{1,0:T(1,128)S(1)} %fusion.92), channel_id=1, source_target_pairs={{0,2},{1,3},{2,0},{3,1},{4,6},{5,7},{6,4},{7,5},{8,10},{9,11},{10,... | collective-permute-start | bytes 44 | tf_op jit(solution)/shard_map/ppermute | solution.py:36
  108.1 4.5 %collective-permute-start.12 = (f32[1,3]{1,0:T(1,128)S(1)}, f32[1,3]{1,0:T(1,128)S(1)}, u32[]{:S(2)}, u32[]{:S(2)}) collective-permute-start(f32[1,3]{1,0:T(1,128)S(1)} %fusion.95), channel_id=1, source_target_pairs={{0,4},{1,5},{2,6},{3,7},{4,0},{5,1},{6,2},{7,3},{8,12},{9,13},{10,... | collective-permute-start | bytes 44 | tf_op jit(solution)/shard_map/ppermute | solution.py:36
  116.2 1.4 collective-permute-start.13
  118.8 3.7 %collective-permute-start.14 = (f32[1]{0:T(128)}, f32[1]{0:T(128)}, u32[]{:S(2)}, u32[]{:S(2)}) collective-permute-start(f32[1]{0:T(128)} %add.248), channel_id=1, source_target_pairs={{0,2},{1,3},{2,0},{3,1},{4,6},{5,7},{6,4},{7,5},{8,10},{9,11},{10,... | collective-permute-start | bytes 20 | tf_op jit(solution)/shard_map/ppermute | solution.py:36
  123.1 4.6 %collective-permute-start.15 = (f32[1]{0:T(128)}, f32[1]{0:T(128)}, u32[]{:S(2)}, u32[]{:S(2)}) collective-permute-start(f32[1]{0:T(128)} %add.249), channel_id=1, source_target_pairs={{0,4},{1,5},{2,6},{3,7},{4,0},{5,1},{6,2},{7,3},{8,12},{9,13},{10,... | collective-permute-start | bytes 20 | tf_op jit(solution)/shard_map/ppermute | solution.py:36
  130.1 17.4 %all-to-all-start.1 = ((f32[1,16,8,2048]{3,2,0,1:T(8,128)}), f32[1,16,8,2048]{3,2,0,1:T(8,128)S(1)}, u32[]{:S(2)}, u32[]{:S(2)}) async-start(f32[1,16,8,2048]{3,2,0,1:T(8,128)} %copy.15), calls=%async_computation.1 | async-start | bytes 2097152 | tf_op jit(solution)/shard_map/all_to_all | solution.py:112

commit v2 on v1

--- a/solution.py
+++ b/solution.py
@@ -27,15 +27,15 @@
     )
 
 
+def gather_rows(v, axis):
+    n = lax.axis_size(axis)
+    return lax.all_to_all(jnp.concatenate([v] * n, axis=0), axis, 0, 0, tiled=True)
+
+
 def tile_sum(v):
     n = lax.axis_size("tile")
-    if n & (n - 1):
-        return lax.psum(v, "tile")
-    s = 1
-    while s < n:
-        v = v + lax.ppermute(v, "tile", [(i, i ^ s) for i in range(n)])
-        s *= 2
-    return v
+    g = gather_rows(v, "tile").reshape((n,) + v.shape)
+    return jnp.sum(g, axis=0)
 
 
 def halo_rows(block, width):
@@ -105,14 +105,17 @@
         betas.append(beta)
         alphas.append(alpha)
     w_own = own(w, off)
-    sums = tile_sum(jnp.sum(w_own * w_own, axis=(1, 2, 3)))
-    beta = jnp.sqrt(sums + epsilon)
-    betas.append(beta)
-    last = (w_own / beta[:, None, None, None]) * norm[:, None, None, None]
-    last = lax.all_to_all(last, "trait", split_axis=1, concat_axis=0, tiled=True)
-    scalars = jnp.concatenate([jnp.stack(alphas, axis=1), jnp.stack(betas, axis=1)], axis=1)
-    scalars = lax.all_gather(scalars, "trait", axis=0, tiled=True)
-    return scalars[:, :iters], scalars[:, iters:], last
+    w_back = lax.all_to_all(w_own, "trait", split_axis=1, concat_axis=0, tiled=True)
+    sums = tile_sum(jnp.sum(w_own * w_own, axis=(1, 2, 3))[:, None])
+    scalars = jnp.concatenate(
+        [jnp.stack(alphas, axis=1), jnp.stack(betas, axis=1), sums, norm[:, None]], axis=1
+    )
+    scalars = gather_rows(scalars, "trait")
+    beta = jnp.sqrt(scalars[:, 2 * iters - 1] + epsilon)
+    norm_all = scalars[:, 2 * iters]
+    last = (w_back / beta[:, None, None, None]) * norm_all[:, None, None, None]
+    betas_all = jnp.concatenate([scalars[:, iters : 2 * iters - 1], beta[:, None]], axis=1)
+    return scalars[:, :iters], betas_all, last
 
 
 def solution(mesh):

time: 149 us -> 149 us (level)
  starting transfers between devices: 41.6 us -> 32.7 us
  waiting for transfers between devices: 23.8 us -> 29 us
  local copies, waits for them, and re-layouts: 6.77 us -> 11.6 us
  blocking collectives: 12.8 us -> 15.9 us
  between operations: 8.73 us -> 6.16 us
  other arithmetic: 48.3 us -> 45.9 us
    ppermute x12 -> x0, starting transfers between devices: 25.2 us -> none  [tile_sum(): v = v + lax.ppermute(v, 'tile', [(i, i ^ s) for i in range(n)])]
    all_to_all x1 -> x4, waiting for transfers between devices: 0.01 us -> 23.9 us  [the longest x3 12.4 us: gather_rows(): lax.all_to_all(jnp.concatenate([v] * n, axis=0), axis, 0, 0, tiled=True)]
    ppermute x12 -> x0, waiting for transfers between devices: 17.5 us -> none  [tile_sum(): v = v + lax.ppermute(v, 'tile', [(i, i ^ s) for i in range(n)])]
    all_to_all x1 -> x4, starting transfers between devices: 3.86 us -> 20.2 us  [the longest x3 16.7 us: gather_rows(): lax.all_to_all(jnp.concatenate([v] * n, axis=0), axis, 0, 0, tiled=True)]
    all_to_all x0 -> x2, blocking collectives: none -> 15.9 us  [gather_rows(): lax.all_to_all(jnp.concatenate([v] * n, axis=0), axis, 0, 0, tiled=True)]
    all_gather x1 -> x0, blocking collectives: 12.8 us -> none  [shards(): scalars = lax.all_gather(scalars, 'trait', axis=0, tiled=True)]
    add x9 -> x0, other arithmetic: 10.7 us -> none  [tile_sum(): v = v + lax.ppermute(v, 'tile', [(i, i ^ s) for i in range(n)])]
    concatenate x1 -> x6, local copies, waits for them, and re-layouts: 0.1 us -> 3.08 us  [the longest x5 2.34 us: gather_rows(): jnp.concatenate([v] * n, axis=0)]
  transfers between devices with their start and end apart: 18 -> 9, of which waited for: 15 -> 7; matrix products, arithmetic and copies ran while one was open for 1% -> 4% of each run, Pallas kernels for 0% -> 0%
where the time goes in v2:
time: 149 us; the launch traced here: 148 us
  other arithmetic  45.9 us (31%)
  starting transfers between devices  32.7 us (22%)
  waiting for transfers between devices  29 us (19%)
  blocking collectives  15.9 us (11%)
  local copies, waits for them, and re-layouts  11.6 us (8%)
  matrix products  6.48 us (4%)
  between operations  6.16 us (4%)
    all_to_all x3, starting transfers between devices, gather_rows(): lax.all_to_all(jnp.concatenate([v] * n, axis=0), axis, 0, 0, tiled=True)  16.7 us
    all_to_all x2, blocking collectives, gather_rows(): lax.all_to_all(jnp.concatenate([v] * n, axis=0), axis, 0, 0, tiled=True)  15.9 us
    all_to_all x3, waiting for transfers between devices, gather_rows(): lax.all_to_all(jnp.concatenate([v] * n, axis=0), axis, 0, 0, tiled=True)  12.4 us
    all_to_all x1, waiting for transfers between devices, shards(): lax.all_to_all(w_own, 'trait', split_axis=1, concat_axis=0, tiled=True)  11.5 us
    mul x3, other arithmetic, apply_a(): land_ext[off + 1:off + r - 1]  9.96 us
    dot_general x3, matrix products, apply_a(): jnp.einsum('ts,psrc->ptrc', trait_covariance, x, precision=lax.Precision....  6.48 us
    mul x2, other arithmetic, apply_a(): land_ext[off + 2:off + r - 2]  6.38 us
    reduce_sum x3, other arithmetic, dot(): return jnp.sum(own(a, off) * own(b, off), axis=(1, 2, 3))  5.34 us
  transfers between devices with their start and end apart: 9, of which 7 were waited for; matrix products, arithmetic and copies ran while one was open for 4% of the time, Pallas kernels for 0%

profile of v2, /device:TPU:0, one launch (start us, length us, event | category | flops | bytes accessed | tf_op | source)
XLA Modules:
  0.0 147.8 jit_solution(13509861656725137724)
XLA Ops:
  0.7 2.2 %multiply_convert_fusion = bf16[4,4,8,2048]{3,2,1,0:T(8,128)(2,1)} fusion(s32[4,4,8,2048]{3,2,1,0:T(8,128)} %param.4, s32[8,2048]{1,0:T(8,128)} %param.5), kind=kLoop, calls=%fused_computation.150 | loop fusion | flops 1048576 | bytes 1638400 | tf_op jit(solution)/shard_map/convert_element_type | solution.py:56
  2.9 5.2 %all-to-all-start = ((bf16[4,4,8,2048]{3,2,1,0:T(8,128)(2,1)}), bf16[4,4,8,2048]{3,2,1,0:T(8,128)(2,1)S(1)}, u32[]{:S(2)}, u32[]{:S(2)}) async-start(bf16[4,4,8,2048]{3,2,1,0:T(8,128)(2,1)} %multiply_convert_fusion), calls=%async_computation | async-start | bytes 1048576 | tf_op jit(solution)/shard_map/all_to_all | solution.py:57
  8.1 1.5 collective-permute-start.2
  12.2 2.2 %collective-permute-done.3 = f32[6,2048]{1,0:T(8,128)S(1)} collective-permute-done((f32[6,2048]{1,0:T(8,128)S(1)}, f32[6,2048]{1,0:T(8,128)S(1)}, u32[]{:S(2)}, u32[]{:S(2)}) %collective-permute-start.3) | collective-permute-done | bytes 49184 | tf_op jit(solution)/shard_map/ppermute | solution.py:49
  14.5 1.6 %all-to-all-done = bf16[4,4,8,2048]{3,2,1,0:T(8,128)(2,1)S(1)} async-done(((bf16[4,4,8,2048]{3,2,1,0:T(8,128)(2,1)}), bf16[4,4,8,2048]{3,2,1,0:T(8,128)(2,1)S(1)}, u32[]{:S(2)}, u32[]{:S(2)}) %all-to-all-start) | async-done | bytes 524320 | tf_op jit(solution)/shard_map/all_to_all | solution.py:57
  16.5 3.3 %collective-permute-start = (bf16[1,16,6,2048]{3,1,2,0:T(8,128)(2,1)S(1)}, bf16[1,16,6,2048]{3,1,2,0:T(8,128)(2,1)S(1)}, u32[]{:S(2)}, u32[]{:S(2)}) collective-permute-start(bf16[1,16,6,2048]{3,1,2,0:T(8,128)(2,1)S(1)} %get-tuple-element.20), channel_id=1, source_target_pairs={{0,1},{1,2},{2,3},{3,4},{4,5},{5,6},{6,7},{8,9},{9,10},{10,11},{11... | collective-permute-start | bytes 1179656 | tf_op jit(solution)/shard_map/ppermute | solution.py:48
  23.8 3.0 %convolution_bitcast_fusion = f32[1,16,20,2048]{3,1,2,0:T(8,128)S(1)} fusion(bf16[16,6,2048]{2,0,1:T(8,128)(2,1)S(1)} %bitcast.81, bf16[16,8,2048]{2,0,1:T(8,128)(2,1)S(1)} %copy.27, bf16[16,6,2048]{2,0,1:T(8,128)(2,1)S(1)} %bitcast.80, f32[16]{0:T(128)S(1)} %gather_fusion, f32[16,16]{1,0:T(8,128)S(1)} %copy-done), kind=kOutput, calls=%fused_computation.1 | convolution fusion | flops 128450560 | bytes 3933248 | tf_op jit(solution)/shard_map/ts,psrc->ptrc/dot_general | solution.py:66
  26.9 4.4 %fusion.7 = f32[1,16,18,2048]{3,1,2,0:T(8,128)S(1)} fusion(f32[1,16,20,2048]{3,1,2,0:T(8,128)S(1)} %convolution_bitcast_fusion, f32[18,2048]{1,0:T(8,128)S(1)} %slice_add_fusion.6, f32[18,2048]{1,0:T(8,128)S(1)} %bitcast.86), kind=kLoop, calls=%fused_computation.17 | loop fusion | flops 7667712 | bytes 12451840 | tf_op jit(solution)/shard_map/mul | solution.py:67
  31.2 3.9 %fusion.18 = f32[1,16,16,2048]{3,1,2,0:T(8,128)S(1)} fusion(f32[1,16,18,2048]{3,1,2,0:T(8,128)S(1)} %fusion.7, f32[16,2048]{1,0:T(8,128)S(1)} %slice_add_fusion.10, f32[16,2048]{1,0:T(8,128)S(1)} %bitcast.82), kind=kLoop, calls=%fused_computation.36 | loop fusion | flops 6815744 | bytes 11010048 | tf_op jit(solution)/shard_map/mul | solution.py:68
  35.5 1.5 %copy-done.2 = f32[1,16,20,2048]{3,1,2,0:T(8,128)} copy-done((f32[1,16,20,2048]{3,1,2,0:T(8,128)}, f32[1,16,20,2048]{3,1,2,0:T(8,128)S(1)}, u32[]{:S(2)}) %copy-start.2) | copy-done | bytes 2621464
  39.9 9.3 %all-to-all-start.1 = ((f32[8,1,2]{2,1,0:T(1,128)}), f32[8,1,2]{2,1,0:T(1,128)S(1)}, u32[]{:S(2)}, u32[]{:S(2)}) async-start(f32[8,1,2]{2,1,0:T(1,128)} %concatenate.61), calls=%async_computation.1 | async-start | bytes 8192 | tf_op jit(solution)/shard_map/all_to_all | solution.py:32
  49.2 5.5 %all-to-all-done.1 = f32[8,1,2]{2,1,0:T(1,128)S(1)} async-done(((f32[8,1,2]{2,1,0:T(1,128)}), f32[8,1,2]{2,1,0:T(1,128)S(1)}, u32[]{:S(2)}, u32[]{:S(2)}) %all-to-all-start.1) | async-done | bytes 96 | tf_op jit(solution)/shard_map/all_to_all | solution.py:32
  56.7 5.2 %slice_divide_fusion = (f32[1,16,16,2048]{3,1,2,0:T(8,128)S(1)}, f32[1,16,16,2048]{3,1,2,0:T(8,128)S(1)}) fusion(f32[1,16,20,2048]{3,1,2,0:T(8,128)} %copy-done.2, f32[]{:T(128)} %bitcast.13, f32[]{:T(128)} %bitcast.14, f32[1,16,18,2048]{3,1,2,0:T(8,128)S(1)} %fusion.7, f32[16,2048]{1,0:T(8,128)S(1)} %slice_add_fusion.10, f32[16,2048]{1,0:T(8,128)S(1)} %bitcast.83), kind=kLoop, calls=%fused_computation.41 | loop fusion | flops 8912896 | bytes 15204360 | tf_op jit(solution)/shard_map/div | solution.py:84
  61.9 2.0 %convolution_bitcast_fusion.1 = f32[1,16,16,2048]{3,1,2,0:T(8,128)S(1)} fusion(f32[1,16,16,2048]{3,1,2,0:T(8,128)S(1)} %get-tuple-element.17, f32[16,16]{1,0:T(8,128)S(1)} %copy-done), kind=kOutput, calls=%fused_computation.2 | convolution fusion | flops 100663296 | bytes 4195328 | tf_op jit(solution)/shard_map/ts,psrc->ptrc/dot_general | solution.py:66
  63.9 3.5 %fusion.30 = f32[1,16,14,2048]{3,1,2,0:T(8,128)S(1)} fusion(f32[1,16,16,2048]{3,1,2,0:T(8,128)S(1)} %convolution_bitcast_fusion.1, f32[14,2048]{1,0:T(8,128)S(1)} %slice_add_fusion.8, f32[14,2048]{1,0:T(8,128)S(1)} %bitcast.88), kind=kLoop, calls=%fused_computation.58 | loop fusion | flops 5963776 | bytes 9699328 | tf_op jit(solution)/shard_map/mul | solution.py:67
  67.4 2.5 %fusion.41 = f32[1,16,12,2048]{3,1,2,0:T(8,128)S(1)} fusion(f32[1,16,14,2048]{3,1,2,0:T(8,128)S(1)} %fusion.30, f32[12,2048]{1,0:T(8,128)S(1)} %slice_add_fusion.9, f32[12,2048]{1,0:T(8,128)S(1)} %bitcast.84), kind=kLoop, calls=%fused_computation.77 | loop fusion | flops 5111808 | bytes 8388608 | tf_op jit(solution)/shard_map/mul | solution.py:68
  71.0 2.0 %maximum_bitcast_fusion.1 = f32[3]{0:T(128)S(1)} fusion(f32[1,1]{1,0:T(1,128)} %bitcast.21, f32[1,1]{1,0:T(1,128)} %bitcast.20, f32[1,1]{1,0:T(1,128)} %bitcast.15), kind=kLoop, calls=%fused_computation.172 | loop fusion | flops 6 | bytes 24 | tf_op jit(solution)/shard_map/stack | solution.py:97
  73.6 3.5 %all-to-all-start.2 = ((f32[8,1,3]{2,1,0:T(1,128)}), f32[8,1,3]{2,1,0:T(1,128)S(1)}, u32[]{:S(2)}, u32[]{:S(2)}) async-start(f32[8,1,3]{2,1,0:T(1,128)} %concatenate.62), calls=%async_computation.2 | async-start | bytes 8192 | tf_op jit(solution)/shard_map/all_to_all | solution.py:32
  78.4 4.0 %all-to-all-done.2 = f32[8,1,3]{2,1,0:T(1,128)S(1)} async-done(((f32[8,1,3]{2,1,0:T(1,128)}), f32[8,1,3]{2,1,0:T(1,128)S(1)}, u32[]{:S(2)}, u32[]{:S(2)}) %all-to-all-start.2) | async-done | bytes 128 | tf_op jit(solution)/shard_map/all_to_all | solution.py:32
  84.8 4.5 %slice_divide_fusion.1 = (f32[1,16,12,2048]{3,1,2,0:T(8,128)S(1)}, f32[1,16,12,2048]{3,1,2,0:T(8,128)S(1)}) fusion(f32[1,16,16,2048]{3,1,2,0:T(8,128)} %copy-done.1, f32[]{:T(128)} %bitcast.24, f32[]{:T(128)} %bitcast.25, f32[1,16,16,2048]{3,1,2,0:T(8,128)} %copy-done.3, f32[1,16,14,2048]{3,1,2,0:T(8,128)S(1)} %fusion.30, f32[12,2048]{1,0:T(8,128)} %copy-done.6, ...), kind=kLoop, calls=%fused_computation.82 | loop fusion | flops 7471104 | bytes 13074440 | tf_op jit(solution)/shard_map/div | solution.py:101
  89.4 1.5 %convolution_bitcast_fusion.2 = f32[1,16,12,2048]{3,1,2,0:T(8,128)S(1)} fusion(f32[1,16,12,2048]{3,1,2,0:T(8,128)S(1)} %get-tuple-element.19, f32[16,16]{1,0:T(8,128)S(1)} %copy-done), kind=kOutput, calls=%fused_computation.5 | convolution fusion | flops 75497472 | bytes 3146752 | tf_op jit(solution)/shard_map/ts,psrc->ptrc/dot_general | solution.py:66
  90.9 2.1 %fusion.55 = f32[1,16,10,2048]{3,1,2,0:T(8,128)S(1)} fusion(f32[1,16,12,2048]{3,1,2,0:T(8,128)S(1)} %convolution_bitcast_fusion.2, f32[10,2048]{1,0:T(8,128)S(1)} %copy-done.8, f32[10,2048]{1,0:T(8,128)S(1)} %bitcast.87), kind=kLoop, calls=%fused_computation.101 | loop fusion | flops 4259840 | bytes 7077888 | tf_op jit(solution)/shard_map/mul | solution.py:67
  93.1 3.3 %multiply_reduce_fusion.3 = (f32[]{:T(128)}, f32[]{:T(128)}, f32[]{:T(128)}, f32[1,16,8,2048]{3,1,2,0:T(8,128)}) fusion(f32[1,16,12,2048]{3,1,2,0:T(8,128)S(1)} %get-tuple-element.19, f32[1,16,12,2048]{3,1,2,0:T(8,128)S(1)} %get-tuple-element.18, f32[1,16,10,2048]{3,1,2,0:T(8,128)S(1)} %fusion.55, f32[8,2048]{1,0:T(8,128)S(1)} %copy-done.10, ...), kind=kLoop, calls=%fused_computation.147 | loop fusion | flops 4980733 | bytes 7733260 | tf_op jit(solution)/shard_map/reduce_sum | solution.py:74
  96.4 1.9 %maximum_bitcast_fusion.2 = f32[3]{0:T(128)S(1)} fusion(f32[1,1]{1,0:T(1,128)} %bitcast.32, f32[1,1]{1,0:T(1,128)} %bitcast.31, f32[1,1]{1,0:T(1,128)} %bitcast.26), kind=kLoop, calls=%fused_computation.173 | loop fusion | flops 6 | bytes 24 | tf_op jit(solution)/shard_map/stack | solution.py:97
  98.3 7.9 %all_to_all.57 = f32[8,1,3]{2,1,0:T(1,128)S(1)} all-to-all(f32[8,1,3]{2,1,0:T(1,128)S(1)} %concatenate.63), channel_id=1, replica_groups=mesh['trait'=4,'tile'=8] {'tile'}, dimensions={0} | all-to-all | bytes 192 | tf_op jit(solution)/shard_map/all_to_all | solution.py:32
  108.8 2.4 %multiply_reduce_fusion = (f32[]{:T(128)}, f32[1,16,8,2048]{3,1,2,0:T(8,128)S(1)}) fusion(f32[1,16,12,2048]{3,1,2,0:T(8,128)S(1)} %get-tuple-element.19, f32[]{:T(128)} %bitcast.36, f32[1,16,12,2048]{3,1,2,0:T(8,128)} %copy-done.4, f32[1,16,8,2048]{3,1,2,0:T(8,128)} %get-tuple-element.15, f32[]{:T(128)} %bitcast.35), kind=kLoop, calls=%fused_computation.143 | loop fusion | flops 2097151 | bytes 4194316 | tf_op jit(solution)/shard_map/reduce_sum | solution.py:109
  111.7 8.0 %all_to_all.58 = f32[8,1,1]{2,1,0:T(1,128)S(1)} all-to-all(f32[8,1,1]{2,1,0:T(1,128)S(1)} %concatenate.64), channel_id=1, replica_groups=mesh['trait'=4,'tile'=8] {'tile'}, dimensions={0} | all-to-all | bytes 64 | tf_op jit(solution)/shard_map/all_to_all | solution.py:32
  121.6 3.9 %all-to-all-start.5 = ((f32[4,1,7]{2,1,0:T(1,128)}), f32[4,1,7]{2,1,0:T(1,128)S(1)}, u32[]{:S(2)}, u32[]{:S(2)}) async-start(f32[4,1,7]{2,1,0:T(1,128)} %concatenate.67), calls=%async_computation.5 | async-start | bytes 4096 | tf_op jit(solution)/shard_map/all_to_all | solution.py:32
  125.5 1.6 %copy.32 = f32[1,16,8,2048]{3,2,0,1:T(8,128)} copy(f32[1,16,8,2048]{3,1,2,0:T(8,128)S(1)} %get-tuple-element.14) | data formatting | bytes 2097152 | tf_op jit(solution)/shard_map/sub | solution.py:103
  127.1 3.0 %all-to-all-done.5 = f32[4,1,7]{2,1,0:T(1,128)S(1)} async-done(((f32[4,1,7]{2,1,0:T(1,128)}), f32[4,1,7]{2,1,0:T(1,128)S(1)}, u32[]{:S(2)}, u32[]{:S(2)}) %all-to-all-start.5) | async-done | bytes 144 | tf_op jit(solution)/shard_map/all_to_all | solution.py:32
  130.1 3.5 %all-to-all-start.6 = ((f32[1,16,8,2048]{3,2,0,1:T(8,128)}), f32[1,16,8,2048]{3,2,0,1:T(8,128)S(1)}, u32[]{:S(2)}, u32[]{:S(2)}) async-start(f32[1,16,8,2048]{3,2,0,1:T(8,128)} %copy.32), calls=%async_computation.6 | async-start | bytes 2097152 | tf_op jit(solution)/shard_map/all_to_all | solution.py:108
  134.6 11.5 %all-to-all-done.6 = f32[1,16,8,2048]{3,2,0,1:T(8,128)S(1)} async-done(((f32[1,16,8,2048]{3,2,0,1:T(8,128)}), f32[1,16,8,2048]{3,2,0,1:T(8,128)S(1)}, u32[]{:S(2)}, u32[]{:S(2)}) %all-to-all-start.6) | async-done | bytes 1048608 | tf_op jit(solution)/shard_map/all_to_all | solution.py:108
  (81 shorter events, 20.5 us)
Async XLA Ops:
  0.6 10.9 %copy-start = (f32[16,16]{1,0:T(8,128)S(1)}, f32[16,16]{1,0:T(8,128)}, u32[]{:S(2)}) copy-start(f32[16,16]{1,0:T(8,128)} %param.7) | copy-start | bytes 3076
  0.6 7.4 %copy-start.7 = (f32[8,2048]{1,0:T(8,128)S(1)}, f32[8,2048]{1,0:T(8,128)}, u32[]{:S(2)}) copy-start(f32[8,2048]{1,0:T(8,128)} %param.6) | copy-start | bytes 196612
  2.9 13.2 %all-to-all-start = ((bf16[4,4,8,2048]{3,2,1,0:T(8,128)(2,1)}), bf16[4,4,8,2048]{3,2,1,0:T(8,128)(2,1)S(1)}, u32[]{:S(2)}, u32[]{:S(2)}) async-start(bf16[4,4,8,2048]{3,2,1,0:T(8,128)(2,1)} %multiply_convert_fusion), calls=%async_computation | async-start | bytes 1048576 | tf_op jit(solution)/shard_map/all_to_all | solution.py:57
  8.1 4.1 %collective-permute-start.2 = (f32[6,2048]{1,0:T(8,128)S(1)}, f32[6,2048]{1,0:T(8,128)S(1)}, u32[]{:S(2)}, u32[]{:S(2)}) collective-permute-start(f32[6,2048]{1,0:T(8,128)S(1)} %get-tuple-element.22), channel_id=1, source_target_pairs={{0,1},{1,2},{2,3},{3,4},{4,5},{5,6},{6,7},{8,9},{9,10},{10,11},{11... | collective-permute-start | bytes 147464 | tf_op jit(solution)/shard_map/ppermute | solution.py:48
  9.6 4.8 %collective-permute-start.3 = (f32[6,2048]{1,0:T(8,128)S(1)}, f32[6,2048]{1,0:T(8,128)S(1)}, u32[]{:S(2)}, u32[]{:S(2)}) collective-permute-start(f32[6,2048]{1,0:T(8,128)S(1)} %get-tuple-element.23), channel_id=1, source_target_pairs={{1,0},{2,1},{3,2},{4,3},{5,4},{6,5},{7,6},{9,8},{10,9},{11,10},{12... | collective-permute-start | bytes 147464 | tf_op jit(solution)/shard_map/ppermute | solution.py:49
  14.5 52.9 %copy-start.6 = (f32[12,2048]{1,0:T(8,128)}, f32[12,2048]{1,0:T(8,128)S(1)}, u32[]{:S(2)}) copy-start(f32[12,2048]{1,0:T(8,128)S(1)} %slice_add_fusion.9) | copy-start | bytes 294916
  16.5 5.6 %collective-permute-start = (bf16[1,16,6,2048]{3,1,2,0:T(8,128)(2,1)S(1)}, bf16[1,16,6,2048]{3,1,2,0:T(8,128)(2,1)S(1)}, u32[]{:S(2)}, u32[]{:S(2)}) collective-permute-start(bf16[1,16,6,2048]{3,1,2,0:T(8,128)(2,1)S(1)} %get-tuple-element.20), channel_id=1, source_target_pairs={{0,1},{1,2},{2,3},{3,4},{4,5},{5,6},{6,7},{8,9},{9,10},{10,11},{11... | collective-permute-start | bytes 1179656 | tf_op jit(solution)/shard_map/ppermute | solution.py:48
  19.8 3.6 %collective-permute-start.1 = (bf16[1,16,6,2048]{3,1,2,0:T(8,128)(2,1)S(1)}, bf16[1,16,6,2048]{3,1,2,0:T(8,128)(2,1)S(1)}, u32[]{:S(2)}, u32[]{:S(2)}) collective-permute-start(bf16[1,16,6,2048]{3,1,2,0:T(8,128)(2,1)S(1)} %get-tuple-element.21), channel_id=1, source_target_pairs={{1,0},{2,1},{3,2},{4,3},{5,4},{6,5},{7,6},{9,8},{10,9},{11,10},{12... | collective-permute-start | bytes 1179656 | tf_op jit(solution)/shard_map/ppermute | solution.py:49
  23.7 3.2 %copy-start.5 = (f32[1,1,20,2048]{3,1,2,0:T(1,128)}, f32[1,1,20,2048]{3,1,2,0:T(1,128)S(1)}, u32[]{:S(2)}) copy-start(f32[1,1,20,2048]{3,1,2,0:T(1,128)S(1)} %slice_multiply_fusion.10) | copy-start | bytes 491524
  35.4 1.5 %copy-start.2 = (f32[1,16,20,2048]{3,1,2,0:T(8,128)}, f32[1,16,20,2048]{3,1,2,0:T(8,128)S(1)}, u32[]{:S(2)}) copy-start(f32[1,16,20,2048]{3,1,2,0:T(8,128)S(1)} %broadcast_multiply_fusion) | copy-start | bytes 7864324
  37.0 12.2 %slice-start = ((f32[1,1,20,2048]{3,1,2,0:T(1,128)}), f32[1,1,14,2048]{3,1,2,0:T(1,128)S(1)}, s32[]{:S(2)}) async-start(f32[1,1,20,2048]{3,1,2,0:T(1,128)} %copy-done.5), calls=%async_computation.7 | async-start | bytes 229376 | tf_op jit(solution)/shard_map/slice | solution.py:67
  37.0 12.2 %slice-start.1 = ((f32[1,1,20,2048]{3,1,2,0:T(1,128)}), f32[1,1,12,2048]{3,1,2,0:T(1,128)S(1)}, s32[]{:S(2)}) async-start(f32[1,1,20,2048]{3,1,2,0:T(1,128)} %copy-done.5), calls=%async_computation.8 | async-start | bytes 196608 | tf_op jit(solution)/shard_map/slice | solution.py:68
  39.9 14.8 %all-to-all-start.1 = ((f32[8,1,2]{2,1,0:T(1,128)}), f32[8,1,2]{2,1,0:T(1,128)S(1)}, u32[]{:S(2)}, u32[]{:S(2)}) async-start(f32[8,1,2]{2,1,0:T(1,128)} %concatenate.61), calls=%async_computation.1 | async-start | bytes 8192 | tf_op jit(solution)/shard_map/all_to_all | solution.py:32
  61.8 8.1 %copy-start.1 = (f32[1,16,16,2048]{3,1,2,0:T(8,128)}, f32[1,16,16,2048]{3,1,2,0:T(8,128)S(1)}, u32[]{:S(2)}) copy-start(f32[1,16,16,2048]{3,1,2,0:T(8,128)S(1)} %get-tuple-element.17) | copy-start | bytes 6291460
  61.9 8.1 %copy-start.3 = (f32[1,16,16,2048]{3,1,2,0:T(8,128)}, f32[1,16,16,2048]{3,1,2,0:T(8,128)S(1)}, u32[]{:S(2)}) copy-start(f32[1,16,16,2048]{3,1,2,0:T(8,128)S(1)} %get-tuple-element.16) | copy-start | bytes 6291460
  69.9 7.2 %slice-start.2 = ((f32[1,1,20,2048]{3,1,2,0:T(1,128)}), f32[1,1,10,2048]{3,1,2,0:T(1,128)S(1)}, s32[]{:S(2)}) async-start(f32[1,1,20,2048]{3,1,2,0:T(1,128)} %copy-done.5), calls=%async_computation.9 | async-start | bytes 163840 | tf_op jit(solution)/shard_map/slice | solution.py:67
  69.9 7.9 %slice-start.3 = ((f32[1,1,20,2048]{3,1,2,0:T(1,128)}), f32[1,1,8,2048]{3,1,2,0:T(1,128)S(1)}, s32[]{:S(2)}) async-start(f32[1,1,20,2048]{3,1,2,0:T(1,128)} %copy-done.5), calls=%async_computation.10 | async-start | bytes 131072 | tf_op jit(solution)/shard_map/slice | solution.py:68
  73.6 8.8 %all-to-all-start.2 = ((f32[8,1,3]{2,1,0:T(1,128)}), f32[8,1,3]{2,1,0:T(1,128)S(1)}, u32[]{:S(2)}, u32[]{:S(2)}) async-start(f32[8,1,3]{2,1,0:T(1,128)} %concatenate.62), calls=%async_computation.2 | async-start | bytes 8192 | tf_op jit(solution)/shard_map/all_to_all | solution.py:32
  89.4 3.7 %copy-start.4 = (f32[1,16,12,2048]{3,1,2,0:T(8,128)}, f32[1,16,12,2048]{3,1,2,0:T(8,128)S(1)}, u32[]{:S(2)}) copy-start(f32[1,16,12,2048]{3,1,2,0:T(8,128)S(1)} %get-tuple-element.18) | copy-start | bytes 4718596
  89.4 1.5 %copy-start.8 = (f32[10,2048]{1,0:T(8,128)S(1)}, f32[10,2048]{1,0:T(8,128)}, u32[]{:S(2)}) copy-start(f32[10,2048]{1,0:T(8,128)} %slice_add_fusion.7) | copy-start | bytes 245764
  89.4 1.5 %copy-start.9 = (f32[1,1,10,2048]{3,2,1,0:T(8,128)S(1)}, f32[1,1,10,2048]{3,2,1,0:T(8,128)}, u32[]{:S(2)}) copy-start(f32[1,1,10,2048]{3,2,1,0:T(8,128)} %copy.51) | copy-start | bytes 245764
  90.9 2.1 %copy-start.10 = (f32[8,2048]{1,0:T(8,128)S(1)}, f32[8,2048]{1,0:T(8,128)}, u32[]{:S(2)}) copy-start(f32[8,2048]{1,0:T(8,128)} %broadcast_add_fusion) | copy-start | bytes 196612
  90.9 2.1 %copy-start.11 = (f32[1,1,8,2048]{3,2,1,0:T(8,128)S(1)}, f32[1,1,8,2048]{3,2,1,0:T(8,128)}, u32[]{:S(2)}) copy-start(f32[1,1,8,2048]{3,2,1,0:T(8,128)} %copy.55) | copy-start | bytes 196612
  121.6 8.5 %all-to-all-start.5 = ((f32[4,1,7]{2,1,0:T(1,128)}), f32[4,1,7]{2,1,0:T(1,128)S(1)}, u32[]{:S(2)}, u32[]{:S(2)}) async-start(f32[4,1,7]{2,1,0:T(1,128)} %concatenate.67), calls=%async_computation.5 | async-start | bytes 4096 | tf_op jit(solution)/shard_map/all_to_all | solution.py:32
  130.1 16.0 %all-to-all-start.6 = ((f32[1,16,8,2048]{3,2,0,1:T(8,128)}), f32[1,16,8,2048]{3,2,0,1:T(8,128)S(1)}, u32[]{:S(2)}, u32[]{:S(2)}) async-start(f32[1,16,8,2048]{3,2,0,1:T(8,128)} %copy.32), calls=%async_computation.6 | async-start | bytes 2097152 | tf_op jit(solution)/shard_map/all_to_all | solution.py:108

commit v3 on v2

--- a/solution.py
+++ b/solution.py
@@ -36,6 +36,17 @@
     n = lax.axis_size("tile")
     g = gather_rows(v, "tile").reshape((n,) + v.shape)
     return jnp.sum(g, axis=0)
+
+
+def butterfly_sum(v, axis):
+    n = lax.axis_size(axis)
+    if n & (n - 1):
+        return lax.psum(v, axis)
+    s = 1
+    while s < n:
+        v = v + lax.ppermute(v, axis, [(i, i ^ s) for i in range(n)])
+        s *= 2
+    return v
 
 
 def halo_rows(block, width):
@@ -106,11 +117,18 @@
         alphas.append(alpha)
     w_own = own(w, off)
     w_back = lax.all_to_all(w_own, "trait", split_axis=1, concat_axis=0, tiled=True)
-    sums = tile_sum(jnp.sum(w_own * w_own, axis=(1, 2, 3))[:, None])
-    scalars = jnp.concatenate(
-        [jnp.stack(alphas, axis=1), jnp.stack(betas, axis=1), sums, norm[:, None]], axis=1
+    partial = jnp.sum(w_own * w_own, axis=(1, 2, 3))[:, None]
+    first = (lax.axis_index("tile") == 0).astype(jnp.float32)
+    known = jnp.concatenate([jnp.stack(alphas, axis=1), jnp.stack(betas, axis=1)], axis=1)
+    mine = jnp.concatenate([known * first, partial, norm[:, None] * first], axis=1)
+    probes_local = mine.shape[0]
+    n_trait = lax.axis_size("trait")
+    spread = lax.dynamic_update_slice(
+        jnp.zeros((probes_local * n_trait, mine.shape[1]), jnp.float32),
+        mine,
+        (lax.axis_index("trait") * probes_local, 0),
     )
-    scalars = gather_rows(scalars, "trait")
+    scalars = butterfly_sum(butterfly_sum(spread, "tile"), "trait")
     beta = jnp.sqrt(scalars[:, 2 * iters - 1] + epsilon)
     norm_all = scalars[:, 2 * iters]
     last = (w_back / beta[:, None, None, None]) * norm_all[:, None, None, None]

time: 149 us -> 140 us (0.940)
  blocking collectives: 15.9 us -> 0 us
  starting transfers between devices: 32.7 us -> 39 us
    all_to_all x2 -> x0, blocking collectives: 15.9 us -> none  [gather_rows(): lax.all_to_all(jnp.concatenate([v] * n, axis=0), axis, 0, 0, tiled=True)]
    all_to_all x1, waiting for transfers between devices: 11.5 us -> 0.01 us  [shards(): lax.all_to_all(w_own, 'trait', split_axis=1, concat_axis=0, tiled=True)]
    ppermute x0 -> x5, waiting for transfers between devices: none -> 11.2 us  [butterfly_sum(): v = v + lax.ppermute(v, axis, [(i, i ^ s) for i in range(n)])]
    ppermute x0 -> x5, starting transfers between devices: none -> 5.29 us  [butterfly_sum(): v = v + lax.ppermute(v, axis, [(i, i ^ s) for i in range(n)])]
    div x1 -> x0, other arithmetic: 5.17 us -> none  [shards(): q = z2 / norm[:, None, None, None]]
    sub x0 -> x1, other arithmetic: none -> 5.17 us  [shards(): w = v - alpha[:, None, None, None] * q]
    all_to_all x3, waiting for transfers between devices: 12.4 us -> 14.3 us  [gather_rows(): lax.all_to_all(jnp.concatenate([v] * n, axis=0), axis, 0, 0, tiled=True)]
    unnamed x31 -> x36, local copies, waits for them, and re-layouts: 3.63 us -> 3.71 us
  transfers between devices with their start and end apart: 9 -> 14, of which waited for: 7 -> 11; matrix products, arithmetic and copies ran while one was open for 4% -> 6% of each run, Pallas kernels for 0% -> 0%
where the time goes in v3:
time: 140 us; the launch traced here: 139 us
  other arithmetic  47.2 us (34%)
  starting transfers between devices  39 us (28%)
  waiting for transfers between devices  29.3 us (21%)
  local copies, waits for them, and re-layouts  10.6 us (8%)
  matrix products  6.48 us (5%)
  between operations  6.45 us (5%)
    all_to_all x3, starting transfers between devices, gather_rows(): lax.all_to_all(jnp.concatenate([v] * n, axis=0), axis, 0, 0, tiled=True)  15.7 us
    all_to_all x3, waiting for transfers between devices, gather_rows(): lax.all_to_all(jnp.concatenate([v] * n, axis=0), axis, 0, 0, tiled=True)  14.3 us
    ppermute x5, waiting for transfers between devices, butterfly_sum(): v = v + lax.ppermute(v, axis, [(i, i ^ s) for i in range(n)])  11.2 us
    mul x3, other arithmetic, apply_a(): land_ext[off + 1:off + r - 1]  9.95 us
    dot_general x3, matrix products, apply_a(): jnp.einsum('ts,psrc->ptrc', trait_covariance, x, precision=lax.Precision....  6.48 us
    mul x2, other arithmetic, apply_a(): land_ext[off + 2:off + r - 2]  6.38 us
    ppermute x2, starting transfers between devices, halo_rows(): lax.ppermute(lax.slice_in_dim(block, rows - width, rows, axis=dim), 'tile...  6.03 us
    ppermute x5, starting transfers between devices, butterfly_sum(): v = v + lax.ppermute(v, axis, [(i, i ^ s) for i in range(n)])  5.29 us
  transfers between devices with their start and end apart: 14, of which 11 were waited for; matrix products, arithmetic and copies ran while one was open for 6% of the time, Pallas kernels for 0%

profile of v3, /device:TPU:0, one launch (start us, length us, event | category | flops | bytes accessed | tf_op | source)
XLA Modules:
  0.0 139.0 jit_solution(13893989693359481667)
XLA Ops:
  0.7 2.2 %multiply_convert_fusion = bf16[4,4,8,2048]{3,2,1,0:T(8,128)(2,1)} fusion(s32[4,4,8,2048]{3,2,1,0:T(8,128)} %param.4, s32[8,2048]{1,0:T(8,128)} %param.5), kind=kLoop, calls=%fused_computation.150 | loop fusion | flops 1048576 | bytes 1638400 | tf_op jit(solution)/shard_map/convert_element_type | solution.py:67
  2.9 5.2 %all-to-all-start = ((bf16[4,4,8,2048]{3,2,1,0:T(8,128)(2,1)}), bf16[4,4,8,2048]{3,2,1,0:T(8,128)(2,1)S(1)}, u32[]{:S(2)}, u32[]{:S(2)}) async-start(bf16[4,4,8,2048]{3,2,1,0:T(8,128)(2,1)} %multiply_convert_fusion), calls=%async_computation | async-start | bytes 1048576 | tf_op jit(solution)/shard_map/all_to_all | solution.py:68
  12.2 2.2 %collective-permute-done.3 = f32[6,2048]{1,0:T(8,128)S(1)} collective-permute-done((f32[6,2048]{1,0:T(8,128)S(1)}, f32[6,2048]{1,0:T(8,128)S(1)}, u32[]{:S(2)}, u32[]{:S(2)}) %collective-permute-start.3) | collective-permute-done | bytes 49184 | tf_op jit(solution)/shard_map/ppermute | solution.py:60
  16.5 4.6 %collective-permute-start = (bf16[1,16,6,2048]{3,1,2,0:T(8,128)(2,1)S(1)}, bf16[1,16,6,2048]{3,1,2,0:T(8,128)(2,1)S(1)}, u32[]{:S(2)}, u32[]{:S(2)}) collective-permute-start(bf16[1,16,6,2048]{3,1,2,0:T(8,128)(2,1)S(1)} %get-tuple-element.20), channel_id=1, source_target_pairs={{0,1},{1,2},{2,3},{3,4},{4,5},{5,6},{6,7},{8,9},{9,10},{10,11},{11... | collective-permute-start | bytes 1179656 | tf_op jit(solution)/shard_map/ppermute | solution.py:59
  25.1 3.0 %convolution_bitcast_fusion = f32[1,16,20,2048]{3,1,2,0:T(8,128)S(1)} fusion(bf16[16,6,2048]{2,0,1:T(8,128)(2,1)S(1)} %bitcast.80, bf16[16,8,2048]{2,0,1:T(8,128)(2,1)S(1)} %copy.26, bf16[16,6,2048]{2,0,1:T(8,128)(2,1)S(1)} %bitcast.79, f32[16]{0:T(128)S(1)} %gather_fusion, f32[16,16]{1,0:T(8,128)S(1)} %copy-done), kind=kOutput, calls=%fused_computation.1 | convolution fusion | flops 128450560 | bytes 3933248 | tf_op jit(solution)/shard_map/ts,psrc->ptrc/dot_general | solution.py:77
  28.1 4.4 %fusion.7 = f32[1,16,18,2048]{3,1,2,0:T(8,128)S(1)} fusion(f32[1,16,20,2048]{3,1,2,0:T(8,128)S(1)} %convolution_bitcast_fusion, f32[18,2048]{1,0:T(8,128)S(1)} %slice_add_fusion.6, f32[18,2048]{1,0:T(8,128)S(1)} %bitcast.85), kind=kLoop, calls=%fused_computation.17 | loop fusion | flops 7667712 | bytes 12451840 | tf_op jit(solution)/shard_map/mul | solution.py:78
  32.5 3.9 %fusion.18 = f32[1,16,16,2048]{3,1,2,0:T(8,128)S(1)} fusion(f32[1,16,18,2048]{3,1,2,0:T(8,128)S(1)} %fusion.7, f32[16,2048]{1,0:T(8,128)S(1)} %slice_add_fusion.10, f32[16,2048]{1,0:T(8,128)S(1)} %bitcast.81), kind=kLoop, calls=%fused_computation.36 | loop fusion | flops 6815744 | bytes 11010048 | tf_op jit(solution)/shard_map/mul | solution.py:79
  36.7 1.5 %copy-done.2 = f32[1,16,20,2048]{3,1,2,0:T(8,128)} copy-done((f32[1,16,20,2048]{3,1,2,0:T(8,128)}, f32[1,16,20,2048]{3,1,2,0:T(8,128)S(1)}, u32[]{:S(2)}) %copy-start.2) | copy-done | bytes 2621464
  41.1 8.9 %all-to-all-start.1 = ((f32[8,1,2]{2,1,0:T(1,128)}), f32[8,1,2]{2,1,0:T(1,128)S(1)}, u32[]{:S(2)}, u32[]{:S(2)}) async-start(f32[8,1,2]{2,1,0:T(1,128)} %concatenate.68), calls=%async_computation.1 | async-start | bytes 8192 | tf_op jit(solution)/shard_map/all_to_all | solution.py:32
  50.8 4.9 %all-to-all-done.1 = f32[8,1,2]{2,1,0:T(1,128)S(1)} async-done(((f32[8,1,2]{2,1,0:T(1,128)}), f32[8,1,2]{2,1,0:T(1,128)S(1)}, u32[]{:S(2)}, u32[]{:S(2)}) %all-to-all-start.1) | async-done | bytes 96 | tf_op jit(solution)/shard_map/all_to_all | solution.py:32
  57.6 5.2 %multiply_subtract_fusion = (f32[1,16,16,2048]{3,1,2,0:T(8,128)S(1)}, f32[1,16,16,2048]{3,1,2,0:T(8,128)S(1)}) fusion(f32[]{:T(128)} %bitcast.14, f32[]{:T(128)} %bitcast.13, f32[1,16,20,2048]{3,1,2,0:T(8,128)} %copy-done.2, f32[1,16,18,2048]{3,1,2,0:T(8,128)S(1)} %fusion.7, f32[16,2048]{1,0:T(8,128)S(1)} %slice_add_fusion.10, f32[16,2048]{1,0:T(8,128)S(1)} %bitcast.82), kind=kLoop, calls=%fused_computation.46 | loop fusion | flops 8912896 | bytes 15204360 | tf_op jit(solution)/shard_map/sub | solution.py:97
  62.8 2.0 %convolution_bitcast_fusion.1 = f32[1,16,16,2048]{3,1,2,0:T(8,128)S(1)} fusion(f32[1,16,16,2048]{3,1,2,0:T(8,128)S(1)} %get-tuple-element.16, f32[16,16]{1,0:T(8,128)S(1)} %copy-done), kind=kOutput, calls=%fused_computation.2 | convolution fusion | flops 100663296 | bytes 4195328 | tf_op jit(solution)/shard_map/ts,psrc->ptrc/dot_general | solution.py:77
  64.9 3.5 %fusion.30 = f32[1,16,14,2048]{3,1,2,0:T(8,128)S(1)} fusion(f32[1,16,16,2048]{3,1,2,0:T(8,128)S(1)} %convolution_bitcast_fusion.1, f32[14,2048]{1,0:T(8,128)S(1)} %copy-done.9, f32[14,2048]{1,0:T(8,128)S(1)} %bitcast.87), kind=kLoop, calls=%fused_computation.58 | loop fusion | flops 5963776 | bytes 9699328 | tf_op jit(solution)/shard_map/mul | solution.py:78
  68.4 2.5 %fusion.41 = f32[1,16,12,2048]{3,1,2,0:T(8,128)S(1)} fusion(f32[1,16,14,2048]{3,1,2,0:T(8,128)S(1)} %fusion.30, f32[12,2048]{1,0:T(8,128)S(1)} %copy-done.6, f32[12,2048]{1,0:T(8,128)S(1)} %bitcast.83), kind=kLoop, calls=%fused_computation.77 | loop fusion | flops 5111808 | bytes 8388608 | tf_op jit(solution)/shard_map/mul | solution.py:79
  72.0 2.0 %maximum_bitcast_fusion.1 = f32[3]{0:T(128)S(1)} fusion(f32[1,1]{1,0:T(1,128)} %bitcast.21, f32[1,1]{1,0:T(1,128)} %bitcast.20, f32[1,1]{1,0:T(1,128)} %bitcast.15), kind=kLoop, calls=%fused_computation.172 | loop fusion | flops 6 | bytes 24 | tf_op jit(solution)/shard_map/stack | solution.py:108
  74.7 3.5 %all-to-all-start.2 = ((f32[8,1,3]{2,1,0:T(1,128)}), f32[8,1,3]{2,1,0:T(1,128)S(1)}, u32[]{:S(2)}, u32[]{:S(2)}) async-start(f32[8,1,3]{2,1,0:T(1,128)} %concatenate.69), calls=%async_computation.2 | async-start | bytes 8192 | tf_op jit(solution)/shard_map/all_to_all | solution.py:32
  79.5 4.0 %all-to-all-done.2 = f32[8,1,3]{2,1,0:T(1,128)S(1)} async-done(((f32[8,1,3]{2,1,0:T(1,128)}), f32[8,1,3]{2,1,0:T(1,128)S(1)}, u32[]{:S(2)}, u32[]{:S(2)}) %all-to-all-start.2) | async-done | bytes 128 | tf_op jit(solution)/shard_map/all_to_all | solution.py:32
  86.1 4.5 %slice_divide_fusion.1 = (f32[1,16,12,2048]{3,1,2,0:T(8,128)S(1)}, f32[1,16,12,2048]{3,1,2,0:T(8,128)S(1)}) fusion(f32[1,16,16,2048]{3,1,2,0:T(8,128)} %copy-done.1, f32[]{:T(128)} %bitcast.24, f32[]{:T(128)} %bitcast.25, f32[1,16,16,2048]{3,1,2,0:T(8,128)} %copy-done.3, f32[1,16,14,2048]{3,1,2,0:T(8,128)S(1)} %fusion.30, f32[12,2048]{1,0:T(8,128)} %slice_add_fusion.9, ...), kind=kLoop, calls=%fused_computation.82 | loop fusion | flops 7471104 | bytes 13074440 | tf_op jit(solution)/shard_map/div | solution.py:112
  92.1 2.1 %fusion.55 = f32[1,16,10,2048]{3,1,2,0:T(8,128)S(1)} fusion(f32[1,16,12,2048]{3,1,2,0:T(8,128)S(1)} %convolution_bitcast_fusion.2, f32[10,2048]{1,0:T(8,128)S(1)} %copy-done.8, f32[10,2048]{1,0:T(8,128)S(1)} %bitcast.86), kind=kLoop, calls=%fused_computation.101 | loop fusion | flops 4259840 | bytes 7077888 | tf_op jit(solution)/shard_map/mul | solution.py:78
  94.3 2.4 %multiply_reduce_fusion.3 = (f32[]{:T(128)}, f32[]{:T(128)}, f32[]{:T(128)}, f32[1,16,8,2048]{3,1,2,0:T(8,128)S(1)}) fusion(f32[1,16,12,2048]{3,1,2,0:T(8,128)S(1)} %get-tuple-element.19, f32[1,16,12,2048]{3,1,2,0:T(8,128)S(1)} %get-tuple-element.18, f32[1,16,10,2048]{3,1,2,0:T(8,128)S(1)} %fusion.55, f32[8,2048]{1,0:T(8,128)S(1)} %copy-done.12, ...), kind=kLoop, calls=%fused_computation.147 | loop fusion | flops 4980733 | bytes 7733260 | tf_op jit(solution)/shard_map/reduce_sum | solution.py:85
  96.6 2.0 %maximum_bitcast_fusion.2 = f32[3]{0:T(128)S(1)} fusion(f32[1,1]{1,0:T(1,128)} %bitcast.32, f32[1,1]{1,0:T(1,128)} %bitcast.31, f32[1,1]{1,0:T(1,128)} %bitcast.26), kind=kLoop, calls=%fused_computation.173 | loop fusion | flops 6 | bytes 24 | tf_op jit(solution)/shard_map/stack | solution.py:108
  99.2 3.3 %all-to-all-start.3 = ((f32[8,1,3]{2,1,0:T(1,128)}), f32[8,1,3]{2,1,0:T(1,128)S(1)}, u32[]{:S(2)}, u32[]{:S(2)}) async-start(f32[8,1,3]{2,1,0:T(1,128)} %concatenate.71), calls=%async_computation.3 | async-start | bytes 8192 | tf_op jit(solution)/shard_map/all_to_all | solution.py:32
  102.6 5.4 %all-to-all-done.3 = f32[8,1,3]{2,1,0:T(1,128)S(1)} async-done(((f32[8,1,3]{2,1,0:T(1,128)}), f32[8,1,3]{2,1,0:T(1,128)S(1)}, u32[]{:S(2)}, u32[]{:S(2)}) %all-to-all-start.3) | async-done | bytes 128 | tf_op jit(solution)/shard_map/all_to_all | solution.py:32
  110.7 2.2 %multiply_reduce_fusion = (f32[]{:T(128)}, f32[1,16,8,2048]{3,1,2,0:T(8,128)S(1)}) fusion(f32[1,16,12,2048]{3,1,2,0:T(8,128)S(1)} %get-tuple-element.19, f32[]{:T(128)} %bitcast.36, f32[1,16,12,2048]{3,1,2,0:T(8,128)} %copy-done.4, f32[1,16,8,2048]{3,1,2,0:T(8,128)S(1)} %get-tuple-element.15, f32[]{:T(128)} %bitcast.35), kind=kLoop, calls=%fused_computation.143 | loop fusion | flops 2097151 | bytes 4194316 | tf_op jit(solution)/shard_map/reduce_sum | solution.py:120
  112.9 1.6 %copy.30 = f32[1,16,8,2048]{3,2,0,1:T(8,128)} copy(f32[1,16,8,2048]{3,1,2,0:T(8,128)S(1)} %get-tuple-element.14) | data formatting | bytes 2097152 | tf_op jit(solution)/shard_map/sub | solution.py:114
  114.5 4.2 %all-to-all-start.4 = ((f32[1,16,8,2048]{3,2,0,1:T(8,128)}), f32[1,16,8,2048]{3,2,0,1:T(8,128)S(1)}, u32[]{:S(2)}, u32[]{:S(2)}) async-start(f32[1,16,8,2048]{3,2,0,1:T(8,128)} %copy.30), calls=%async_computation.4 | async-start | bytes 2097152 | tf_op jit(solution)/shard_map/all_to_all | solution.py:119
  122.2 3.0 %collective-permute-done.5 = f32[4,7]{1,0:T(4,128)S(1)} collective-permute-done((f32[4,7]{1,0:T(4,128)S(1)}, f32[4,7]{1,0:T(4,128)S(1)}, u32[]{:S(2)}, u32[]{:S(2)}) %collective-permute-start.5) | collective-permute-done | bytes 144 | tf_op jit(solution)/shard_map/ppermute | solution.py:47
  125.8 3.9 %collective-permute-done.6 = f32[4,7]{1,0:T(4,128)S(1)} collective-permute-done((f32[4,7]{1,0:T(4,128)S(1)}, f32[4,7]{1,0:T(4,128)S(1)}, u32[]{:S(2)}, u32[]{:S(2)}) %collective-permute-start.6) | collective-permute-done | bytes 144 | tf_op jit(solution)/shard_map/ppermute | solution.py:47
  129.7 2.0 %collective-permute-start.7 = (f32[4,7]{1,0:T(4,128)S(1)}, f32[4,7]{1,0:T(4,128)S(1)}, u32[]{:S(2)}, u32[]{:S(2)}) collective-permute-start(f32[4,7]{1,0:T(4,128)S(1)} %add.231), channel_id=1, source_target_pairs={{0,8},{8,0},{16,24},{24,16},{1,9},{9,1},{17,25},{25,17},{2,10},{10... | collective-permute-start | bytes 344 | tf_op jit(solution)/shard_map/ppermute | solution.py:47
  131.8 1.6 %collective-permute-done.7 = f32[4,7]{1,0:T(4,128)S(1)} collective-permute-done((f32[4,7]{1,0:T(4,128)S(1)}, f32[4,7]{1,0:T(4,128)S(1)}, u32[]{:S(2)}, u32[]{:S(2)}) %collective-permute-start.7) | collective-permute-done | bytes 144 | tf_op jit(solution)/shard_map/ppermute | solution.py:47
  133.3 2.0 %collective-permute-start.8 = (f32[4,7]{1,0:T(4,128)S(1)}, f32[4,7]{1,0:T(4,128)S(1)}, u32[]{:S(2)}, u32[]{:S(2)}) collective-permute-start(f32[4,7]{1,0:T(4,128)S(1)} %add.232), channel_id=1, source_target_pairs={{0,16},{8,24},{16,0},{24,8},{1,17},{9,25},{17,1},{25,9},{2,18},{10... | collective-permute-start | bytes 344 | tf_op jit(solution)/shard_map/ppermute | solution.py:47
  135.3 1.6 %collective-permute-done.8 = f32[4,7]{1,0:T(4,128)S(1)} collective-permute-done((f32[4,7]{1,0:T(4,128)S(1)}, f32[4,7]{1,0:T(4,128)S(1)}, u32[]{:S(2)}, u32[]{:S(2)}) %collective-permute-start.8) | collective-permute-done | bytes 144 | tf_op jit(solution)/shard_map/ppermute | solution.py:47
  (101 shorter events, 27.5 us)
Async XLA Ops:
  0.6 10.9 %copy-start = (f32[16,16]{1,0:T(8,128)S(1)}, f32[16,16]{1,0:T(8,128)}, u32[]{:S(2)}) copy-start(f32[16,16]{1,0:T(8,128)} %param.7) | copy-start | bytes 3076
  0.6 7.4 %copy-start.7 = (f32[8,2048]{1,0:T(8,128)S(1)}, f32[8,2048]{1,0:T(8,128)}, u32[]{:S(2)}) copy-start(f32[8,2048]{1,0:T(8,128)} %param.6) | copy-start | bytes 196612
  2.9 13.2 %all-to-all-start = ((bf16[4,4,8,2048]{3,2,1,0:T(8,128)(2,1)}), bf16[4,4,8,2048]{3,2,1,0:T(8,128)(2,1)S(1)}, u32[]{:S(2)}, u32[]{:S(2)}) async-start(bf16[4,4,8,2048]{3,2,1,0:T(8,128)(2,1)} %multiply_convert_fusion), calls=%async_computation | async-start | bytes 1048576 | tf_op jit(solution)/shard_map/all_to_all | solution.py:68
  8.1 4.1 %collective-permute-start.2 = (f32[6,2048]{1,0:T(8,128)S(1)}, f32[6,2048]{1,0:T(8,128)S(1)}, u32[]{:S(2)}, u32[]{:S(2)}) collective-permute-start(f32[6,2048]{1,0:T(8,128)S(1)} %get-tuple-element.22), channel_id=1, source_target_pairs={{0,1},{1,2},{2,3},{3,4},{4,5},{5,6},{6,7},{8,9},{9,10},{10,11},{11... | collective-permute-start | bytes 147464 | tf_op jit(solution)/shard_map/ppermute | solution.py:59
  9.6 4.8 %collective-permute-start.3 = (f32[6,2048]{1,0:T(8,128)S(1)}, f32[6,2048]{1,0:T(8,128)S(1)}, u32[]{:S(2)}, u32[]{:S(2)}) collective-permute-start(f32[6,2048]{1,0:T(8,128)S(1)} %get-tuple-element.23), channel_id=1, source_target_pairs={{1,0},{2,1},{3,2},{4,3},{5,4},{6,5},{7,6},{9,8},{10,9},{11,10},{12... | collective-permute-start | bytes 147464 | tf_op jit(solution)/shard_map/ppermute | solution.py:60
  16.5 6.8 %collective-permute-start = (bf16[1,16,6,2048]{3,1,2,0:T(8,128)(2,1)S(1)}, bf16[1,16,6,2048]{3,1,2,0:T(8,128)(2,1)S(1)}, u32[]{:S(2)}, u32[]{:S(2)}) collective-permute-start(bf16[1,16,6,2048]{3,1,2,0:T(8,128)(2,1)S(1)} %get-tuple-element.20), channel_id=1, source_target_pairs={{0,1},{1,2},{2,3},{3,4},{4,5},{5,6},{6,7},{8,9},{9,10},{10,11},{11... | collective-permute-start | bytes 1179656 | tf_op jit(solution)/shard_map/ppermute | solution.py:59
  21.0 3.6 %collective-permute-start.1 = (bf16[1,16,6,2048]{3,1,2,0:T(8,128)(2,1)S(1)}, bf16[1,16,6,2048]{3,1,2,0:T(8,128)(2,1)S(1)}, u32[]{:S(2)}, u32[]{:S(2)}) collective-permute-start(bf16[1,16,6,2048]{3,1,2,0:T(8,128)(2,1)S(1)} %get-tuple-element.21), channel_id=1, source_target_pairs={{1,0},{2,1},{3,2},{4,3},{5,4},{6,5},{7,6},{9,8},{10,9},{11,10},{12... | collective-permute-start | bytes 1179656 | tf_op jit(solution)/shard_map/ppermute | solution.py:60
  25.0 3.2 %copy-start.5 = (f32[1,1,20,2048]{3,1,2,0:T(1,128)}, f32[1,1,20,2048]{3,1,2,0:T(1,128)S(1)}, u32[]{:S(2)}) copy-start(f32[1,1,20,2048]{3,1,2,0:T(1,128)S(1)} %slice_multiply_fusion.10) | copy-start | bytes 491524
  38.2 11.8 %slice-start = ((f32[1,1,20,2048]{3,1,2,0:T(1,128)}), f32[1,1,14,2048]{3,1,2,0:T(1,128)S(1)}, s32[]{:S(2)}) async-start(f32[1,1,20,2048]{3,1,2,0:T(1,128)} %copy-done.5), calls=%async_computation.5 | async-start | bytes 229376 | tf_op jit(solution)/shard_map/slice | solution.py:78
  38.2 12.5 %slice-start.1 = ((f32[1,1,20,2048]{3,1,2,0:T(1,128)}), f32[1,1,12,2048]{3,1,2,0:T(1,128)S(1)}, s32[]{:S(2)}) async-start(f32[1,1,20,2048]{3,1,2,0:T(1,128)} %copy-done.5), calls=%async_computation.6 | async-start | bytes 196608 | tf_op jit(solution)/shard_map/slice | solution.py:79
  41.1 14.5 %all-to-all-start.1 = ((f32[8,1,2]{2,1,0:T(1,128)}), f32[8,1,2]{2,1,0:T(1,128)S(1)}, u32[]{:S(2)}, u32[]{:S(2)}) async-start(f32[8,1,2]{2,1,0:T(1,128)} %concatenate.68), calls=%async_computation.1 | async-start | bytes 8192 | tf_op jit(solution)/shard_map/all_to_all | solution.py:32
  62.8 8.1 %copy-start.1 = (f32[1,16,16,2048]{3,1,2,0:T(8,128)}, f32[1,16,16,2048]{3,1,2,0:T(8,128)S(1)}, u32[]{:S(2)}) copy-start(f32[1,16,16,2048]{3,1,2,0:T(8,128)S(1)} %get-tuple-element.16) | copy-start | bytes 6291460
  62.8 8.1 %copy-start.3 = (f32[1,16,16,2048]{3,1,2,0:T(8,128)}, f32[1,16,16,2048]{3,1,2,0:T(8,128)S(1)}, u32[]{:S(2)}) copy-start(f32[1,16,16,2048]{3,1,2,0:T(8,128)S(1)} %get-tuple-element.17) | copy-start | bytes 6291460
  62.8 2.0 %copy-start.9 = (f32[14,2048]{1,0:T(8,128)S(1)}, f32[14,2048]{1,0:T(8,128)}, u32[]{:S(2)}) copy-start(f32[14,2048]{1,0:T(8,128)} %slice_add_fusion.8) | copy-start | bytes 344068
  62.8 2.0 %copy-start.11 = (f32[1,1,14,2048]{3,2,1,0:T(8,128)S(1)}, f32[1,1,14,2048]{3,2,1,0:T(8,128)}, u32[]{:S(2)}) copy-start(f32[1,1,14,2048]{3,2,1,0:T(8,128)} %copy.49) | copy-start | bytes 344068
  64.8 3.5 %copy-start.6 = (f32[12,2048]{1,0:T(8,128)S(1)}, f32[12,2048]{1,0:T(8,128)}, u32[]{:S(2)}) copy-start(f32[12,2048]{1,0:T(8,128)} %slice_add_fusion.9) | copy-start | bytes 294916
  70.9 7.3 %slice-start.2 = ((f32[1,1,20,2048]{3,1,2,0:T(1,128)}), f32[1,1,10,2048]{3,1,2,0:T(1,128)S(1)}, s32[]{:S(2)}) async-start(f32[1,1,20,2048]{3,1,2,0:T(1,128)} %copy-done.5), calls=%async_computation.7 | async-start | bytes 163840 | tf_op jit(solution)/shard_map/slice | solution.py:78
  70.9 8.0 %slice-start.3 = ((f32[1,1,20,2048]{3,1,2,0:T(1,128)}), f32[1,1,8,2048]{3,1,2,0:T(1,128)S(1)}, s32[]{:S(2)}) async-start(f32[1,1,20,2048]{3,1,2,0:T(1,128)} %copy-done.5), calls=%async_computation.8 | async-start | bytes 131072 | tf_op jit(solution)/shard_map/slice | solution.py:79
  74.7 8.8 %all-to-all-start.2 = ((f32[8,1,3]{2,1,0:T(1,128)}), f32[8,1,3]{2,1,0:T(1,128)S(1)}, u32[]{:S(2)}, u32[]{:S(2)}) async-start(f32[8,1,3]{2,1,0:T(1,128)} %concatenate.69), calls=%async_computation.2 | async-start | bytes 8192 | tf_op jit(solution)/shard_map/all_to_all | solution.py:32
  90.6 3.7 %copy-start.4 = (f32[1,16,12,2048]{3,1,2,0:T(8,128)}, f32[1,16,12,2048]{3,1,2,0:T(8,128)S(1)}, u32[]{:S(2)}) copy-start(f32[1,16,12,2048]{3,1,2,0:T(8,128)S(1)} %get-tuple-element.18) | copy-start | bytes 4718596
  90.6 1.5 %copy-start.8 = (f32[10,2048]{1,0:T(8,128)S(1)}, f32[10,2048]{1,0:T(8,128)}, u32[]{:S(2)}) copy-start(f32[10,2048]{1,0:T(8,128)} %slice_add_fusion.7) | copy-start | bytes 245764
  90.6 1.5 %copy-start.10 = (f32[1,1,10,2048]{3,2,1,0:T(8,128)S(1)}, f32[1,1,10,2048]{3,2,1,0:T(8,128)}, u32[]{:S(2)}) copy-start(f32[1,1,10,2048]{3,2,1,0:T(8,128)} %copy.48) | copy-start | bytes 245764
  92.1 2.1 %copy-start.12 = (f32[8,2048]{1,0:T(8,128)S(1)}, f32[8,2048]{1,0:T(8,128)}, u32[]{:S(2)}) copy-start(f32[8,2048]{1,0:T(8,128)} %broadcast_add_fusion) | copy-start | bytes 196612
  92.1 2.1 %copy-start.13 = (f32[1,1,8,2048]{3,2,1,0:T(8,128)S(1)}, f32[1,1,8,2048]{3,2,1,0:T(8,128)}, u32[]{:S(2)}) copy-start(f32[1,1,8,2048]{3,2,1,0:T(8,128)} %copy.52) | copy-start | bytes 196612
  99.2 8.8 %all-to-all-start.3 = ((f32[8,1,3]{2,1,0:T(1,128)}), f32[8,1,3]{2,1,0:T(1,128)S(1)}, u32[]{:S(2)}, u32[]{:S(2)}) async-start(f32[8,1,3]{2,1,0:T(1,128)} %concatenate.71), calls=%async_computation.3 | async-start | bytes 8192 | tf_op jit(solution)/shard_map/all_to_all | solution.py:32
  114.5 23.4 %all-to-all-start.4 = ((f32[1,16,8,2048]{3,2,0,1:T(8,128)}), f32[1,16,8,2048]{3,2,0,1:T(8,128)S(1)}, u32[]{:S(2)}, u32[]{:S(2)}) async-start(f32[1,16,8,2048]{3,2,0,1:T(8,128)} %copy.30), calls=%async_computation.4 | async-start | bytes 2097152 | tf_op jit(solution)/shard_map/all_to_all | solution.py:119
  119.6 1.2 collective-permute-start.4
  121.6 3.6 %collective-permute-start.5 = (f32[4,7]{1,0:T(4,128)S(1)}, f32[4,7]{1,0:T(4,128)S(1)}, u32[]{:S(2)}, u32[]{:S(2)}) collective-permute-start(f32[4,7]{1,0:T(4,128)S(1)} %add.229), channel_id=1, source_target_pairs={{0,2},{1,3},{2,0},{3,1},{4,6},{5,7},{6,4},{7,5},{8,10},{9,11},{10,... | collective-permute-start | bytes 344 | tf_op jit(solution)/shard_map/ppermute | solution.py:47
  125.2 4.5 %collective-permute-start.6 = (f32[4,7]{1,0:T(4,128)S(1)}, f32[4,7]{1,0:T(4,128)S(1)}, u32[]{:S(2)}, u32[]{:S(2)}) collective-permute-start(f32[4,7]{1,0:T(4,128)S(1)} %add.230), channel_id=1, source_target_pairs={{0,4},{1,5},{2,6},{3,7},{4,0},{5,1},{6,2},{7,3},{8,12},{9,13},{10,... | collective-permute-start | bytes 344 | tf_op jit(solution)/shard_map/ppermute | solution.py:47
  129.7 3.6 %collective-permute-start.7 = (f32[4,7]{1,0:T(4,128)S(1)}, f32[4,7]{1,0:T(4,128)S(1)}, u32[]{:S(2)}, u32[]{:S(2)}) collective-permute-start(f32[4,7]{1,0:T(4,128)S(1)} %add.231), channel_id=1, source_target_pairs={{0,8},{8,0},{16,24},{24,16},{1,9},{9,1},{17,25},{25,17},{2,10},{10... | collective-permute-start | bytes 344 | tf_op jit(solution)/shard_map/ppermute | solution.py:47
  133.3 3.6 %collective-permute-start.8 = (f32[4,7]{1,0:T(4,128)S(1)}, f32[4,7]{1,0:T(4,128)S(1)}, u32[]{:S(2)}, u32[]{:S(2)}) collective-permute-start(f32[4,7]{1,0:T(4,128)S(1)} %add.232), channel_id=1, source_target_pairs={{0,16},{8,24},{16,0},{24,8},{1,17},{9,25},{17,1},{25,9},{2,18},{10... | collective-permute-start | bytes 344 | tf_op jit(solution)/shard_map/ppermute | solution.py:47
  136.9 2.1 %copy-start.14 = (f32[4,7]{1,0:T(4,128)}, f32[4,7]{1,0:T(4,128)S(1)}, u32[]{:S(2)}) copy-start(f32[4,7]{1,0:T(4,128)S(1)} %add.233) | copy-start | bytes 340
  (1 other events, 1.5 us)

commit v4 on v3

--- a/solution.py
+++ b/solution.py
@@ -87,32 +87,49 @@
     def crop(x, k):
         return x[:, :, k : x.shape[2] - k]
 
+    def reduce_tile(parts):
+        return butterfly_sum(lax.optimization_barrier(jnp.stack(parts, axis=-1)), "tile")
+
     az = apply_a(z, 0)
     z2 = crop(z, 2)
-    sums = tile_sum(jnp.stack([dot(z2, z2, 2), dot(az, z2, 2)], axis=-1))
+    sums = reduce_tile([dot(z2, z2, 2), dot(az, z2, 2)])
+    aaz = apply_a(az, 2)
     norm = jnp.sqrt(sums[:, 0] + epsilon)
     alpha = sums[:, 1] / (norm * norm)
     q = z2 / norm[:, None, None, None]
-    v = az / norm[:, None, None, None]
-    w = v - alpha[:, None, None, None] * q
-    off = 2
+    aq = az / norm[:, None, None, None]
+    w = aq - alpha[:, None, None, None] * q
+    aw = aaz / norm[:, None, None, None] - alpha[:, None, None, None] * crop(aq, 2)
+    aq = crop(aq, 2)
+    q = crop(q, 2)
+    w = crop(w, 2)
+    off = 4
     alphas = [alpha]
     betas = []
     iters = 3
     for step in range(1, iters):
-        aw = apply_a(w, off)
-        w2 = crop(w, 2)
-        q2 = crop(q, 2)
-        off += 2
-        sums = tile_sum(
-            jnp.stack([dot(w2, w2, off), dot(aw, w2, off), dot(q2, w2, off)], axis=-1)
-        )
+        sums = reduce_tile([dot(w, w, off), dot(aw, w, off), dot(q, w, off)])
+        last_step = step == iters - 1
+        if not last_step:
+            aaw = apply_a(aw, off)
         beta = jnp.sqrt(sums[:, 0] + epsilon)
         alpha = sums[:, 1] / (beta * beta) - sums[:, 2]
-        q_next = w2 / beta[:, None, None, None]
-        v = aw / beta[:, None, None, None] - beta[:, None, None, None] * q2
-        w = v - alpha[:, None, None, None] * q_next
-        q = q_next
+        q_next = w / beta[:, None, None, None]
+        w_next = aw / beta[:, None, None, None] - beta[:, None, None, None] * q - alpha[:, None, None, None] * q_next
+        if not last_step:
+            aw_next = (
+                aaw / beta[:, None, None, None]
+                - beta[:, None, None, None] * crop(aq, 2)
+                - alpha[:, None, None, None] * crop(aw, 2) / beta[:, None, None, None]
+            )
+            aq = crop(aw, 2) / beta[:, None, None, None]
+            q = crop(q_next, 2)
+            w = crop(w_next, 2)
+            aw = aw_next
+            off += 2
+        else:
+            q = q_next
+            w = w_next
         betas.append(beta)
         alphas.append(alpha)
     w_own = own(w, off)

time: 140 us -> 128 us (0.914)
  other arithmetic: 47.2 us -> 38.5 us
  local copies, waits for them, and re-layouts: 10.6 us -> 5.41 us
  starting transfers between devices: 39 us -> 43.2 us
  waiting for transfers between devices: 29.3 us -> 27.3 us
    ppermute x5 -> x14, starting transfers between devices: 5.29 us -> 26.8 us  [butterfly_sum(): v = v + lax.ppermute(v, axis, [(i, i ^ s) for i in range(n)])]
    all_to_all x3 -> x0, starting transfers between devices: 15.7 us -> none  [gather_rows(): lax.all_to_all(jnp.concatenate([v] * n, axis=0), axis, 0, 0, tiled=True)]
    all_to_all x3 -> x0, waiting for transfers between devices: 14.3 us -> none  [gather_rows(): lax.all_to_all(jnp.concatenate([v] * n, axis=0), axis, 0, 0, tiled=True)]
    ppermute x5 -> x14, waiting for transfers between devices: 11.2 us -> 20.9 us  [butterfly_sum(): v = v + lax.ppermute(v, axis, [(i, i ^ s) for i in range(n)])]
    div x1, other arithmetic: 4.5 us -> 0.19 us  [shards(): q_next = w / beta[:, None, None, None]]
    unnamed x36 -> x14, local copies, waits for them, and re-layouts: 3.71 us -> 0.24 us
    add x6, other arithmetic: 2.69 us -> 0.11 us  [nine_valid(): kappa_rows + 2.0 * along_cols + 2.0 * along_rows]
    mul x2 -> x1, other arithmetic: 6.38 us -> 3.87 us  [apply_a(): land_ext[off + 2:off + r - 2]]
  transfers between devices with their start and end apart: 14 -> 20, of which waited for: 11 -> 15; matrix products, arithmetic and copies ran while one was open for 6% -> 7% of each run, Pallas kernels for 0% -> 0%
where the time goes in v4:
time: 128 us; the launch traced here: 127 us
  starting transfers between devices  43.2 us (34%)
  other arithmetic  38.5 us (30%)
  waiting for transfers between devices  27.3 us (21%)
  matrix products  6.47 us (5%)
  between operations  6.41 us (5%)
  local copies, waits for them, and re-layouts  5.41 us (4%)
    ppermute x14, starting transfers between devices, butterfly_sum(): v = v + lax.ppermute(v, axis, [(i, i ^ s) for i in range(n)])  26.8 us
    ppermute x14, waiting for transfers between devices, butterfly_sum(): v = v + lax.ppermute(v, axis, [(i, i ^ s) for i in range(n)])  20.9 us
    mul x3, other arithmetic, apply_a(): land_ext[off + 1:off + r - 1]  10.1 us
    dot_general x3, matrix products, apply_a(): jnp.einsum('ts,psrc->ptrc', trait_covariance, x, precision=lax.Precision....  6.47 us
    another operation x3, other arithmetic, reduce_tile(): jnp.stack(parts, axis=-1)  5.28 us
    all_to_all x1, starting transfers between devices, shards(): lax.all_to_all(signed, 'trait', split_axis=0, concat_axis=1, tiled=True)  5.19 us
    ppermute x2, waiting for transfers between devices, halo_rows(): lax.ppermute(lax.slice_in_dim(block, 0, width, axis=dim), 'tile', backward)  4.76 us
    ppermute x2, starting transfers between devices, halo_rows(): lax.ppermute(lax.slice_in_dim(block, rows - width, rows, axis=dim), 'tile...  4.75 us
  transfers between devices with their start and end apart: 20, of which 15 were waited for; matrix products, arithmetic and copies ran while one was open for 7% of the time, Pallas kernels for 0%

profile of v4, /device:TPU:0, one launch (start us, length us, event | category | flops | bytes accessed | tf_op | source)
XLA Modules:
  0.0 127.2 jit_solution(11928990922146600163)
XLA Ops:
  0.7 2.2 %multiply_convert_fusion = bf16[4,4,8,2048]{3,2,1,0:T(8,128)(2,1)} fusion(s32[4,4,8,2048]{3,2,1,0:T(8,128)} %param.4, s32[8,2048]{1,0:T(8,128)} %param.5), kind=kLoop, calls=%fused_computation.157 | loop fusion | flops 1048576 | bytes 1638400 | tf_op jit(solution)/shard_map/convert_element_type | solution.py:67
  2.9 5.2 %all-to-all-start = ((bf16[4,4,8,2048]{3,2,1,0:T(8,128)(2,1)}), bf16[4,4,8,2048]{3,2,1,0:T(8,128)(2,1)S(1)}, u32[]{:S(2)}, u32[]{:S(2)}) async-start(bf16[4,4,8,2048]{3,2,1,0:T(8,128)(2,1)} %multiply_convert_fusion), calls=%async_computation | async-start | bytes 1048576 | tf_op jit(solution)/shard_map/all_to_all | solution.py:68
  11.6 2.8 %collective-permute-done.3 = f32[6,2048]{1,0:T(8,128)S(1)} collective-permute-done((f32[6,2048]{1,0:T(8,128)S(1)}, f32[6,2048]{1,0:T(8,128)S(1)}, u32[]{:S(2)}, u32[]{:S(2)}) %collective-permute-start.3) | collective-permute-done | bytes 49184 | tf_op jit(solution)/shard_map/ppermute | solution.py:60
  16.5 3.3 %collective-permute-start = (bf16[1,16,6,2048]{3,1,2,0:T(8,128)(2,1)S(1)}, bf16[1,16,6,2048]{3,1,2,0:T(8,128)(2,1)S(1)}, u32[]{:S(2)}, u32[]{:S(2)}) collective-permute-start(bf16[1,16,6,2048]{3,1,2,0:T(8,128)(2,1)S(1)} %get-tuple-element.20), channel_id=1, source_target_pairs={{0,1},{1,2},{2,3},{3,4},{4,5},{5,6},{6,7},{8,9},{9,10},{10,11},{11... | collective-permute-start | bytes 1179656 | tf_op jit(solution)/shard_map/ppermute | solution.py:59
  21.4 2.0 %collective-permute-done.1 = bf16[1,16,6,2048]{3,1,2,0:T(8,128)(2,1)S(1)} collective-permute-done((bf16[1,16,6,2048]{3,1,2,0:T(8,128)(2,1)S(1)}, bf16[1,16,6,2048]{3,1,2,0:T(8,128)(2,1)S(1)}, u32[]{:S(2)}, u32[]{:S(2)}) %collective-permute-start.1) | collective-permute-done | bytes 393248 | tf_op jit(solution)/shard_map/ppermute | solution.py:60
  23.8 3.0 %convolution_bitcast_fusion = f32[1,16,20,2048]{3,1,2,0:T(8,128)S(1)} fusion(bf16[16,6,2048]{2,0,1:T(8,128)(2,1)S(1)} %bitcast.71, bf16[16,8,2048]{2,0,1:T(8,128)(2,1)S(1)} %copy.14, bf16[16,6,2048]{2,0,1:T(8,128)(2,1)S(1)} %bitcast.70, f32[16]{0:T(128)S(1)} %gather_fusion, f32[16,16]{1,0:T(8,128)S(1)} %copy-done), kind=kOutput, calls=%fused_computation.1 | convolution fusion | flops 128450560 | bytes 3933248 | tf_op jit(solution)/shard_map/ts,psrc->ptrc/dot_general | solution.py:77
  26.8 4.6 %fusion.7 = f32[1,16,18,2048]{3,1,2,0:T(8,128)S(1)} fusion(f32[1,16,20,2048]{3,1,2,0:T(8,128)S(1)} %convolution_bitcast_fusion, f32[18,2048]{1,0:T(8,128)S(1)} %slice_add_fusion.6, f32[18,2048]{1,0:T(8,128)S(1)} %bitcast.74), kind=kLoop, calls=%fused_computation.17 | loop fusion | flops 7667712 | bytes 12451840 | tf_op jit(solution)/shard_map/mul | solution.py:78
  31.4 3.9 %fusion.18 = f32[1,16,16,2048]{3,1,2,0:T(8,128)S(1)} fusion(f32[1,16,18,2048]{3,1,2,0:T(8,128)S(1)} %fusion.7, f32[16,2048]{1,0:T(8,128)S(1)} %slice_add_fusion.10, f32[16,2048]{1,0:T(8,128)S(1)} %bitcast.72), kind=kLoop, calls=%fused_computation.36 | loop fusion | flops 6815744 | bytes 11010048 | tf_op jit(solution)/shard_map/mul | solution.py:79
  35.3 2.0 %convolution_bitcast_fusion.1 = f32[1,16,16,2048]{3,1,2,0:T(8,128)S(1)} fusion(f32[1,16,16,2048]{3,1,2,0:T(8,128)S(1)} %fusion.18, f32[16,16]{1,0:T(8,128)S(1)} %copy-done), kind=kOutput, calls=%fused_computation.2 | convolution fusion | flops 100663296 | bytes 4195328 | tf_op jit(solution)/shard_map/ts,psrc->ptrc/dot_general | solution.py:77
  40.0 5.8 %collective-permute-start.4 = (f32[1,2]{1,0:T(1,128)S(1)}, f32[1,2]{1,0:T(1,128)S(1)}, u32[]{:S(2)}, u32[]{:S(2)}) collective-permute-start(f32[1,2]{1,0:T(1,128)S(1)} %pad_maximum_fusion.2), channel_id=1, source_target_pairs={{0,1},{1,0},{2,3},{3,2},{4,5},{5,4},{6,7},{7,6},{8,9},{9,8},{10,11... | collective-permute-start | bytes 32 | tf_op jit(solution)/shard_map/ppermute | solution.py:47
  46.0 3.4 %fusion.30 = f32[1,16,14,2048]{3,1,2,0:T(8,128)S(1)} fusion(f32[1,16,16,2048]{3,1,2,0:T(8,128)S(1)} %convolution_bitcast_fusion.1, f32[14,2048]{1,0:T(8,128)S(1)} %slice_add_fusion.8, f32[14,2048]{1,0:T(8,128)S(1)} %bitcast.77), kind=kLoop, calls=%fused_computation.58 | loop fusion | flops 5963776 | bytes 9699328 | tf_op jit(solution)/shard_map/mul | solution.py:78
  51.1 2.0 %collective-permute-done.5 = f32[1,2]{1,0:T(1,128)S(1)} collective-permute-done((f32[1,2]{1,0:T(1,128)S(1)}, f32[1,2]{1,0:T(1,128)S(1)}, u32[]{:S(2)}, u32[]{:S(2)}) %collective-permute-start.5) | collective-permute-done | bytes 40 | tf_op jit(solution)/shard_map/ppermute | solution.py:47
  53.1 2.6 %collective-permute-start.6 = (f32[1,2]{1,0:T(1,128)S(1)}, f32[1,2]{1,0:T(1,128)S(1)}, u32[]{:S(2)}, u32[]{:S(2)}) collective-permute-start(f32[1,2]{1,0:T(1,128)S(1)} %add.229), channel_id=1, source_target_pairs={{0,4},{1,5},{2,6},{3,7},{4,0},{5,1},{6,2},{7,3},{8,12},{9,13},{10,... | collective-permute-start | bytes 32 | tf_op jit(solution)/shard_map/ppermute | solution.py:47
  55.7 1.9 %collective-permute-done.6 = f32[1,2]{1,0:T(1,128)S(1)} collective-permute-done((f32[1,2]{1,0:T(1,128)S(1)}, f32[1,2]{1,0:T(1,128)S(1)}, u32[]{:S(2)}, u32[]{:S(2)}) %collective-permute-start.6) | collective-permute-done | bytes 40 | tf_op jit(solution)/shard_map/ppermute | solution.py:47
  59.5 3.9 %multiply_subtract_fusion = (f32[1,16,16,2048]{3,1,2,0:T(8,128)S(1)}, f32[1,16,16,2048]{3,1,2,0:T(8,128)S(1)}, f32[1,16,16,2048]{3,1,2,0:T(8,128)S(1)}) fusion(f32[]{:T(128)} %bitcast.12, f32[]{:T(128)} %bitcast.11, f32[1,16,20,2048]{3,1,2,0:T(8,128)S(1)} %broadcast_multiply_fusion, f32[1,16,18,2048]{3,1,2,0:T(8,128)S(1)} %fusion.7, ...), kind=kLoop, calls=%fused_computation.46 | loop fusion | flops 8912896 | bytes 17301512 | tf_op jit(solution)/shard_map/sub | solution.py:101
  63.4 3.2 %fusion.43 = f32[1,16,12,2048]{3,1,2,0:T(8,128)S(1)} fusion(f32[1,16,14,2048]{3,1,2,0:T(8,128)S(1)} %fusion.30, f32[1,16,16,2048]{3,1,2,0:T(8,128)S(1)} %get-tuple-element.18, f32[]{:T(128)} %bitcast.12, f32[]{:T(128)} %bitcast.11, f32[12,2048]{1,0:T(8,128)S(1)} %slice_add_fusion.9, f32[12,2048]{1,0:T(8,128)S(1)} %bitcast.75), kind=kLoop, calls=%fused_computation.79 | loop fusion | flops 6291456 | bytes 9961480 | tf_op jit(solution)/shard_map/sub | solution.py:102
  69.3 1.9 %pad_maximum_fusion.3 = f32[1,3]{1,0:T(1,128)S(1)} fusion(f32[1,1]{1,0:T(1,128)} %bitcast.19, f32[1,1]{1,0:T(1,128)} %bitcast.18, f32[1,1]{1,0:T(1,128)} %bitcast.13), kind=kLoop, calls=%fused_computation.179 | loop fusion | flops 6 | bytes 24 | tf_op jit(solution)/shard_map/stack | solution.py:91
  71.2 2.1 %fusion.55 = f32[1,16,10,2048]{3,1,2,0:T(8,128)S(1)} fusion(f32[1,16,12,2048]{3,1,2,0:T(8,128)S(1)} %convolution_bitcast_fusion.2, f32[10,2048]{1,0:T(8,128)S(1)} %slice_add_fusion.7, f32[10,2048]{1,0:T(8,128)S(1)} %bitcast.76), kind=kLoop, calls=%fused_computation.101 | loop fusion | flops 4259840 | bytes 7077888 | tf_op jit(solution)/shard_map/mul | solution.py:78
  75.0 2.0 %collective-permute-done.8 = f32[1,3]{1,0:T(1,128)S(1)} collective-permute-done((f32[1,3]{1,0:T(1,128)S(1)}, f32[1,3]{1,0:T(1,128)S(1)}, u32[]{:S(2)}, u32[]{:S(2)}) %collective-permute-start.8) | collective-permute-done | bytes 44 | tf_op jit(solution)/shard_map/ppermute | solution.py:47
  77.0 2.6 %collective-permute-start.9 = (f32[1,3]{1,0:T(1,128)S(1)}, f32[1,3]{1,0:T(1,128)S(1)}, u32[]{:S(2)}, u32[]{:S(2)}) collective-permute-start(f32[1,3]{1,0:T(1,128)S(1)} %add.245), channel_id=1, source_target_pairs={{0,4},{1,5},{2,6},{3,7},{4,0},{5,1},{6,2},{7,3},{8,12},{9,13},{10,... | collective-permute-start | bytes 44 | tf_op jit(solution)/shard_map/ppermute | solution.py:47
  79.6 1.9 %collective-permute-done.9 = f32[1,3]{1,0:T(1,128)S(1)} collective-permute-done((f32[1,3]{1,0:T(1,128)S(1)}, f32[1,3]{1,0:T(1,128)S(1)}, u32[]{:S(2)}, u32[]{:S(2)}) %collective-permute-start.9) | collective-permute-done | bytes 44 | tf_op jit(solution)/shard_map/ppermute | solution.py:47
  84.2 2.7 %multiply_reduce_fusion.3 = (f32[]{:T(128)}, f32[]{:T(128)}, f32[]{:T(128)}, f32[1,16,8,2048]{3,1,2,0:T(8,128)S(1)}, f32[1,16,8,2048]{3,1,2,0:T(8,128)S(1)}) fusion(f32[1,16,12,2048]{3,1,2,0:T(8,128)S(1)} %slice_divide_fusion.1, f32[1,16,12,2048]{3,1,2,0:T(8,128)S(1)} %fusion.43, f32[]{:T(128)} %bitcast.21, f32[1,16,16,2048]{3,1,2,0:T(8,128)S(1)} %get-tuple-element.18, ...), kind=kLoop, calls=%fused_computation.152 | loop fusion | flops 7864317 | bytes 10878996 | tf_op jit(solution)/shard_map/reduce_sum | solution.py:85
  87.0 2.0 %pad_maximum_fusion.4 = f32[1,3]{1,0:T(1,128)S(1)} fusion(f32[1,1]{1,0:T(1,128)} %bitcast.28, f32[1,1]{1,0:T(1,128)} %bitcast.27, f32[1,1]{1,0:T(1,128)} %bitcast.22), kind=kLoop, calls=%fused_computation.180 | loop fusion | flops 6 | bytes 24 | tf_op jit(solution)/shard_map/stack | solution.py:91
  91.7 2.0 %collective-permute-done.11 = f32[1,3]{1,0:T(1,128)S(1)} collective-permute-done((f32[1,3]{1,0:T(1,128)S(1)}, f32[1,3]{1,0:T(1,128)S(1)}, u32[]{:S(2)}, u32[]{:S(2)}) %collective-permute-start.11) | collective-permute-done | bytes 44 | tf_op jit(solution)/shard_map/ppermute | solution.py:47
  93.7 2.6 %collective-permute-start.12 = (f32[1,3]{1,0:T(1,128)S(1)}, f32[1,3]{1,0:T(1,128)S(1)}, u32[]{:S(2)}, u32[]{:S(2)}) collective-permute-start(f32[1,3]{1,0:T(1,128)S(1)} %add.261), channel_id=1, source_target_pairs={{0,4},{1,5},{2,6},{3,7},{4,0},{5,1},{6,2},{7,3},{8,12},{9,13},{10,... | collective-permute-start | bytes 44 | tf_op jit(solution)/shard_map/ppermute | solution.py:47
  96.3 1.9 %collective-permute-done.12 = f32[1,3]{1,0:T(1,128)S(1)} collective-permute-done((f32[1,3]{1,0:T(1,128)S(1)}, f32[1,3]{1,0:T(1,128)S(1)}, u32[]{:S(2)}, u32[]{:S(2)}) %collective-permute-start.12) | collective-permute-done | bytes 44 | tf_op jit(solution)/shard_map/ppermute | solution.py:47
  103.3 3.9 %all-to-all-start.1 = ((f32[1,16,8,2048]{3,2,0,1:T(8,128)}), f32[1,16,8,2048]{3,2,0,1:T(8,128)S(1)}, u32[]{:S(2)}, u32[]{:S(2)}) async-start(f32[1,16,8,2048]{3,2,0,1:T(8,128)} %copy.15), calls=%async_computation.1 | async-start | bytes 2097152 | tf_op jit(solution)/shard_map/all_to_all | solution.py:136
  111.4 2.0 %collective-permute-done.14 = f32[4,7]{1,0:T(4,128)S(1)} collective-permute-done((f32[4,7]{1,0:T(4,128)S(1)}, f32[4,7]{1,0:T(4,128)S(1)}, u32[]{:S(2)}, u32[]{:S(2)}) %collective-permute-start.14) | collective-permute-done | bytes 144 | tf_op jit(solution)/shard_map/ppermute | solution.py:47
  113.4 2.6 %collective-permute-start.15 = (f32[4,7]{1,0:T(4,128)S(1)}, f32[4,7]{1,0:T(4,128)S(1)}, u32[]{:S(2)}, u32[]{:S(2)}) collective-permute-start(f32[4,7]{1,0:T(4,128)S(1)} %add.266), channel_id=1, source_target_pairs={{0,4},{1,5},{2,6},{3,7},{4,0},{5,1},{6,2},{7,3},{8,12},{9,13},{10,... | collective-permute-start | bytes 344 | tf_op jit(solution)/shard_map/ppermute | solution.py:47
  116.0 1.9 %collective-permute-done.15 = f32[4,7]{1,0:T(4,128)S(1)} collective-permute-done((f32[4,7]{1,0:T(4,128)S(1)}, f32[4,7]{1,0:T(4,128)S(1)}, u32[]{:S(2)}, u32[]{:S(2)}) %collective-permute-start.15) | collective-permute-done | bytes 144 | tf_op jit(solution)/shard_map/ppermute | solution.py:47
  117.9 2.0 %collective-permute-start.16 = (f32[4,7]{1,0:T(4,128)S(1)}, f32[4,7]{1,0:T(4,128)S(1)}, u32[]{:S(2)}, u32[]{:S(2)}) collective-permute-start(f32[4,7]{1,0:T(4,128)S(1)} %add.267), channel_id=1, source_target_pairs={{0,8},{8,0},{16,24},{24,16},{1,9},{9,1},{17,25},{25,17},{2,10},{10... | collective-permute-start | bytes 344 | tf_op jit(solution)/shard_map/ppermute | solution.py:47
  121.5 2.0 %collective-permute-start.17 = (f32[4,7]{1,0:T(4,128)S(1)}, f32[4,7]{1,0:T(4,128)S(1)}, u32[]{:S(2)}, u32[]{:S(2)}) collective-permute-start(f32[4,7]{1,0:T(4,128)S(1)} %add.268), channel_id=1, source_target_pairs={{0,16},{8,24},{16,0},{24,8},{1,17},{9,25},{17,1},{25,9},{2,18},{10... | collective-permute-start | bytes 344 | tf_op jit(solution)/shard_map/ppermute | solution.py:47
  (95 shorter events, 33.1 us)
Async XLA Ops:
  0.6 10.3 %copy-start = (f32[16,16]{1,0:T(8,128)S(1)}, f32[16,16]{1,0:T(8,128)}, u32[]{:S(2)}) copy-start(f32[16,16]{1,0:T(8,128)} %param.7) | copy-start | bytes 3076
  0.6 7.4 %copy-start.2 = (f32[8,2048]{1,0:T(8,128)S(1)}, f32[8,2048]{1,0:T(8,128)}, u32[]{:S(2)}) copy-start(f32[8,2048]{1,0:T(8,128)} %param.6) | copy-start | bytes 196612
  2.9 13.2 %all-to-all-start = ((bf16[4,4,8,2048]{3,2,1,0:T(8,128)(2,1)}), bf16[4,4,8,2048]{3,2,1,0:T(8,128)(2,1)S(1)}, u32[]{:S(2)}, u32[]{:S(2)}) async-start(bf16[4,4,8,2048]{3,2,1,0:T(8,128)(2,1)} %multiply_convert_fusion), calls=%async_computation | async-start | bytes 1048576 | tf_op jit(solution)/shard_map/all_to_all | solution.py:68
  8.1 3.5 %collective-permute-start.2 = (f32[6,2048]{1,0:T(8,128)S(1)}, f32[6,2048]{1,0:T(8,128)S(1)}, u32[]{:S(2)}, u32[]{:S(2)}) collective-permute-start(f32[6,2048]{1,0:T(8,128)S(1)} %get-tuple-element.22), channel_id=1, source_target_pairs={{0,1},{1,2},{2,3},{3,4},{4,5},{5,6},{6,7},{8,9},{9,10},{10,11},{11... | collective-permute-start | bytes 147464 | tf_op jit(solution)/shard_map/ppermute | solution.py:59
  9.6 4.8 %collective-permute-start.3 = (f32[6,2048]{1,0:T(8,128)S(1)}, f32[6,2048]{1,0:T(8,128)S(1)}, u32[]{:S(2)}, u32[]{:S(2)}) collective-permute-start(f32[6,2048]{1,0:T(8,128)S(1)} %get-tuple-element.23), channel_id=1, source_target_pairs={{1,0},{2,1},{3,2},{4,3},{5,4},{6,5},{7,6},{9,8},{10,9},{11,10},{12... | collective-permute-start | bytes 147464 | tf_op jit(solution)/shard_map/ppermute | solution.py:60
  16.5 4.9 %collective-permute-start = (bf16[1,16,6,2048]{3,1,2,0:T(8,128)(2,1)S(1)}, bf16[1,16,6,2048]{3,1,2,0:T(8,128)(2,1)S(1)}, u32[]{:S(2)}, u32[]{:S(2)}) collective-permute-start(bf16[1,16,6,2048]{3,1,2,0:T(8,128)(2,1)S(1)} %get-tuple-element.20), channel_id=1, source_target_pairs={{0,1},{1,2},{2,3},{3,4},{4,5},{5,6},{6,7},{8,9},{9,10},{10,11},{11... | collective-permute-start | bytes 1179656 | tf_op jit(solution)/shard_map/ppermute | solution.py:59
  19.8 3.6 %collective-permute-start.1 = (bf16[1,16,6,2048]{3,1,2,0:T(8,128)(2,1)S(1)}, bf16[1,16,6,2048]{3,1,2,0:T(8,128)(2,1)S(1)}, u32[]{:S(2)}, u32[]{:S(2)}) collective-permute-start(bf16[1,16,6,2048]{3,1,2,0:T(8,128)(2,1)S(1)} %get-tuple-element.21), channel_id=1, source_target_pairs={{1,0},{2,1},{3,2},{4,3},{5,4},{6,5},{7,6},{9,8},{10,9},{11,10},{12... | collective-permute-start | bytes 1179656 | tf_op jit(solution)/shard_map/ppermute | solution.py:60
  23.7 3.2 %copy-start.1 = (f32[1,1,20,2048]{3,1,2,0:T(1,128)}, f32[1,1,20,2048]{3,1,2,0:T(1,128)S(1)}, u32[]{:S(2)}) copy-start(f32[1,1,20,2048]{3,1,2,0:T(1,128)S(1)} %slice_multiply_fusion.11) | copy-start | bytes 491524
  37.3 8.5 %slice-start = ((f32[1,1,20,2048]{3,1,2,0:T(1,128)}), f32[1,1,14,2048]{3,1,2,0:T(1,128)S(1)}, s32[]{:S(2)}) async-start(f32[1,1,20,2048]{3,1,2,0:T(1,128)} %copy-done.1), calls=%async_computation.2 | async-start | bytes 229376 | tf_op jit(solution)/shard_map/slice | solution.py:78
  37.6 8.2 %slice-start.1 = ((f32[1,1,20,2048]{3,1,2,0:T(1,128)}), f32[1,1,12,2048]{3,1,2,0:T(1,128)S(1)}, s32[]{:S(2)}) async-start(f32[1,1,20,2048]{3,1,2,0:T(1,128)} %copy-done.1), calls=%async_computation.3 | async-start | bytes 196608 | tf_op jit(solution)/shard_map/slice | solution.py:79
  37.6 8.2 %slice-start.2 = ((f32[1,1,20,2048]{3,1,2,0:T(1,128)}), f32[1,1,10,2048]{3,1,2,0:T(1,128)S(1)}, s32[]{:S(2)}) async-start(f32[1,1,20,2048]{3,1,2,0:T(1,128)} %copy-done.1), calls=%async_computation.4 | async-start | bytes 163840 | tf_op jit(solution)/shard_map/slice | solution.py:78
  37.7 8.3 %slice-start.3 = ((f32[1,1,20,2048]{3,1,2,0:T(1,128)}), f32[1,1,8,2048]{3,1,2,0:T(1,128)S(1)}, s32[]{:S(2)}) async-start(f32[1,1,20,2048]{3,1,2,0:T(1,128)} %copy-done.1), calls=%async_computation.5 | async-start | bytes 131072 | tf_op jit(solution)/shard_map/slice | solution.py:79
  40.0 9.4 %collective-permute-start.4 = (f32[1,2]{1,0:T(1,128)S(1)}, f32[1,2]{1,0:T(1,128)S(1)}, u32[]{:S(2)}, u32[]{:S(2)}) collective-permute-start(f32[1,2]{1,0:T(1,128)S(1)} %pad_maximum_fusion.2), channel_id=1, source_target_pairs={{0,1},{1,0},{2,3},{3,2},{4,5},{5,4},{6,7},{7,6},{8,9},{9,8},{10,11... | collective-permute-start | bytes 32 | tf_op jit(solution)/shard_map/ppermute | solution.py:47
  49.4 3.6 %collective-permute-start.5 = (f32[1,2]{1,0:T(1,128)S(1)}, f32[1,2]{1,0:T(1,128)S(1)}, u32[]{:S(2)}, u32[]{:S(2)}) collective-permute-start(f32[1,2]{1,0:T(1,128)S(1)} %add.228), channel_id=1, source_target_pairs={{0,2},{1,3},{2,0},{3,1},{4,6},{5,7},{6,4},{7,5},{8,10},{9,11},{10,... | collective-permute-start | bytes 32 | tf_op jit(solution)/shard_map/ppermute | solution.py:47
  53.1 4.5 %collective-permute-start.6 = (f32[1,2]{1,0:T(1,128)S(1)}, f32[1,2]{1,0:T(1,128)S(1)}, u32[]{:S(2)}, u32[]{:S(2)}) collective-permute-start(f32[1,2]{1,0:T(1,128)S(1)} %add.229), channel_id=1, source_target_pairs={{0,4},{1,5},{2,6},{3,7},{4,0},{5,1},{6,2},{7,3},{8,12},{9,13},{10,... | collective-permute-start | bytes 32 | tf_op jit(solution)/shard_map/ppermute | solution.py:47
  71.2 2.1 %collective-permute-start.7 = (f32[1,3]{1,0:T(1,128)S(1)}, f32[1,3]{1,0:T(1,128)S(1)}, u32[]{:S(2)}, u32[]{:S(2)}) collective-permute-start(f32[1,3]{1,0:T(1,128)S(1)} %pad_maximum_fusion.3), channel_id=1, source_target_pairs={{0,1},{1,0},{2,3},{3,2},{4,5},{5,4},{6,7},{7,6},{8,9},{9,8},{10,11... | collective-permute-start | bytes 44 | tf_op jit(solution)/shard_map/ppermute | solution.py:47
  73.3 3.6 %collective-permute-start.8 = (f32[1,3]{1,0:T(1,128)S(1)}, f32[1,3]{1,0:T(1,128)S(1)}, u32[]{:S(2)}, u32[]{:S(2)}) collective-permute-start(f32[1,3]{1,0:T(1,128)S(1)} %add.244), channel_id=1, source_target_pairs={{0,2},{1,3},{2,0},{3,1},{4,6},{5,7},{6,4},{7,5},{8,10},{9,11},{10,... | collective-permute-start | bytes 44 | tf_op jit(solution)/shard_map/ppermute | solution.py:47
  77.0 4.5 %collective-permute-start.9 = (f32[1,3]{1,0:T(1,128)S(1)}, f32[1,3]{1,0:T(1,128)S(1)}, u32[]{:S(2)}, u32[]{:S(2)}) collective-permute-start(f32[1,3]{1,0:T(1,128)S(1)} %add.245), channel_id=1, source_target_pairs={{0,4},{1,5},{2,6},{3,7},{4,0},{5,1},{6,2},{7,3},{8,12},{9,13},{10,... | collective-permute-start | bytes 44 | tf_op jit(solution)/shard_map/ppermute | solution.py:47
  89.0 1.2 collective-permute-start.10
  90.1 3.6 %collective-permute-start.11 = (f32[1,3]{1,0:T(1,128)S(1)}, f32[1,3]{1,0:T(1,128)S(1)}, u32[]{:S(2)}, u32[]{:S(2)}) collective-permute-start(f32[1,3]{1,0:T(1,128)S(1)} %add.260), channel_id=1, source_target_pairs={{0,2},{1,3},{2,0},{3,1},{4,6},{5,7},{6,4},{7,5},{8,10},{9,11},{10,... | collective-permute-start | bytes 44 | tf_op jit(solution)/shard_map/ppermute | solution.py:47
  93.7 4.5 %collective-permute-start.12 = (f32[1,3]{1,0:T(1,128)S(1)}, f32[1,3]{1,0:T(1,128)S(1)}, u32[]{:S(2)}, u32[]{:S(2)}) collective-permute-start(f32[1,3]{1,0:T(1,128)S(1)} %add.261), channel_id=1, source_target_pairs={{0,4},{1,5},{2,6},{3,7},{4,0},{5,1},{6,2},{7,3},{8,12},{9,13},{10,... | collective-permute-start | bytes 44 | tf_op jit(solution)/shard_map/ppermute | solution.py:47
  103.3 22.8 %all-to-all-start.1 = ((f32[1,16,8,2048]{3,2,0,1:T(8,128)}), f32[1,16,8,2048]{3,2,0,1:T(8,128)S(1)}, u32[]{:S(2)}, u32[]{:S(2)}) async-start(f32[1,16,8,2048]{3,2,0,1:T(8,128)} %copy.15), calls=%async_computation.1 | async-start | bytes 2097152 | tf_op jit(solution)/shard_map/all_to_all | solution.py:136
  107.9 1.2 collective-permute-start.13
  109.7 3.6 %collective-permute-start.14 = (f32[4,7]{1,0:T(4,128)S(1)}, f32[4,7]{1,0:T(4,128)S(1)}, u32[]{:S(2)}, u32[]{:S(2)}) collective-permute-start(f32[4,7]{1,0:T(4,128)S(1)} %add.265), channel_id=1, source_target_pairs={{0,2},{1,3},{2,0},{3,1},{4,6},{5,7},{6,4},{7,5},{8,10},{9,11},{10,... | collective-permute-start | bytes 344 | tf_op jit(solution)/shard_map/ppermute | solution.py:47
  113.4 4.5 %collective-permute-start.15 = (f32[4,7]{1,0:T(4,128)S(1)}, f32[4,7]{1,0:T(4,128)S(1)}, u32[]{:S(2)}, u32[]{:S(2)}) collective-permute-start(f32[4,7]{1,0:T(4,128)S(1)} %add.266), channel_id=1, source_target_pairs={{0,4},{1,5},{2,6},{3,7},{4,0},{5,1},{6,2},{7,3},{8,12},{9,13},{10,... | collective-permute-start | bytes 344 | tf_op jit(solution)/shard_map/ppermute | solution.py:47
  117.9 3.6 %collective-permute-start.16 = (f32[4,7]{1,0:T(4,128)S(1)}, f32[4,7]{1,0:T(4,128)S(1)}, u32[]{:S(2)}, u32[]{:S(2)}) collective-permute-start(f32[4,7]{1,0:T(4,128)S(1)} %add.267), channel_id=1, source_target_pairs={{0,8},{8,0},{16,24},{24,16},{1,9},{9,1},{17,25},{25,17},{2,10},{10... | collective-permute-start | bytes 344 | tf_op jit(solution)/shard_map/ppermute | solution.py:47
  121.5 3.6 %collective-permute-start.17 = (f32[4,7]{1,0:T(4,128)S(1)}, f32[4,7]{1,0:T(4,128)S(1)}, u32[]{:S(2)}, u32[]{:S(2)}) collective-permute-start(f32[4,7]{1,0:T(4,128)S(1)} %add.268), channel_id=1, source_target_pairs={{0,16},{8,24},{16,0},{24,8},{1,17},{9,25},{17,1},{25,9},{2,18},{10... | collective-permute-start | bytes 344 | tf_op jit(solution)/shard_map/ppermute | solution.py:47
  125.1 2.2 %copy-start.3 = (f32[4,7]{1,0:T(4,128)}, f32[4,7]{1,0:T(4,128)S(1)}, u32[]{:S(2)}) copy-start(f32[4,7]{1,0:T(4,128)S(1)} %add.269) | copy-start | bytes 340

commit v5 on v4

--- a/solution.py
+++ b/solution.py
@@ -87,12 +87,13 @@
     def crop(x, k):
         return x[:, :, k : x.shape[2] - k]
 
-    def reduce_tile(parts):
-        return butterfly_sum(lax.optimization_barrier(jnp.stack(parts, axis=-1)), "tile")
+    def reduce_tile(pairs, off):
+        prods = jnp.stack([own(a, off) * own(b, off) for a, b in pairs], axis=-1)
+        return butterfly_sum(jnp.sum(prods, axis=(1, 2, 3)), "tile")
 
     az = apply_a(z, 0)
     z2 = crop(z, 2)
-    sums = reduce_tile([dot(z2, z2, 2), dot(az, z2, 2)])
+    sums = reduce_tile([(z2, z2), (az, z2)], 2)
     aaz = apply_a(az, 2)
     norm = jnp.sqrt(sums[:, 0] + epsilon)
     alpha = sums[:, 1] / (norm * norm)
@@ -108,7 +109,7 @@
     betas = []
     iters = 3
     for step in range(1, iters):
-        sums = reduce_tile([dot(w, w, off), dot(aw, w, off), dot(q, w, off)])
+        sums = reduce_tile([(w, w), (aw, w), (q, w)], off)
         last_step = step == iters - 1
         if not last_step:
             aaw = apply_a(aw, off)

time: 128 us -> 122 us (0.953)
  other arithmetic: 38.5 us -> 32.8 us
    reduce_sum x3, other arithmetic: 4.69 us -> 1.14 us  [reduce_tile(): return butterfly_sum(jnp.sum(prods, axis=(1, 2, 3)), 'tile')]
    another operation x3 -> x4, other arithmetic: 5.28 us -> 2.84 us  [reduce_tile(): prods = jnp.stack([own(a, off) * own(b, off) for a, b in pairs], axis=-1)]
  transfers between devices with their start and end apart: 20 -> 20, of which waited for: 15 -> 15; matrix products, arithmetic and copies ran while one was open for 7% -> 8% of each run, Pallas kernels for 0% -> 0%
where the time goes in v5:
time: 122 us; the launch traced here: 121 us
  starting transfers between devices  43.2 us (35%)
  other arithmetic  32.8 us (27%)
  waiting for transfers between devices  27.3 us (22%)
  matrix products  6.47 us (5%)
  between operations  6.36 us (5%)
  local copies, waits for them, and re-layouts  5.39 us (4%)
    ppermute x14, starting transfers between devices, butterfly_sum(): v = v + lax.ppermute(v, axis, [(i, i ^ s) for i in range(n)])  26.8 us
    ppermute x14, waiting for transfers between devices, butterfly_sum(): v = v + lax.ppermute(v, axis, [(i, i ^ s) for i in range(n)])  20.9 us
    mul x3, other arithmetic, apply_a(): land_ext[off + 1:off + r - 1]  10.1 us
    dot_general x3, matrix products, apply_a(): jnp.einsum('ts,psrc->ptrc', trait_covariance, x, precision=lax.Precision....  6.47 us
    all_to_all x1, starting transfers between devices, shards(): lax.all_to_all(signed, 'trait', split_axis=0, concat_axis=1, tiled=True)  5.19 us
    ppermute x2, waiting for transfers between devices, halo_rows(): lax.ppermute(lax.slice_in_dim(block, 0, width, axis=dim), 'tile', backward)  4.76 us
    ppermute x2, starting transfers between devices, halo_rows(): lax.ppermute(lax.slice_in_dim(block, rows - width, rows, axis=dim), 'tile...  4.75 us
    sub x1, other arithmetic, shards(): w = aq - alpha[:, None, None, None] * q  3.93 us
  transfers between devices with their start and end apart: 20, of which 15 were waited for; matrix products, arithmetic and copies ran while one was open for 8% of the time, Pallas kernels for 0%

profile of v5, /device:TPU:0, one launch (start us, length us, event | category | flops | bytes accessed | tf_op | source)
XLA Modules:
  0.0 121.5 jit_solution(7811998562088500223)
XLA Ops:
  0.7 2.2 %multiply_convert_fusion = bf16[4,4,8,2048]{3,2,1,0:T(8,128)(2,1)} fusion(s32[4,4,8,2048]{3,2,1,0:T(8,128)} %param.4, s32[8,2048]{1,0:T(8,128)} %param.5), kind=kLoop, calls=%fused_computation.160 | loop fusion | flops 1048576 | bytes 1638400 | tf_op jit(solution)/shard_map/convert_element_type | solution.py:67
  2.9 5.2 %all-to-all-start = ((bf16[4,4,8,2048]{3,2,1,0:T(8,128)(2,1)}), bf16[4,4,8,2048]{3,2,1,0:T(8,128)(2,1)S(1)}, u32[]{:S(2)}, u32[]{:S(2)}) async-start(bf16[4,4,8,2048]{3,2,1,0:T(8,128)(2,1)} %multiply_convert_fusion), calls=%async_computation | async-start | bytes 1048576 | tf_op jit(solution)/shard_map/all_to_all | solution.py:68
  11.6 2.8 %collective-permute-done.3 = f32[6,2048]{1,0:T(8,128)S(1)} collective-permute-done((f32[6,2048]{1,0:T(8,128)S(1)}, f32[6,2048]{1,0:T(8,128)S(1)}, u32[]{:S(2)}, u32[]{:S(2)}) %collective-permute-start.3) | collective-permute-done | bytes 49184 | tf_op jit(solution)/shard_map/ppermute | solution.py:60
  16.5 3.3 %collective-permute-start = (bf16[1,16,6,2048]{3,1,2,0:T(8,128)(2,1)S(1)}, bf16[1,16,6,2048]{3,1,2,0:T(8,128)(2,1)S(1)}, u32[]{:S(2)}, u32[]{:S(2)}) collective-permute-start(bf16[1,16,6,2048]{3,1,2,0:T(8,128)(2,1)S(1)} %get-tuple-element.20), channel_id=1, source_target_pairs={{0,1},{1,2},{2,3},{3,4},{4,5},{5,6},{6,7},{8,9},{9,10},{10,11},{11... | collective-permute-start | bytes 1179656 | tf_op jit(solution)/shard_map/ppermute | solution.py:59
  21.4 2.0 %collective-permute-done.1 = bf16[1,16,6,2048]{3,1,2,0:T(8,128)(2,1)S(1)} collective-permute-done((bf16[1,16,6,2048]{3,1,2,0:T(8,128)(2,1)S(1)}, bf16[1,16,6,2048]{3,1,2,0:T(8,128)(2,1)S(1)}, u32[]{:S(2)}, u32[]{:S(2)}) %collective-permute-start.1) | collective-permute-done | bytes 393248 | tf_op jit(solution)/shard_map/ppermute | solution.py:60
  23.8 3.0 %convolution_bitcast_fusion = f32[1,16,20,2048]{3,1,2,0:T(8,128)S(1)} fusion(bf16[16,6,2048]{2,0,1:T(8,128)(2,1)S(1)} %bitcast.85, bf16[16,8,2048]{2,0,1:T(8,128)(2,1)S(1)} %copy.14, bf16[16,6,2048]{2,0,1:T(8,128)(2,1)S(1)} %bitcast.84, f32[16]{0:T(128)S(1)} %gather_fusion, f32[16,16]{1,0:T(8,128)S(1)} %copy-done), kind=kOutput, calls=%fused_computation.3 | convolution fusion | flops 128450560 | bytes 3933248 | tf_op jit(solution)/shard_map/ts,psrc->ptrc/dot_general | solution.py:77
  26.8 4.6 %fusion.7 = f32[1,16,18,2048]{3,1,2,0:T(8,128)S(1)} fusion(f32[1,16,20,2048]{3,1,2,0:T(8,128)S(1)} %convolution_bitcast_fusion, f32[18,2048]{1,0:T(8,128)S(1)} %slice_add_fusion.6, f32[18,2048]{1,0:T(8,128)S(1)} %bitcast.88), kind=kLoop, calls=%fused_computation.19 | loop fusion | flops 7667712 | bytes 12451840 | tf_op jit(solution)/shard_map/mul | solution.py:78
  31.4 3.9 %fusion.18 = f32[1,16,16,2048]{3,1,2,0:T(8,128)S(1)} fusion(f32[1,16,18,2048]{3,1,2,0:T(8,128)S(1)} %fusion.7, f32[16,2048]{1,0:T(8,128)S(1)} %slice_add_fusion.10, f32[16,2048]{1,0:T(8,128)S(1)} %bitcast.86), kind=kLoop, calls=%fused_computation.38 | loop fusion | flops 6815744 | bytes 11010048 | tf_op jit(solution)/shard_map/mul | solution.py:79
  35.3 2.0 %convolution_bitcast_fusion.1 = f32[1,16,16,2048]{3,1,2,0:T(8,128)S(1)} fusion(f32[1,16,16,2048]{3,1,2,0:T(8,128)S(1)} %fusion.18, f32[16,16]{1,0:T(8,128)S(1)} %copy-done), kind=kOutput, calls=%fused_computation.4 | convolution fusion | flops 100663296 | bytes 4195328 | tf_op jit(solution)/shard_map/ts,psrc->ptrc/dot_general | solution.py:77
  38.2 5.8 %collective-permute-start.4 = (f32[1,2]{1,0:T(1,128)S(1)}, f32[1,2]{1,0:T(1,128)S(1)}, u32[]{:S(2)}, u32[]{:S(2)}) collective-permute-start(f32[1,2]{1,0:T(1,128)S(1)} %bitcast.94), channel_id=1, source_target_pairs={{0,1},{1,0},{2,3},{3,2},{4,5},{5,4},{6,7},{7,6},{8,9},{9,8},{10,11... | collective-permute-start | bytes 32 | tf_op jit(solution)/shard_map/ppermute | solution.py:47
  44.2 3.4 %fusion.30 = f32[1,16,14,2048]{3,1,2,0:T(8,128)S(1)} fusion(f32[1,16,16,2048]{3,1,2,0:T(8,128)S(1)} %convolution_bitcast_fusion.1, f32[14,2048]{1,0:T(8,128)S(1)} %slice_add_fusion.8, f32[14,2048]{1,0:T(8,128)S(1)} %bitcast.91), kind=kLoop, calls=%fused_computation.61 | loop fusion | flops 5963776 | bytes 9699328 | tf_op jit(solution)/shard_map/mul | solution.py:78
  47.6 1.6 %collective-permute-start.5 = (f32[1,2]{1,0:T(1,128)S(1)}, f32[1,2]{1,0:T(1,128)S(1)}, u32[]{:S(2)}, u32[]{:S(2)}) collective-permute-start(f32[1,2]{1,0:T(1,128)S(1)} %bitcast_add_fusion.2), channel_id=1, source_target_pairs={{0,2},{1,3},{2,0},{3,1},{4,6},{5,7},{6,4},{7,5},{8,10},{9,11},{10,... | collective-permute-start | bytes 32 | tf_op jit(solution)/shard_map/ppermute | solution.py:47
  49.3 2.0 %collective-permute-done.5 = f32[1,2]{1,0:T(1,128)S(1)} collective-permute-done((f32[1,2]{1,0:T(1,128)S(1)}, f32[1,2]{1,0:T(1,128)S(1)}, u32[]{:S(2)}, u32[]{:S(2)}) %collective-permute-start.5) | collective-permute-done | bytes 40 | tf_op jit(solution)/shard_map/ppermute | solution.py:47
  51.3 2.6 %collective-permute-start.6 = (f32[1,2]{1,0:T(1,128)S(1)}, f32[1,2]{1,0:T(1,128)S(1)}, u32[]{:S(2)}, u32[]{:S(2)}) collective-permute-start(f32[1,2]{1,0:T(1,128)S(1)} %add.229), channel_id=1, source_target_pairs={{0,4},{1,5},{2,6},{3,7},{4,0},{5,1},{6,2},{7,3},{8,12},{9,13},{10,... | collective-permute-start | bytes 32 | tf_op jit(solution)/shard_map/ppermute | solution.py:47
  53.9 1.9 %collective-permute-done.6 = f32[1,2]{1,0:T(1,128)S(1)} collective-permute-done((f32[1,2]{1,0:T(1,128)S(1)}, f32[1,2]{1,0:T(1,128)S(1)}, u32[]{:S(2)}, u32[]{:S(2)}) %collective-permute-start.6) | collective-permute-done | bytes 40 | tf_op jit(solution)/shard_map/ppermute | solution.py:47
  57.7 3.9 %multiply_subtract_fusion = (f32[1,16,16,2048]{3,1,2,0:T(8,128)S(1)}, f32[1,16,16,2048]{3,1,2,0:T(8,128)S(1)}, f32[1,16,16,2048]{3,1,2,0:T(8,128)S(1)}) fusion(f32[]{:T(128)} %bitcast.13, f32[]{:T(128)} %bitcast.12, f32[1,16,20,2048]{3,1,2,0:T(8,128)S(1)} %broadcast_multiply_fusion, f32[1,16,18,2048]{3,1,2,0:T(8,128)S(1)} %fusion.7, ...), kind=kLoop, calls=%fused_computation.49 | loop fusion | flops 8912896 | bytes 17301512 | tf_op jit(solution)/shard_map/sub | solution.py:102
  61.6 3.2 %fusion.43 = f32[1,16,12,2048]{3,1,2,0:T(8,128)S(1)} fusion(f32[1,16,14,2048]{3,1,2,0:T(8,128)S(1)} %fusion.30, f32[1,16,16,2048]{3,1,2,0:T(8,128)S(1)} %get-tuple-element.12, f32[]{:T(128)} %bitcast.13, f32[]{:T(128)} %bitcast.12, f32[12,2048]{1,0:T(8,128)S(1)} %slice_add_fusion.9, f32[12,2048]{1,0:T(8,128)S(1)} %bitcast.89), kind=kLoop, calls=%fused_computation.82 | loop fusion | flops 6291456 | bytes 9961480 | tf_op jit(solution)/shard_map/sub | solution.py:103
  67.3 2.1 %fusion.55 = f32[1,16,10,2048]{3,1,2,0:T(8,128)S(1)} fusion(f32[1,16,12,2048]{3,1,2,0:T(8,128)S(1)} %convolution_bitcast_fusion.2, f32[10,2048]{1,0:T(8,128)S(1)} %slice_add_fusion.7, f32[10,2048]{1,0:T(8,128)S(1)} %bitcast.90), kind=kLoop, calls=%fused_computation.104 | loop fusion | flops 4259840 | bytes 7077888 | tf_op jit(solution)/shard_map/mul | solution.py:78
  69.4 1.6 %collective-permute-start.8 = (f32[1,3]{1,0:T(1,128)S(1)}, f32[1,3]{1,0:T(1,128)S(1)}, u32[]{:S(2)}, u32[]{:S(2)}) collective-permute-start(f32[1,3]{1,0:T(1,128)S(1)} %bitcast_add_fusion.1), channel_id=1, source_target_pairs={{0,2},{1,3},{2,0},{3,1},{4,6},{5,7},{6,4},{7,5},{8,10},{9,11},{10,... | collective-permute-start | bytes 44 | tf_op jit(solution)/shard_map/ppermute | solution.py:47
  71.0 2.0 %collective-permute-done.8 = f32[1,3]{1,0:T(1,128)S(1)} collective-permute-done((f32[1,3]{1,0:T(1,128)S(1)}, f32[1,3]{1,0:T(1,128)S(1)}, u32[]{:S(2)}, u32[]{:S(2)}) %collective-permute-start.8) | collective-permute-done | bytes 44 | tf_op jit(solution)/shard_map/ppermute | solution.py:47
  73.0 2.6 %collective-permute-start.9 = (f32[1,3]{1,0:T(1,128)S(1)}, f32[1,3]{1,0:T(1,128)S(1)}, u32[]{:S(2)}, u32[]{:S(2)}) collective-permute-start(f32[1,3]{1,0:T(1,128)S(1)} %add.245), channel_id=1, source_target_pairs={{0,4},{1,5},{2,6},{3,7},{4,0},{5,1},{6,2},{7,3},{8,12},{9,13},{10,... | collective-permute-start | bytes 44 | tf_op jit(solution)/shard_map/ppermute | solution.py:47
  75.6 1.9 %collective-permute-done.9 = f32[1,3]{1,0:T(1,128)S(1)} collective-permute-done((f32[1,3]{1,0:T(1,128)S(1)}, f32[1,3]{1,0:T(1,128)S(1)}, u32[]{:S(2)}, u32[]{:S(2)}) %collective-permute-start.9) | collective-permute-done | bytes 44 | tf_op jit(solution)/shard_map/ppermute | solution.py:47
  80.7 1.9 %multiply_bitcast_fusion.1 = (f32[1,16,8,2048,1]{3,1,2,4,0:T(8,128)S(1)}, f32[1,16,8,2048]{3,1,2,0:T(8,128)S(1)}, f32[1,16,8,2048,1]{3,1,2,4,0:T(8,128)S(1)}) fusion(f32[1,16,8,2048]{3,1,2,0:T(8,128)S(1)} %get-tuple-element.8, f32[1,16,12,2048]{3,1,2,0:T(8,128)S(1)} %fusion.43, f32[]{:T(128)} %bitcast.23, f32[1,16,16,2048]{3,1,2,0:T(8,128)S(1)} %get-tuple-element.12, ...), kind=kLoop, calls=%fused_computation.154 | loop fusion | flops 5505024 | bytes 11927560 | tf_op jit(solution)/shard_map/stack | solution.py:91
  85.8 2.0 %collective-permute-done.11 = f32[1,3]{1,0:T(1,128)S(1)} collective-permute-done((f32[1,3]{1,0:T(1,128)S(1)}, f32[1,3]{1,0:T(1,128)S(1)}, u32[]{:S(2)}, u32[]{:S(2)}) %collective-permute-start.11) | collective-permute-done | bytes 44 | tf_op jit(solution)/shard_map/ppermute | solution.py:47
  87.8 2.6 %collective-permute-start.12 = (f32[1,3]{1,0:T(1,128)S(1)}, f32[1,3]{1,0:T(1,128)S(1)}, u32[]{:S(2)}, u32[]{:S(2)}) collective-permute-start(f32[1,3]{1,0:T(1,128)S(1)} %add.261), channel_id=1, source_target_pairs={{0,4},{1,5},{2,6},{3,7},{4,0},{5,1},{6,2},{7,3},{8,12},{9,13},{10,... | collective-permute-start | bytes 44 | tf_op jit(solution)/shard_map/ppermute | solution.py:47
  90.3 1.9 %collective-permute-done.12 = f32[1,3]{1,0:T(1,128)S(1)} collective-permute-done((f32[1,3]{1,0:T(1,128)S(1)}, f32[1,3]{1,0:T(1,128)S(1)}, u32[]{:S(2)}, u32[]{:S(2)}) %collective-permute-start.12) | collective-permute-done | bytes 44 | tf_op jit(solution)/shard_map/ppermute | solution.py:47
  97.3 3.9 %all-to-all-start.1 = ((f32[1,16,8,2048]{3,2,0,1:T(8,128)}), f32[1,16,8,2048]{3,2,0,1:T(8,128)S(1)}, u32[]{:S(2)}, u32[]{:S(2)}) async-start(f32[1,16,8,2048]{3,2,0,1:T(8,128)} %copy.15), calls=%async_computation.1 | async-start | bytes 2097152 | tf_op jit(solution)/shard_map/all_to_all | solution.py:137
  105.6 2.0 %collective-permute-done.14 = f32[4,7]{1,0:T(4,128)S(1)} collective-permute-done((f32[4,7]{1,0:T(4,128)S(1)}, f32[4,7]{1,0:T(4,128)S(1)}, u32[]{:S(2)}, u32[]{:S(2)}) %collective-permute-start.14) | collective-permute-done | bytes 144 | tf_op jit(solution)/shard_map/ppermute | solution.py:47
  107.6 2.6 %collective-permute-start.15 = (f32[4,7]{1,0:T(4,128)S(1)}, f32[4,7]{1,0:T(4,128)S(1)}, u32[]{:S(2)}, u32[]{:S(2)}) collective-permute-start(f32[4,7]{1,0:T(4,128)S(1)} %add.266), channel_id=1, source_target_pairs={{0,4},{1,5},{2,6},{3,7},{4,0},{5,1},{6,2},{7,3},{8,12},{9,13},{10,... | collective-permute-start | bytes 344 | tf_op jit(solution)/shard_map/ppermute | solution.py:47
  110.2 1.9 %collective-permute-done.15 = f32[4,7]{1,0:T(4,128)S(1)} collective-permute-done((f32[4,7]{1,0:T(4,128)S(1)}, f32[4,7]{1,0:T(4,128)S(1)}, u32[]{:S(2)}, u32[]{:S(2)}) %collective-permute-start.15) | collective-permute-done | bytes 144 | tf_op jit(solution)/shard_map/ppermute | solution.py:47
  112.1 2.0 %collective-permute-start.16 = (f32[4,7]{1,0:T(4,128)S(1)}, f32[4,7]{1,0:T(4,128)S(1)}, u32[]{:S(2)}, u32[]{:S(2)}) collective-permute-start(f32[4,7]{1,0:T(4,128)S(1)} %add.267), channel_id=1, source_target_pairs={{0,8},{8,0},{16,24},{24,16},{1,9},{9,1},{17,25},{25,17},{2,10},{10... | collective-permute-start | bytes 344 | tf_op jit(solution)/shard_map/ppermute | solution.py:47
  115.7 2.0 %collective-permute-start.17 = (f32[4,7]{1,0:T(4,128)S(1)}, f32[4,7]{1,0:T(4,128)S(1)}, u32[]{:S(2)}, u32[]{:S(2)}) collective-permute-start(f32[4,7]{1,0:T(4,128)S(1)} %add.268), channel_id=1, source_target_pairs={{0,16},{8,24},{16,0},{24,8},{1,17},{9,25},{17,1},{25,9},{2,18},{10... | collective-permute-start | bytes 344 | tf_op jit(solution)/shard_map/ppermute | solution.py:47
  (96 shorter events, 28.8 us)
Async XLA Ops:
  0.6 10.3 %copy-start = (f32[16,16]{1,0:T(8,128)S(1)}, f32[16,16]{1,0:T(8,128)}, u32[]{:S(2)}) copy-start(f32[16,16]{1,0:T(8,128)} %param.7) | copy-start | bytes 3076
  0.6 7.4 %copy-start.2 = (f32[8,2048]{1,0:T(8,128)S(1)}, f32[8,2048]{1,0:T(8,128)}, u32[]{:S(2)}) copy-start(f32[8,2048]{1,0:T(8,128)} %param.6) | copy-start | bytes 196612
  2.9 13.2 %all-to-all-start = ((bf16[4,4,8,2048]{3,2,1,0:T(8,128)(2,1)}), bf16[4,4,8,2048]{3,2,1,0:T(8,128)(2,1)S(1)}, u32[]{:S(2)}, u32[]{:S(2)}) async-start(bf16[4,4,8,2048]{3,2,1,0:T(8,128)(2,1)} %multiply_convert_fusion), calls=%async_computation | async-start | bytes 1048576 | tf_op jit(solution)/shard_map/all_to_all | solution.py:68
  8.1 3.5 %collective-permute-start.2 = (f32[6,2048]{1,0:T(8,128)S(1)}, f32[6,2048]{1,0:T(8,128)S(1)}, u32[]{:S(2)}, u32[]{:S(2)}) collective-permute-start(f32[6,2048]{1,0:T(8,128)S(1)} %get-tuple-element.22), channel_id=1, source_target_pairs={{0,1},{1,2},{2,3},{3,4},{4,5},{5,6},{6,7},{8,9},{9,10},{10,11},{11... | collective-permute-start | bytes 147464 | tf_op jit(solution)/shard_map/ppermute | solution.py:59
  9.6 4.8 %collective-permute-start.3 = (f32[6,2048]{1,0:T(8,128)S(1)}, f32[6,2048]{1,0:T(8,128)S(1)}, u32[]{:S(2)}, u32[]{:S(2)}) collective-permute-start(f32[6,2048]{1,0:T(8,128)S(1)} %get-tuple-element.23), channel_id=1, source_target_pairs={{1,0},{2,1},{3,2},{4,3},{5,4},{6,5},{7,6},{9,8},{10,9},{11,10},{12... | collective-permute-start | bytes 147464 | tf_op jit(solution)/shard_map/ppermute | solution.py:60
  16.5 4.9 %collective-permute-start = (bf16[1,16,6,2048]{3,1,2,0:T(8,128)(2,1)S(1)}, bf16[1,16,6,2048]{3,1,2,0:T(8,128)(2,1)S(1)}, u32[]{:S(2)}, u32[]{:S(2)}) collective-permute-start(bf16[1,16,6,2048]{3,1,2,0:T(8,128)(2,1)S(1)} %get-tuple-element.20), channel_id=1, source_target_pairs={{0,1},{1,2},{2,3},{3,4},{4,5},{5,6},{6,7},{8,9},{9,10},{10,11},{11... | collective-permute-start | bytes 1179656 | tf_op jit(solution)/shard_map/ppermute | solution.py:59
  19.8 3.6 %collective-permute-start.1 = (bf16[1,16,6,2048]{3,1,2,0:T(8,128)(2,1)S(1)}, bf16[1,16,6,2048]{3,1,2,0:T(8,128)(2,1)S(1)}, u32[]{:S(2)}, u32[]{:S(2)}) collective-permute-start(bf16[1,16,6,2048]{3,1,2,0:T(8,128)(2,1)S(1)} %get-tuple-element.21), channel_id=1, source_target_pairs={{1,0},{2,1},{3,2},{4,3},{5,4},{6,5},{7,6},{9,8},{10,9},{11,10},{12... | collective-permute-start | bytes 1179656 | tf_op jit(solution)/shard_map/ppermute | solution.py:60
  23.7 3.2 %copy-start.1 = (f32[1,1,20,2048]{3,1,2,0:T(1,128)}, f32[1,1,20,2048]{3,1,2,0:T(1,128)S(1)}, u32[]{:S(2)}) copy-start(f32[1,1,20,2048]{3,1,2,0:T(1,128)S(1)} %slice_multiply_fusion.11) | copy-start | bytes 491524
  37.8 6.2 %slice-start = ((f32[1,1,20,2048]{3,1,2,0:T(1,128)}), f32[1,1,14,2048]{3,1,2,0:T(1,128)S(1)}, s32[]{:S(2)}) async-start(f32[1,1,20,2048]{3,1,2,0:T(1,128)} %copy-done.1), calls=%async_computation.2 | async-start | bytes 229376 | tf_op jit(solution)/shard_map/slice | solution.py:78
  37.8 6.3 %slice-start.1 = ((f32[1,1,20,2048]{3,1,2,0:T(1,128)}), f32[1,1,12,2048]{3,1,2,0:T(1,128)S(1)}, s32[]{:S(2)}) async-start(f32[1,1,20,2048]{3,1,2,0:T(1,128)} %copy-done.1), calls=%async_computation.3 | async-start | bytes 196608 | tf_op jit(solution)/shard_map/slice | solution.py:79
  37.8 6.3 %slice-start.2 = ((f32[1,1,20,2048]{3,1,2,0:T(1,128)}), f32[1,1,10,2048]{3,1,2,0:T(1,128)S(1)}, s32[]{:S(2)}) async-start(f32[1,1,20,2048]{3,1,2,0:T(1,128)} %copy-done.1), calls=%async_computation.4 | async-start | bytes 163840 | tf_op jit(solution)/shard_map/slice | solution.py:78
  37.8 6.3 %slice-start.3 = ((f32[1,1,20,2048]{3,1,2,0:T(1,128)}), f32[1,1,8,2048]{3,1,2,0:T(1,128)S(1)}, s32[]{:S(2)}) async-start(f32[1,1,20,2048]{3,1,2,0:T(1,128)} %copy-done.1), calls=%async_computation.5 | async-start | bytes 131072 | tf_op jit(solution)/shard_map/slice | solution.py:79
  38.2 9.4 %collective-permute-start.4 = (f32[1,2]{1,0:T(1,128)S(1)}, f32[1,2]{1,0:T(1,128)S(1)}, u32[]{:S(2)}, u32[]{:S(2)}) collective-permute-start(f32[1,2]{1,0:T(1,128)S(1)} %bitcast.94), channel_id=1, source_target_pairs={{0,1},{1,0},{2,3},{3,2},{4,5},{5,4},{6,7},{7,6},{8,9},{9,8},{10,11... | collective-permute-start | bytes 32 | tf_op jit(solution)/shard_map/ppermute | solution.py:47
  47.6 3.6 %collective-permute-start.5 = (f32[1,2]{1,0:T(1,128)S(1)}, f32[1,2]{1,0:T(1,128)S(1)}, u32[]{:S(2)}, u32[]{:S(2)}) collective-permute-start(f32[1,2]{1,0:T(1,128)S(1)} %bitcast_add_fusion.2), channel_id=1, source_target_pairs={{0,2},{1,3},{2,0},{3,1},{4,6},{5,7},{6,4},{7,5},{8,10},{9,11},{10,... | collective-permute-start | bytes 32 | tf_op jit(solution)/shard_map/ppermute | solution.py:47
  51.3 4.5 %collective-permute-start.6 = (f32[1,2]{1,0:T(1,128)S(1)}, f32[1,2]{1,0:T(1,128)S(1)}, u32[]{:S(2)}, u32[]{:S(2)}) collective-permute-start(f32[1,2]{1,0:T(1,128)S(1)} %add.229), channel_id=1, source_target_pairs={{0,4},{1,5},{2,6},{3,7},{4,0},{5,1},{6,2},{7,3},{8,12},{9,13},{10,... | collective-permute-start | bytes 32 | tf_op jit(solution)/shard_map/ppermute | solution.py:47
  67.2 2.1 %collective-permute-start.7 = (f32[1,3]{1,0:T(1,128)S(1)}, f32[1,3]{1,0:T(1,128)S(1)}, u32[]{:S(2)}, u32[]{:S(2)}) collective-permute-start(f32[1,3]{1,0:T(1,128)S(1)} %bitcast.95), channel_id=1, source_target_pairs={{0,1},{1,0},{2,3},{3,2},{4,5},{5,4},{6,7},{7,6},{8,9},{9,8},{10,11... | collective-permute-start | bytes 44 | tf_op jit(solution)/shard_map/ppermute | solution.py:47
  69.4 3.6 %collective-permute-start.8 = (f32[1,3]{1,0:T(1,128)S(1)}, f32[1,3]{1,0:T(1,128)S(1)}, u32[]{:S(2)}, u32[]{:S(2)}) collective-permute-start(f32[1,3]{1,0:T(1,128)S(1)} %bitcast_add_fusion.1), channel_id=1, source_target_pairs={{0,2},{1,3},{2,0},{3,1},{4,6},{5,7},{6,4},{7,5},{8,10},{9,11},{10,... | collective-permute-start | bytes 44 | tf_op jit(solution)/shard_map/ppermute | solution.py:47
  73.0 4.5 %collective-permute-start.9 = (f32[1,3]{1,0:T(1,128)S(1)}, f32[1,3]{1,0:T(1,128)S(1)}, u32[]{:S(2)}, u32[]{:S(2)}) collective-permute-start(f32[1,3]{1,0:T(1,128)S(1)} %add.245), channel_id=1, source_target_pairs={{0,4},{1,5},{2,6},{3,7},{4,0},{5,1},{6,2},{7,3},{8,12},{9,13},{10,... | collective-permute-start | bytes 44 | tf_op jit(solution)/shard_map/ppermute | solution.py:47
  83.0 1.2 collective-permute-start.10
  84.2 3.6 %collective-permute-start.11 = (f32[1,3]{1,0:T(1,128)S(1)}, f32[1,3]{1,0:T(1,128)S(1)}, u32[]{:S(2)}, u32[]{:S(2)}) collective-permute-start(f32[1,3]{1,0:T(1,128)S(1)} %bitcast_add_fusion), channel_id=1, source_target_pairs={{0,2},{1,3},{2,0},{3,1},{4,6},{5,7},{6,4},{7,5},{8,10},{9,11},{10,... | collective-permute-start | bytes 44 | tf_op jit(solution)/shard_map/ppermute | solution.py:47
  87.8 4.5 %collective-permute-start.12 = (f32[1,3]{1,0:T(1,128)S(1)}, f32[1,3]{1,0:T(1,128)S(1)}, u32[]{:S(2)}, u32[]{:S(2)}) collective-permute-start(f32[1,3]{1,0:T(1,128)S(1)} %add.261), channel_id=1, source_target_pairs={{0,4},{1,5},{2,6},{3,7},{4,0},{5,1},{6,2},{7,3},{8,12},{9,13},{10,... | collective-permute-start | bytes 44 | tf_op jit(solution)/shard_map/ppermute | solution.py:47
  97.3 22.9 %all-to-all-start.1 = ((f32[1,16,8,2048]{3,2,0,1:T(8,128)}), f32[1,16,8,2048]{3,2,0,1:T(8,128)S(1)}, u32[]{:S(2)}, u32[]{:S(2)}) async-start(f32[1,16,8,2048]{3,2,0,1:T(8,128)} %copy.15), calls=%async_computation.1 | async-start | bytes 2097152 | tf_op jit(solution)/shard_map/all_to_all | solution.py:137
  102.0 1.2 collective-permute-start.13
  104.0 3.6 %collective-permute-start.14 = (f32[4,7]{1,0:T(4,128)S(1)}, f32[4,7]{1,0:T(4,128)S(1)}, u32[]{:S(2)}, u32[]{:S(2)}) collective-permute-start(f32[4,7]{1,0:T(4,128)S(1)} %add.265), channel_id=1, source_target_pairs={{0,2},{1,3},{2,0},{3,1},{4,6},{5,7},{6,4},{7,5},{8,10},{9,11},{10,... | collective-permute-start | bytes 344 | tf_op jit(solution)/shard_map/ppermute | solution.py:47
  107.6 4.5 %collective-permute-start.15 = (f32[4,7]{1,0:T(4,128)S(1)}, f32[4,7]{1,0:T(4,128)S(1)}, u32[]{:S(2)}, u32[]{:S(2)}) collective-permute-start(f32[4,7]{1,0:T(4,128)S(1)} %add.266), channel_id=1, source_target_pairs={{0,4},{1,5},{2,6},{3,7},{4,0},{5,1},{6,2},{7,3},{8,12},{9,13},{10,... | collective-permute-start | bytes 344 | tf_op jit(solution)/shard_map/ppermute | solution.py:47
  112.1 3.6 %collective-permute-start.16 = (f32[4,7]{1,0:T(4,128)S(1)}, f32[4,7]{1,0:T(4,128)S(1)}, u32[]{:S(2)}, u32[]{:S(2)}) collective-permute-start(f32[4,7]{1,0:T(4,128)S(1)} %add.267), channel_id=1, source_target_pairs={{0,8},{8,0},{16,24},{24,16},{1,9},{9,1},{17,25},{25,17},{2,10},{10... | collective-permute-start | bytes 344 | tf_op jit(solution)/shard_map/ppermute | solution.py:47
  115.7 3.6 %collective-permute-start.17 = (f32[4,7]{1,0:T(4,128)S(1)}, f32[4,7]{1,0:T(4,128)S(1)}, u32[]{:S(2)}, u32[]{:S(2)}) collective-permute-start(f32[4,7]{1,0:T(4,128)S(1)} %add.268), channel_id=1, source_target_pairs={{0,16},{8,24},{16,0},{24,8},{1,17},{9,25},{17,1},{25,9},{2,18},{10... | collective-permute-start | bytes 344 | tf_op jit(solution)/shard_map/ppermute | solution.py:47
  119.3 2.2 %copy-start.3 = (f32[4,7]{1,0:T(4,128)}, f32[4,7]{1,0:T(4,128)S(1)}, u32[]{:S(2)}) copy-start(f32[4,7]{1,0:T(4,128)S(1)} %add.269) | copy-start | bytes 340

commit v6 on v5

--- a/solution.py
+++ b/solution.py
@@ -74,7 +74,7 @@
 
     def apply_a(x, off):
         r = x.shape[2]
-        mixed = jnp.einsum("ts,psrc->ptrc", trait_covariance, x, precision=lax.Precision.HIGHEST)
+        mixed = jnp.einsum("ts,psrc->ptrc", trait_covariance, x, precision=lax.Precision.HIGH)
         first = land_ext[off + 1 : off + r - 1] * nine_valid(mixed, kappa_ext[off + 1 : off + r - 1])
         return land_ext[off + 2 : off + r - 2] * nine_valid(first, kappa_ext[off + 2 : off + r - 2])
 

time: 122 us -> 119 us (0.975)
  matrix products: 6.47 us -> 3.44 us
    dot_general x3, matrix products: 6.47 us -> 3.44 us  [apply_a(): jnp.einsum('ts,psrc->ptrc', trait_covariance, x, precision=lax.Precision....]
where the time goes in v6:
time: 119 us; the launch traced here: 118 us
  starting transfers between devices  43.1 us (36%)
  other arithmetic  32.8 us (28%)
  waiting for transfers between devices  27.3 us (23%)
  between operations  6.36 us (5%)
  local copies, waits for them, and re-layouts  5.39 us (5%)
  matrix products  3.44 us (3%)
    ppermute x14, starting transfers between devices, butterfly_sum(): v = v + lax.ppermute(v, axis, [(i, i ^ s) for i in range(n)])  26.8 us
    ppermute x14, waiting for transfers between devices, butterfly_sum(): v = v + lax.ppermute(v, axis, [(i, i ^ s) for i in range(n)])  21 us
    mul x3, other arithmetic, apply_a(): land_ext[off + 1:off + r - 1]  10.1 us
    all_to_all x1, starting transfers between devices, shards(): lax.all_to_all(signed, 'trait', split_axis=0, concat_axis=1, tiled=True)  5.19 us
    ppermute x2, waiting for transfers between devices, halo_rows(): lax.ppermute(lax.slice_in_dim(block, 0, width, axis=dim), 'tile', backward)  4.76 us
    ppermute x2, starting transfers between devices, halo_rows(): lax.ppermute(lax.slice_in_dim(block, rows - width, rows, axis=dim), 'tile...  4.75 us
    sub x1, other arithmetic, shards(): w = aq - alpha[:, None, None, None] * q  3.93 us
    mul x1, other arithmetic, apply_a(): land_ext[off + 2:off + r - 2]  3.87 us
  transfers between devices with their start and end apart: 20, of which 15 were waited for; matrix products, arithmetic and copies ran while one was open for 8% of the time, Pallas kernels for 0%

profile of v6, /device:TPU:0, one launch (start us, length us, event | category | flops | bytes accessed | tf_op | source)
XLA Modules:
  0.0 118.4 jit_solution(11458569564129102568)
XLA Ops:
  0.7 2.2 %multiply_convert_fusion = bf16[4,4,8,2048]{3,2,1,0:T(8,128)(2,1)} fusion(s32[4,4,8,2048]{3,2,1,0:T(8,128)} %param.4, s32[8,2048]{1,0:T(8,128)} %param.5), kind=kLoop, calls=%fused_computation.160 | loop fusion | flops 1048576 | bytes 1638400 | tf_op jit(solution)/shard_map/convert_element_type | solution.py:67
  2.9 5.2 %all-to-all-start = ((bf16[4,4,8,2048]{3,2,1,0:T(8,128)(2,1)}), bf16[4,4,8,2048]{3,2,1,0:T(8,128)(2,1)S(1)}, u32[]{:S(2)}, u32[]{:S(2)}) async-start(bf16[4,4,8,2048]{3,2,1,0:T(8,128)(2,1)} %multiply_convert_fusion), calls=%async_computation | async-start | bytes 1048576 | tf_op jit(solution)/shard_map/all_to_all | solution.py:68
  11.6 2.8 %collective-permute-done.3 = f32[6,2048]{1,0:T(8,128)S(1)} collective-permute-done((f32[6,2048]{1,0:T(8,128)S(1)}, f32[6,2048]{1,0:T(8,128)S(1)}, u32[]{:S(2)}, u32[]{:S(2)}) %collective-permute-start.3) | collective-permute-done | bytes 49184 | tf_op jit(solution)/shard_map/ppermute | solution.py:60
  14.5 1.6 %all-to-all-done = bf16[4,4,8,2048]{3,2,1,0:T(8,128)(2,1)S(1)} async-done(((bf16[4,4,8,2048]{3,2,1,0:T(8,128)(2,1)}), bf16[4,4,8,2048]{3,2,1,0:T(8,128)(2,1)S(1)}, u32[]{:S(2)}, u32[]{:S(2)}) %all-to-all-start) | async-done | bytes 524320 | tf_op jit(solution)/shard_map/all_to_all | solution.py:68
  16.5 3.3 %collective-permute-start = (bf16[1,16,6,2048]{3,1,2,0:T(8,128)(2,1)S(1)}, bf16[1,16,6,2048]{3,1,2,0:T(8,128)(2,1)S(1)}, u32[]{:S(2)}, u32[]{:S(2)}) collective-permute-start(bf16[1,16,6,2048]{3,1,2,0:T(8,128)(2,1)S(1)} %get-tuple-element.20), channel_id=1, source_target_pairs={{0,1},{1,2},{2,3},{3,4},{4,5},{5,6},{6,7},{8,9},{9,10},{10,11},{11... | collective-permute-start | bytes 1179656 | tf_op jit(solution)/shard_map/ppermute | solution.py:59
  21.4 2.0 %collective-permute-done.1 = bf16[1,16,6,2048]{3,1,2,0:T(8,128)(2,1)S(1)} collective-permute-done((bf16[1,16,6,2048]{3,1,2,0:T(8,128)(2,1)S(1)}, bf16[1,16,6,2048]{3,1,2,0:T(8,128)(2,1)S(1)}, u32[]{:S(2)}, u32[]{:S(2)}) %collective-permute-start.1) | collective-permute-done | bytes 393248 | tf_op jit(solution)/shard_map/ppermute | solution.py:60
  25.4 4.6 %fusion.7 = f32[1,16,18,2048]{3,1,2,0:T(8,128)S(1)} fusion(f32[1,16,20,2048]{3,1,2,0:T(8,128)S(1)} %convolution_bitcast_fusion, f32[18,2048]{1,0:T(8,128)S(1)} %slice_add_fusion.6, f32[18,2048]{1,0:T(8,128)S(1)} %bitcast.88), kind=kLoop, calls=%fused_computation.19 | loop fusion | flops 7667712 | bytes 12451840 | tf_op jit(solution)/shard_map/mul | solution.py:78
  30.0 3.9 %fusion.18 = f32[1,16,16,2048]{3,1,2,0:T(8,128)S(1)} fusion(f32[1,16,18,2048]{3,1,2,0:T(8,128)S(1)} %fusion.7, f32[16,2048]{1,0:T(8,128)S(1)} %slice_add_fusion.10, f32[16,2048]{1,0:T(8,128)S(1)} %bitcast.86), kind=kLoop, calls=%fused_computation.38 | loop fusion | flops 6815744 | bytes 11010048 | tf_op jit(solution)/shard_map/mul | solution.py:79
  35.8 5.8 %collective-permute-start.4 = (f32[1,2]{1,0:T(1,128)S(1)}, f32[1,2]{1,0:T(1,128)S(1)}, u32[]{:S(2)}, u32[]{:S(2)}) collective-permute-start(f32[1,2]{1,0:T(1,128)S(1)} %bitcast.94), channel_id=1, source_target_pairs={{0,1},{1,0},{2,3},{3,2},{4,5},{5,4},{6,7},{7,6},{8,9},{9,8},{10,11... | collective-permute-start | bytes 32 | tf_op jit(solution)/shard_map/ppermute | solution.py:47
  41.8 3.4 %fusion.30 = f32[1,16,14,2048]{3,1,2,0:T(8,128)S(1)} fusion(f32[1,16,16,2048]{3,1,2,0:T(8,128)S(1)} %convolution_bitcast_fusion.1, f32[14,2048]{1,0:T(8,128)S(1)} %slice_add_fusion.8, f32[14,2048]{1,0:T(8,128)S(1)} %bitcast.91), kind=kLoop, calls=%fused_computation.61 | loop fusion | flops 5963776 | bytes 9699328 | tf_op jit(solution)/shard_map/mul | solution.py:78
  45.3 1.6 %collective-permute-start.5 = (f32[1,2]{1,0:T(1,128)S(1)}, f32[1,2]{1,0:T(1,128)S(1)}, u32[]{:S(2)}, u32[]{:S(2)}) collective-permute-start(f32[1,2]{1,0:T(1,128)S(1)} %bitcast_add_fusion.2), channel_id=1, source_target_pairs={{0,2},{1,3},{2,0},{3,1},{4,6},{5,7},{6,4},{7,5},{8,10},{9,11},{10,... | collective-permute-start | bytes 32 | tf_op jit(solution)/shard_map/ppermute | solution.py:47
  46.9 2.0 %collective-permute-done.5 = f32[1,2]{1,0:T(1,128)S(1)} collective-permute-done((f32[1,2]{1,0:T(1,128)S(1)}, f32[1,2]{1,0:T(1,128)S(1)}, u32[]{:S(2)}, u32[]{:S(2)}) %collective-permute-start.5) | collective-permute-done | bytes 40 | tf_op jit(solution)/shard_map/ppermute | solution.py:47
  48.9 2.6 %collective-permute-start.6 = (f32[1,2]{1,0:T(1,128)S(1)}, f32[1,2]{1,0:T(1,128)S(1)}, u32[]{:S(2)}, u32[]{:S(2)}) collective-permute-start(f32[1,2]{1,0:T(1,128)S(1)} %add.229), channel_id=1, source_target_pairs={{0,4},{1,5},{2,6},{3,7},{4,0},{5,1},{6,2},{7,3},{8,12},{9,13},{10,... | collective-permute-start | bytes 32 | tf_op jit(solution)/shard_map/ppermute | solution.py:47
  51.5 1.9 %collective-permute-done.6 = f32[1,2]{1,0:T(1,128)S(1)} collective-permute-done((f32[1,2]{1,0:T(1,128)S(1)}, f32[1,2]{1,0:T(1,128)S(1)}, u32[]{:S(2)}, u32[]{:S(2)}) %collective-permute-start.6) | collective-permute-done | bytes 40 | tf_op jit(solution)/shard_map/ppermute | solution.py:47
  55.3 3.9 %multiply_subtract_fusion = (f32[1,16,16,2048]{3,1,2,0:T(8,128)S(1)}, f32[1,16,16,2048]{3,1,2,0:T(8,128)S(1)}, f32[1,16,16,2048]{3,1,2,0:T(8,128)S(1)}) fusion(f32[]{:T(128)} %bitcast.13, f32[]{:T(128)} %bitcast.12, f32[1,16,20,2048]{3,1,2,0:T(8,128)S(1)} %broadcast_multiply_fusion, f32[1,16,18,2048]{3,1,2,0:T(8,128)S(1)} %fusion.7, ...), kind=kLoop, calls=%fused_computation.49 | loop fusion | flops 8912896 | bytes 17301512 | tf_op jit(solution)/shard_map/sub | solution.py:102
  59.3 3.2 %fusion.43 = f32[1,16,12,2048]{3,1,2,0:T(8,128)S(1)} fusion(f32[1,16,14,2048]{3,1,2,0:T(8,128)S(1)} %fusion.30, f32[1,16,16,2048]{3,1,2,0:T(8,128)S(1)} %get-tuple-element.12, f32[]{:T(128)} %bitcast.13, f32[]{:T(128)} %bitcast.12, f32[12,2048]{1,0:T(8,128)S(1)} %slice_add_fusion.9, f32[12,2048]{1,0:T(8,128)S(1)} %bitcast.89), kind=kLoop, calls=%fused_computation.82 | loop fusion | flops 6291456 | bytes 9961480 | tf_op jit(solution)/shard_map/sub | solution.py:103
  64.2 2.1 %fusion.55 = f32[1,16,10,2048]{3,1,2,0:T(8,128)S(1)} fusion(f32[1,16,12,2048]{3,1,2,0:T(8,128)S(1)} %convolution_bitcast_fusion.2, f32[10,2048]{1,0:T(8,128)S(1)} %slice_add_fusion.7, f32[10,2048]{1,0:T(8,128)S(1)} %bitcast.90), kind=kLoop, calls=%fused_computation.104 | loop fusion | flops 4259840 | bytes 7077888 | tf_op jit(solution)/shard_map/mul | solution.py:78
  66.3 1.6 %collective-permute-start.8 = (f32[1,3]{1,0:T(1,128)S(1)}, f32[1,3]{1,0:T(1,128)S(1)}, u32[]{:S(2)}, u32[]{:S(2)}) collective-permute-start(f32[1,3]{1,0:T(1,128)S(1)} %bitcast_add_fusion.1), channel_id=1, source_target_pairs={{0,2},{1,3},{2,0},{3,1},{4,6},{5,7},{6,4},{7,5},{8,10},{9,11},{10,... | collective-permute-start | bytes 44 | tf_op jit(solution)/shard_map/ppermute | solution.py:47
  68.0 2.0 %collective-permute-done.8 = f32[1,3]{1,0:T(1,128)S(1)} collective-permute-done((f32[1,3]{1,0:T(1,128)S(1)}, f32[1,3]{1,0:T(1,128)S(1)}, u32[]{:S(2)}, u32[]{:S(2)}) %collective-permute-start.8) | collective-permute-done | bytes 44 | tf_op jit(solution)/shard_map/ppermute | solution.py:47
  70.0 2.6 %collective-permute-start.9 = (f32[1,3]{1,0:T(1,128)S(1)}, f32[1,3]{1,0:T(1,128)S(1)}, u32[]{:S(2)}, u32[]{:S(2)}) collective-permute-start(f32[1,3]{1,0:T(1,128)S(1)} %add.245), channel_id=1, source_target_pairs={{0,4},{1,5},{2,6},{3,7},{4,0},{5,1},{6,2},{7,3},{8,12},{9,13},{10,... | collective-permute-start | bytes 44 | tf_op jit(solution)/shard_map/ppermute | solution.py:47
  72.6 1.9 %collective-permute-done.9 = f32[1,3]{1,0:T(1,128)S(1)} collective-permute-done((f32[1,3]{1,0:T(1,128)S(1)}, f32[1,3]{1,0:T(1,128)S(1)}, u32[]{:S(2)}, u32[]{:S(2)}) %collective-permute-start.9) | collective-permute-done | bytes 44 | tf_op jit(solution)/shard_map/ppermute | solution.py:47
  77.6 1.9 %multiply_bitcast_fusion.1 = (f32[1,16,8,2048,1]{3,1,2,4,0:T(8,128)S(1)}, f32[1,16,8,2048]{3,1,2,0:T(8,128)S(1)}, f32[1,16,8,2048,1]{3,1,2,4,0:T(8,128)S(1)}) fusion(f32[1,16,8,2048]{3,1,2,0:T(8,128)S(1)} %get-tuple-element.8, f32[1,16,12,2048]{3,1,2,0:T(8,128)S(1)} %fusion.43, f32[]{:T(128)} %bitcast.23, f32[1,16,16,2048]{3,1,2,0:T(8,128)S(1)} %get-tuple-element.12, ...), kind=kLoop, calls=%fused_computation.154 | loop fusion | flops 5505024 | bytes 11927560 | tf_op jit(solution)/shard_map/stack | solution.py:91
  82.7 2.0 %collective-permute-done.11 = f32[1,3]{1,0:T(1,128)S(1)} collective-permute-done((f32[1,3]{1,0:T(1,128)S(1)}, f32[1,3]{1,0:T(1,128)S(1)}, u32[]{:S(2)}, u32[]{:S(2)}) %collective-permute-start.11) | collective-permute-done | bytes 44 | tf_op jit(solution)/shard_map/ppermute | solution.py:47
  84.7 2.6 %collective-permute-start.12 = (f32[1,3]{1,0:T(1,128)S(1)}, f32[1,3]{1,0:T(1,128)S(1)}, u32[]{:S(2)}, u32[]{:S(2)}) collective-permute-start(f32[1,3]{1,0:T(1,128)S(1)} %add.261), channel_id=1, source_target_pairs={{0,4},{1,5},{2,6},{3,7},{4,0},{5,1},{6,2},{7,3},{8,12},{9,13},{10,... | collective-permute-start | bytes 44 | tf_op jit(solution)/shard_map/ppermute | solution.py:47
  87.3 1.9 %collective-permute-done.12 = f32[1,3]{1,0:T(1,128)S(1)} collective-permute-done((f32[1,3]{1,0:T(1,128)S(1)}, f32[1,3]{1,0:T(1,128)S(1)}, u32[]{:S(2)}, u32[]{:S(2)}) %collective-permute-start.12) | collective-permute-done | bytes 44 | tf_op jit(solution)/shard_map/ppermute | solution.py:47
  94.3 3.9 %all-to-all-start.1 = ((f32[1,16,8,2048]{3,2,0,1:T(8,128)}), f32[1,16,8,2048]{3,2,0,1:T(8,128)S(1)}, u32[]{:S(2)}, u32[]{:S(2)}) async-start(f32[1,16,8,2048]{3,2,0,1:T(8,128)} %copy.15), calls=%async_computation.1 | async-start | bytes 2097152 | tf_op jit(solution)/shard_map/all_to_all | solution.py:137
  101.0 1.6 %collective-permute-start.14 = (f32[4,7]{1,0:T(4,128)S(1)}, f32[4,7]{1,0:T(4,128)S(1)}, u32[]{:S(2)}, u32[]{:S(2)}) collective-permute-start(f32[4,7]{1,0:T(4,128)S(1)} %add.265), channel_id=1, source_target_pairs={{0,2},{1,3},{2,0},{3,1},{4,6},{5,7},{6,4},{7,5},{8,10},{9,11},{10,... | collective-permute-start | bytes 344 | tf_op jit(solution)/shard_map/ppermute | solution.py:47
  102.6 2.0 %collective-permute-done.14 = f32[4,7]{1,0:T(4,128)S(1)} collective-permute-done((f32[4,7]{1,0:T(4,128)S(1)}, f32[4,7]{1,0:T(4,128)S(1)}, u32[]{:S(2)}, u32[]{:S(2)}) %collective-permute-start.14) | collective-permute-done | bytes 144 | tf_op jit(solution)/shard_map/ppermute | solution.py:47
  104.6 2.6 %collective-permute-start.15 = (f32[4,7]{1,0:T(4,128)S(1)}, f32[4,7]{1,0:T(4,128)S(1)}, u32[]{:S(2)}, u32[]{:S(2)}) collective-permute-start(f32[4,7]{1,0:T(4,128)S(1)} %add.266), channel_id=1, source_target_pairs={{0,4},{1,5},{2,6},{3,7},{4,0},{5,1},{6,2},{7,3},{8,12},{9,13},{10,... | collective-permute-start | bytes 344 | tf_op jit(solution)/shard_map/ppermute | solution.py:47
  107.2 1.9 %collective-permute-done.15 = f32[4,7]{1,0:T(4,128)S(1)} collective-permute-done((f32[4,7]{1,0:T(4,128)S(1)}, f32[4,7]{1,0:T(4,128)S(1)}, u32[]{:S(2)}, u32[]{:S(2)}) %collective-permute-start.15) | collective-permute-done | bytes 144 | tf_op jit(solution)/shard_map/ppermute | solution.py:47
  109.1 2.0 %collective-permute-start.16 = (f32[4,7]{1,0:T(4,128)S(1)}, f32[4,7]{1,0:T(4,128)S(1)}, u32[]{:S(2)}, u32[]{:S(2)}) collective-permute-start(f32[4,7]{1,0:T(4,128)S(1)} %add.267), channel_id=1, source_target_pairs={{0,8},{8,0},{16,24},{24,16},{1,9},{9,1},{17,25},{25,17},{2,10},{10... | collective-permute-start | bytes 344 | tf_op jit(solution)/shard_map/ppermute | solution.py:47
  112.7 2.0 %collective-permute-start.17 = (f32[4,7]{1,0:T(4,128)S(1)}, f32[4,7]{1,0:T(4,128)S(1)}, u32[]{:S(2)}, u32[]{:S(2)}) collective-permute-start(f32[4,7]{1,0:T(4,128)S(1)} %add.268), channel_id=1, source_target_pairs={{0,16},{8,24},{16,0},{24,8},{1,17},{9,25},{17,1},{25,9},{2,18},{10... | collective-permute-start | bytes 344 | tf_op jit(solution)/shard_map/ppermute | solution.py:47
  (96 shorter events, 27.5 us)
Async XLA Ops:
  0.6 10.3 %copy-start = (f32[16,16]{1,0:T(8,128)S(1)}, f32[16,16]{1,0:T(8,128)}, u32[]{:S(2)}) copy-start(f32[16,16]{1,0:T(8,128)} %param.7) | copy-start | bytes 3076
  0.6 7.4 %copy-start.2 = (f32[8,2048]{1,0:T(8,128)S(1)}, f32[8,2048]{1,0:T(8,128)}, u32[]{:S(2)}) copy-start(f32[8,2048]{1,0:T(8,128)} %param.6) | copy-start | bytes 196612
  2.9 13.2 %all-to-all-start = ((bf16[4,4,8,2048]{3,2,1,0:T(8,128)(2,1)}), bf16[4,4,8,2048]{3,2,1,0:T(8,128)(2,1)S(1)}, u32[]{:S(2)}, u32[]{:S(2)}) async-start(bf16[4,4,8,2048]{3,2,1,0:T(8,128)(2,1)} %multiply_convert_fusion), calls=%async_computation | async-start | bytes 1048576 | tf_op jit(solution)/shard_map/all_to_all | solution.py:68
  8.1 3.5 %collective-permute-start.2 = (f32[6,2048]{1,0:T(8,128)S(1)}, f32[6,2048]{1,0:T(8,128)S(1)}, u32[]{:S(2)}, u32[]{:S(2)}) collective-permute-start(f32[6,2048]{1,0:T(8,128)S(1)} %get-tuple-element.22), channel_id=1, source_target_pairs={{0,1},{1,2},{2,3},{3,4},{4,5},{5,6},{6,7},{8,9},{9,10},{10,11},{11... | collective-permute-start | bytes 147464 | tf_op jit(solution)/shard_map/ppermute | solution.py:59
  9.6 4.8 %collective-permute-start.3 = (f32[6,2048]{1,0:T(8,128)S(1)}, f32[6,2048]{1,0:T(8,128)S(1)}, u32[]{:S(2)}, u32[]{:S(2)}) collective-permute-start(f32[6,2048]{1,0:T(8,128)S(1)} %get-tuple-element.23), channel_id=1, source_target_pairs={{1,0},{2,1},{3,2},{4,3},{5,4},{6,5},{7,6},{9,8},{10,9},{11,10},{12... | collective-permute-start | bytes 147464 | tf_op jit(solution)/shard_map/ppermute | solution.py:60
  16.5 4.9 %collective-permute-start = (bf16[1,16,6,2048]{3,1,2,0:T(8,128)(2,1)S(1)}, bf16[1,16,6,2048]{3,1,2,0:T(8,128)(2,1)S(1)}, u32[]{:S(2)}, u32[]{:S(2)}) collective-permute-start(bf16[1,16,6,2048]{3,1,2,0:T(8,128)(2,1)S(1)} %get-tuple-element.20), channel_id=1, source_target_pairs={{0,1},{1,2},{2,3},{3,4},{4,5},{5,6},{6,7},{8,9},{9,10},{10,11},{11... | collective-permute-start | bytes 1179656 | tf_op jit(solution)/shard_map/ppermute | solution.py:59
  19.8 3.6 %collective-permute-start.1 = (bf16[1,16,6,2048]{3,1,2,0:T(8,128)(2,1)S(1)}, bf16[1,16,6,2048]{3,1,2,0:T(8,128)(2,1)S(1)}, u32[]{:S(2)}, u32[]{:S(2)}) collective-permute-start(bf16[1,16,6,2048]{3,1,2,0:T(8,128)(2,1)S(1)} %get-tuple-element.21), channel_id=1, source_target_pairs={{1,0},{2,1},{3,2},{4,3},{5,4},{6,5},{7,6},{9,8},{10,9},{11,10},{12... | collective-permute-start | bytes 1179656 | tf_op jit(solution)/shard_map/ppermute | solution.py:60
  23.7 1.7 %copy-start.1 = (f32[1,1,20,2048]{3,1,2,0:T(1,128)}, f32[1,1,20,2048]{3,1,2,0:T(1,128)S(1)}, u32[]{:S(2)}) copy-start(f32[1,1,20,2048]{3,1,2,0:T(1,128)S(1)} %slice_multiply_fusion.11) | copy-start | bytes 491524
  35.4 6.2 %slice-start = ((f32[1,1,20,2048]{3,1,2,0:T(1,128)}), f32[1,1,14,2048]{3,1,2,0:T(1,128)S(1)}, s32[]{:S(2)}) async-start(f32[1,1,20,2048]{3,1,2,0:T(1,128)} %copy-done.1), calls=%async_computation.2 | async-start | bytes 229376 | tf_op jit(solution)/shard_map/slice | solution.py:78
  35.4 6.3 %slice-start.1 = ((f32[1,1,20,2048]{3,1,2,0:T(1,128)}), f32[1,1,12,2048]{3,1,2,0:T(1,128)S(1)}, s32[]{:S(2)}) async-start(f32[1,1,20,2048]{3,1,2,0:T(1,128)} %copy-done.1), calls=%async_computation.3 | async-start | bytes 196608 | tf_op jit(solution)/shard_map/slice | solution.py:79
  35.4 6.3 %slice-start.2 = ((f32[1,1,20,2048]{3,1,2,0:T(1,128)}), f32[1,1,10,2048]{3,1,2,0:T(1,128)S(1)}, s32[]{:S(2)}) async-start(f32[1,1,20,2048]{3,1,2,0:T(1,128)} %copy-done.1), calls=%async_computation.4 | async-start | bytes 163840 | tf_op jit(solution)/shard_map/slice | solution.py:78
  35.4 6.3 %slice-start.3 = ((f32[1,1,20,2048]{3,1,2,0:T(1,128)}), f32[1,1,8,2048]{3,1,2,0:T(1,128)S(1)}, s32[]{:S(2)}) async-start(f32[1,1,20,2048]{3,1,2,0:T(1,128)} %copy-done.1), calls=%async_computation.5 | async-start | bytes 131072 | tf_op jit(solution)/shard_map/slice | solution.py:79
  35.8 9.4 %collective-permute-start.4 = (f32[1,2]{1,0:T(1,128)S(1)}, f32[1,2]{1,0:T(1,128)S(1)}, u32[]{:S(2)}, u32[]{:S(2)}) collective-permute-start(f32[1,2]{1,0:T(1,128)S(1)} %bitcast.94), channel_id=1, source_target_pairs={{0,1},{1,0},{2,3},{3,2},{4,5},{5,4},{6,7},{7,6},{8,9},{9,8},{10,11... | collective-permute-start | bytes 32 | tf_op jit(solution)/shard_map/ppermute | solution.py:47
  45.3 3.6 %collective-permute-start.5 = (f32[1,2]{1,0:T(1,128)S(1)}, f32[1,2]{1,0:T(1,128)S(1)}, u32[]{:S(2)}, u32[]{:S(2)}) collective-permute-start(f32[1,2]{1,0:T(1,128)S(1)} %bitcast_add_fusion.2), channel_id=1, source_target_pairs={{0,2},{1,3},{2,0},{3,1},{4,6},{5,7},{6,4},{7,5},{8,10},{9,11},{10,... | collective-permute-start | bytes 32 | tf_op jit(solution)/shard_map/ppermute | solution.py:47
  48.9 4.5 %collective-permute-start.6 = (f32[1,2]{1,0:T(1,128)S(1)}, f32[1,2]{1,0:T(1,128)S(1)}, u32[]{:S(2)}, u32[]{:S(2)}) collective-permute-start(f32[1,2]{1,0:T(1,128)S(1)} %add.229), channel_id=1, source_target_pairs={{0,4},{1,5},{2,6},{3,7},{4,0},{5,1},{6,2},{7,3},{8,12},{9,13},{10,... | collective-permute-start | bytes 32 | tf_op jit(solution)/shard_map/ppermute | solution.py:47
  64.2 2.1 %collective-permute-start.7 = (f32[1,3]{1,0:T(1,128)S(1)}, f32[1,3]{1,0:T(1,128)S(1)}, u32[]{:S(2)}, u32[]{:S(2)}) collective-permute-start(f32[1,3]{1,0:T(1,128)S(1)} %bitcast.95), channel_id=1, source_target_pairs={{0,1},{1,0},{2,3},{3,2},{4,5},{5,4},{6,7},{7,6},{8,9},{9,8},{10,11... | collective-permute-start | bytes 44 | tf_op jit(solution)/shard_map/ppermute | solution.py:47
  66.3 3.6 %collective-permute-start.8 = (f32[1,3]{1,0:T(1,128)S(1)}, f32[1,3]{1,0:T(1,128)S(1)}, u32[]{:S(2)}, u32[]{:S(2)}) collective-permute-start(f32[1,3]{1,0:T(1,128)S(1)} %bitcast_add_fusion.1), channel_id=1, source_target_pairs={{0,2},{1,3},{2,0},{3,1},{4,6},{5,7},{6,4},{7,5},{8,10},{9,11},{10,... | collective-permute-start | bytes 44 | tf_op jit(solution)/shard_map/ppermute | solution.py:47
  70.0 4.5 %collective-permute-start.9 = (f32[1,3]{1,0:T(1,128)S(1)}, f32[1,3]{1,0:T(1,128)S(1)}, u32[]{:S(2)}, u32[]{:S(2)}) collective-permute-start(f32[1,3]{1,0:T(1,128)S(1)} %add.245), channel_id=1, source_target_pairs={{0,4},{1,5},{2,6},{3,7},{4,0},{5,1},{6,2},{7,3},{8,12},{9,13},{10,... | collective-permute-start | bytes 44 | tf_op jit(solution)/shard_map/ppermute | solution.py:47
  80.0 1.2 collective-permute-start.10
  81.2 3.6 %collective-permute-start.11 = (f32[1,3]{1,0:T(1,128)S(1)}, f32[1,3]{1,0:T(1,128)S(1)}, u32[]{:S(2)}, u32[]{:S(2)}) collective-permute-start(f32[1,3]{1,0:T(1,128)S(1)} %bitcast_add_fusion), channel_id=1, source_target_pairs={{0,2},{1,3},{2,0},{3,1},{4,6},{5,7},{6,4},{7,5},{8,10},{9,11},{10,... | collective-permute-start | bytes 44 | tf_op jit(solution)/shard_map/ppermute | solution.py:47
  84.7 4.5 %collective-permute-start.12 = (f32[1,3]{1,0:T(1,128)S(1)}, f32[1,3]{1,0:T(1,128)S(1)}, u32[]{:S(2)}, u32[]{:S(2)}) collective-permute-start(f32[1,3]{1,0:T(1,128)S(1)} %add.261), channel_id=1, source_target_pairs={{0,4},{1,5},{2,6},{3,7},{4,0},{5,1},{6,2},{7,3},{8,12},{9,13},{10,... | collective-permute-start | bytes 44 | tf_op jit(solution)/shard_map/ppermute | solution.py:47
  94.3 22.9 %all-to-all-start.1 = ((f32[1,16,8,2048]{3,2,0,1:T(8,128)}), f32[1,16,8,2048]{3,2,0,1:T(8,128)S(1)}, u32[]{:S(2)}, u32[]{:S(2)}) async-start(f32[1,16,8,2048]{3,2,0,1:T(8,128)} %copy.15), calls=%async_computation.1 | async-start | bytes 2097152 | tf_op jit(solution)/shard_map/all_to_all | solution.py:137
  99.0 1.2 %collective-permute-start.13 = (f32[4,7]{1,0:T(4,128)S(1)}, f32[4,7]{1,0:T(4,128)S(1)}, u32[]{:S(2)}, u32[]{:S(2)}) collective-permute-start(f32[4,7]{1,0:T(4,128)S(1)} %dynamic_update_slice.5), channel_id=1, source_target_pairs={{0,1},{1,0},{2,3},{3,2},{4,5},{5,4},{6,7},{7,6},{8,9},{9,8},{10,11... | collective-permute-start | bytes 344 | tf_op jit(solution)/shard_map/ppermute | solution.py:47
  101.0 3.6 %collective-permute-start.14 = (f32[4,7]{1,0:T(4,128)S(1)}, f32[4,7]{1,0:T(4,128)S(1)}, u32[]{:S(2)}, u32[]{:S(2)}) collective-permute-start(f32[4,7]{1,0:T(4,128)S(1)} %add.265), channel_id=1, source_target_pairs={{0,2},{1,3},{2,0},{3,1},{4,6},{5,7},{6,4},{7,5},{8,10},{9,11},{10,... | collective-permute-start | bytes 344 | tf_op jit(solution)/shard_map/ppermute | solution.py:47
  104.6 4.5 %collective-permute-start.15 = (f32[4,7]{1,0:T(4,128)S(1)}, f32[4,7]{1,0:T(4,128)S(1)}, u32[]{:S(2)}, u32[]{:S(2)}) collective-permute-start(f32[4,7]{1,0:T(4,128)S(1)} %add.266), channel_id=1, source_target_pairs={{0,4},{1,5},{2,6},{3,7},{4,0},{5,1},{6,2},{7,3},{8,12},{9,13},{10,... | collective-permute-start | bytes 344 | tf_op jit(solution)/shard_map/ppermute | solution.py:47
  109.1 3.6 %collective-permute-start.16 = (f32[4,7]{1,0:T(4,128)S(1)}, f32[4,7]{1,0:T(4,128)S(1)}, u32[]{:S(2)}, u32[]{:S(2)}) collective-permute-start(f32[4,7]{1,0:T(4,128)S(1)} %add.267), channel_id=1, source_target_pairs={{0,8},{8,0},{16,24},{24,16},{1,9},{9,1},{17,25},{25,17},{2,10},{10... | collective-permute-start | bytes 344 | tf_op jit(solution)/shard_map/ppermute | solution.py:47
  112.7 3.6 %collective-permute-start.17 = (f32[4,7]{1,0:T(4,128)S(1)}, f32[4,7]{1,0:T(4,128)S(1)}, u32[]{:S(2)}, u32[]{:S(2)}) collective-permute-start(f32[4,7]{1,0:T(4,128)S(1)} %add.268), channel_id=1, source_target_pairs={{0,16},{8,24},{16,0},{24,8},{1,17},{9,25},{17,1},{25,9},{2,18},{10... | collective-permute-start | bytes 344 | tf_op jit(solution)/shard_map/ppermute | solution.py:47
  116.3 2.2 %copy-start.3 = (f32[4,7]{1,0:T(4,128)}, f32[4,7]{1,0:T(4,128)S(1)}, u32[]{:S(2)}) copy-start(f32[4,7]{1,0:T(4,128)S(1)} %add.269) | copy-start | bytes 340

commit v7 on v6

--- a/solution.py
+++ b/solution.py
@@ -38,15 +38,27 @@
     return jnp.sum(g, axis=0)
 
 
-def butterfly_sum(v, axis):
+def butterfly_sum(v, axis, work=()):
     n = lax.axis_size(axis)
+    carry = None
     if n & (n - 1):
-        return lax.psum(v, axis)
+        for stage in work:
+            carry = stage(carry)
+        return lax.psum(v, axis), carry
     s = 1
+    r = 0
     while s < n:
-        v = v + lax.ppermute(v, axis, [(i, i ^ s) for i in range(n)])
+        got = lax.ppermute(v, axis, [(i, i ^ s) for i in range(n)])
+        if r < len(work):
+            carry = work[r](carry)
+            v, carry = lax.optimization_barrier((v + got, carry))
+        else:
+            v = v + got
         s *= 2
-    return v
+        r += 1
+    for stage in work[r:]:
+        carry = stage(carry)
+    return v, carry
 
 
 def halo_rows(block, width):
@@ -72,11 +84,17 @@
     variances = jnp.diagonal(trait_covariance)
     z = field_ext * variances[None, :, None, None]
 
+    def apply_half(x, off, mix):
+        r = x.shape[2]
+        if mix:
+            x = jnp.einsum("ts,psrc->ptrc", trait_covariance, x, precision=lax.Precision.HIGHEST)
+        return land_ext[off + 1 : off + r - 1] * nine_valid(x, kappa_ext[off + 1 : off + r - 1])
+
     def apply_a(x, off):
-        r = x.shape[2]
-        mixed = jnp.einsum("ts,psrc->ptrc", trait_covariance, x, precision=lax.Precision.HIGH)
-        first = land_ext[off + 1 : off + r - 1] * nine_valid(mixed, kappa_ext[off + 1 : off + r - 1])
-        return land_ext[off + 2 : off + r - 2] * nine_valid(first, kappa_ext[off + 2 : off + r - 2])
+        return apply_half(apply_half(x, off, True), off + 1, False)
+
+    def a_stages(x, off):
+        return (lambda _: apply_half(x, off, True), lambda first: apply_half(first, off + 1, False))
 
     def own(x, off):
         return x[:, :, h - off : h - off + rows]
@@ -87,14 +105,13 @@
     def crop(x, k):
         return x[:, :, k : x.shape[2] - k]
 
-    def reduce_tile(pairs, off):
+    def reduce_tile(pairs, off, work=()):
         prods = jnp.stack([own(a, off) * own(b, off) for a, b in pairs], axis=-1)
-        return butterfly_sum(jnp.sum(prods, axis=(1, 2, 3)), "tile")
+        return butterfly_sum(jnp.sum(prods, axis=(1, 2, 3)), "tile", work)
 
     az = apply_a(z, 0)
     z2 = crop(z, 2)
-    sums = reduce_tile([(z2, z2), (az, z2)], 2)
-    aaz = apply_a(az, 2)
+    sums, aaz = reduce_tile([(z2, z2), (az, z2)], 2, a_stages(az, 2))
     norm = jnp.sqrt(sums[:, 0] + epsilon)
     alpha = sums[:, 1] / (norm * norm)
     q = z2 / norm[:, None, None, None]
@@ -109,10 +126,8 @@
     betas = []
     iters = 3
     for step in range(1, iters):
-        sums = reduce_tile([(w, w), (aw, w), (q, w)], off)
         last_step = step == iters - 1
-        if not last_step:
-            aaw = apply_a(aw, off)
+        sums, aaw = reduce_tile([(w, w), (aw, w), (q, w)], off, () if last_step else a_stages(aw, off))
         beta = jnp.sqrt(sums[:, 0] + epsilon)
         alpha = sums[:, 1] / (beta * beta) - sums[:, 2]
         q_next = w / beta[:, None, None, None]
@@ -146,7 +161,7 @@
         mine,
         (lax.axis_index("trait") * probes_local, 0),
     )
-    scalars = butterfly_sum(butterfly_sum(spread, "tile"), "trait")
+    scalars = butterfly_sum(butterfly_sum(spread, "tile")[0], "trait")[0]
     beta = jnp.sqrt(scalars[:, 2 * iters - 1] + epsilon)
     norm_all = scalars[:, 2 * iters]
     last = (w_back / beta[:, None, None, None]) * norm_all[:, None, None, None]

time: 119 us -> 118 us (level)
  starting transfers between devices: 43.1 us -> 39.1 us
  matrix products: 3.44 us -> 6.47 us
    mul x4 -> x6, other arithmetic: 14 us -> 18.2 us  [apply_half(): land_ext[off + 1:off + r - 1]]
    ppermute x14, starting transfers between devices: 26.8 us -> 22.7 us  [butterfly_sum(): got = lax.ppermute(v, axis, [(i, i ^ s) for i in range(n)])]
    dot_general x3, matrix products: 3.44 us -> 6.47 us  [apply_half(): jnp.einsum('ts,psrc->ptrc', trait_covariance, x, precision=lax.Precision....]
    sub x1, other arithmetic: 3.16 us -> 0.22 us  [shards(): aaz / norm[:, None, None, None] - alpha[:, None, None, None] * crop(aq, 2)]
    another operation x4, other arithmetic: 2.84 us -> 1.35 us  [reduce_tile(): prods = jnp.stack([own(a, off) * own(b, off) for a, b in pairs], axis=-1)]
  transfers between devices with their start and end apart: 20 -> 20, of which waited for: 15 -> 14; matrix products, arithmetic and copies ran while one was open for 8% -> 11% of each run, Pallas kernels for 0% -> 0%
where the time goes in v7:
time: 118 us
  starting transfers between devices  39.1 us (33%)
  other arithmetic  32.7 us (28%)
  waiting for transfers between devices  27.8 us (24%)
  matrix products  6.47 us (5%)
  between operations  6.37 us (5%)
  local copies, waits for them, and re-layouts  5.39 us (5%)
    ppermute x14, starting transfers between devices, butterfly_sum(): got = lax.ppermute(v, axis, [(i, i ^ s) for i in range(n)])  22.7 us
    ppermute x14, waiting for transfers between devices, butterfly_sum(): got = lax.ppermute(v, axis, [(i, i ^ s) for i in range(n)])  21.4 us
    mul x6, other arithmetic, apply_half(): land_ext[off + 1:off + r - 1]  18.2 us
    dot_general x3, matrix products, apply_half(): jnp.einsum('ts,psrc->ptrc', trait_covariance, x, precision=lax.Precision....  6.47 us
    all_to_all x1, starting transfers between devices, shards(): lax.all_to_all(signed, 'trait', split_axis=0, concat_axis=1, tiled=True)  5.19 us
    ppermute x2, waiting for transfers between devices, halo_rows(): lax.ppermute(lax.slice_in_dim(block, 0, width, axis=dim), 'tile', backward)  4.76 us
    ppermute x2, starting transfers between devices, halo_rows(): lax.ppermute(lax.slice_in_dim(block, rows - width, rows, axis=dim), 'tile...  4.75 us
    sub x1, other arithmetic, shards(): w = aq - alpha[:, None, None, None] * q  4.13 us
  transfers between devices with their start and end apart: 20, of which 14 were waited for; matrix products, arithmetic and copies ran while one was open for 11% of the time, Pallas kernels for 0%

profile of v7, /device:TPU:0, one launch (start us, length us, event | category | flops | bytes accessed | tf_op | source)
XLA Modules:
  0.0 117.8 jit_solution(16266666386477527329)
XLA Ops:
  0.7 2.2 %multiply_convert_fusion = bf16[4,4,8,2048]{3,2,1,0:T(8,128)(2,1)} fusion(s32[4,4,8,2048]{3,2,1,0:T(8,128)} %param.4, s32[8,2048]{1,0:T(8,128)} %param.5), kind=kLoop, calls=%fused_computation.152 | loop fusion | flops 1048576 | bytes 1638400 | tf_op jit(solution)/shard_map/convert_element_type | solution.py:79
  2.9 5.2 %all-to-all-start = ((bf16[4,4,8,2048]{3,2,1,0:T(8,128)(2,1)}), bf16[4,4,8,2048]{3,2,1,0:T(8,128)(2,1)S(1)}, u32[]{:S(2)}, u32[]{:S(2)}) async-start(bf16[4,4,8,2048]{3,2,1,0:T(8,128)(2,1)} %multiply_convert_fusion), calls=%async_computation | async-start | bytes 1048576 | tf_op jit(solution)/shard_map/all_to_all | solution.py:80
  11.6 2.8 %collective-permute-done.3 = f32[6,2048]{1,0:T(8,128)S(1)} collective-permute-done((f32[6,2048]{1,0:T(8,128)S(1)}, f32[6,2048]{1,0:T(8,128)S(1)}, u32[]{:S(2)}, u32[]{:S(2)}) %collective-permute-start.3) | collective-permute-done | bytes 49184 | tf_op jit(solution)/shard_map/ppermute | solution.py:72
  14.5 1.6 %all-to-all-done = bf16[4,4,8,2048]{3,2,1,0:T(8,128)(2,1)S(1)} async-done(((bf16[4,4,8,2048]{3,2,1,0:T(8,128)(2,1)}), bf16[4,4,8,2048]{3,2,1,0:T(8,128)(2,1)S(1)}, u32[]{:S(2)}, u32[]{:S(2)}) %all-to-all-start) | async-done | bytes 524320 | tf_op jit(solution)/shard_map/all_to_all | solution.py:80
  16.5 3.3 %collective-permute-start = (bf16[1,16,6,2048]{3,1,2,0:T(8,128)(2,1)S(1)}, bf16[1,16,6,2048]{3,1,2,0:T(8,128)(2,1)S(1)}, u32[]{:S(2)}, u32[]{:S(2)}) collective-permute-start(bf16[1,16,6,2048]{3,1,2,0:T(8,128)(2,1)S(1)} %get-tuple-element.36), channel_id=1, source_target_pairs={{0,1},{1,2},{2,3},{3,4},{4,5},{5,6},{6,7},{8,9},{9,10},{10,11},{11... | collective-permute-start | bytes 1179656 | tf_op jit(solution)/shard_map/ppermute | solution.py:71
  21.4 2.0 %collective-permute-done.1 = bf16[1,16,6,2048]{3,1,2,0:T(8,128)(2,1)S(1)} collective-permute-done((bf16[1,16,6,2048]{3,1,2,0:T(8,128)(2,1)S(1)}, bf16[1,16,6,2048]{3,1,2,0:T(8,128)(2,1)S(1)}, u32[]{:S(2)}, u32[]{:S(2)}) %collective-permute-start.1) | collective-permute-done | bytes 393248 | tf_op jit(solution)/shard_map/ppermute | solution.py:72
  23.8 3.0 %convolution_bitcast_fusion = f32[1,16,20,2048]{3,1,2,0:T(8,128)S(1)} fusion(bf16[16,6,2048]{2,0,1:T(8,128)(2,1)S(1)} %bitcast.85, bf16[16,8,2048]{2,0,1:T(8,128)(2,1)S(1)} %copy.14, bf16[16,6,2048]{2,0,1:T(8,128)(2,1)S(1)} %bitcast.84, f32[16]{0:T(128)S(1)} %gather_fusion, f32[16,16]{1,0:T(8,128)S(1)} %copy-done), kind=kOutput, calls=%fused_computation.3 | convolution fusion | flops 128450560 | bytes 3933248 | tf_op jit(solution)/shard_map/ts,psrc->ptrc/dot_general | solution.py:90
  26.8 4.6 %fusion.7 = f32[1,16,18,2048]{3,1,2,0:T(8,128)S(1)} fusion(f32[1,16,20,2048]{3,1,2,0:T(8,128)S(1)} %convolution_bitcast_fusion, f32[18,2048]{1,0:T(8,128)S(1)} %slice_add_fusion.4, f32[18,2048]{1,0:T(8,128)S(1)} %bitcast.88), kind=kLoop, calls=%fused_computation.19 | loop fusion | flops 7667712 | bytes 12451840 | tf_op jit(solution)/shard_map/mul | solution.py:91
  31.4 3.8 %fusion.18 = f32[1,16,16,2048]{3,1,2,0:T(8,128)S(1)} fusion(f32[1,16,18,2048]{3,1,2,0:T(8,128)S(1)} %fusion.7, f32[16,2048]{1,0:T(8,128)S(1)} %slice_add_fusion.8, f32[16,2048]{1,0:T(8,128)S(1)} %bitcast.86), kind=kLoop, calls=%fused_computation.38 | loop fusion | flops 6815744 | bytes 11010048 | tf_op jit(solution)/shard_map/mul | solution.py:91
  35.3 2.0 %convolution_bitcast_fusion.1 = f32[1,16,16,2048]{3,1,2,0:T(8,128)S(1)} fusion(f32[1,16,16,2048]{3,1,2,0:T(8,128)S(1)} %fusion.18, f32[16,16]{1,0:T(8,128)S(1)} %copy-done), kind=kOutput, calls=%fused_computation.4 | convolution fusion | flops 100663296 | bytes 4195328 | tf_op jit(solution)/shard_map/ts,psrc->ptrc/dot_general | solution.py:90
  38.2 5.8 %collective-permute-start.4 = (f32[1,2]{1,0:T(1,128)S(1)}, f32[1,2]{1,0:T(1,128)S(1)}, u32[]{:S(2)}, u32[]{:S(2)}) collective-permute-start(f32[1,2]{1,0:T(1,128)S(1)} %bitcast.94), channel_id=1, source_target_pairs={{0,1},{1,0},{2,3},{3,2},{4,5},{5,4},{6,7},{7,6},{8,9},{9,8},{10,11... | collective-permute-start | bytes 32 | tf_op jit(solution)/shard_map/ppermute | solution.py:51
  44.2 3.4 %fusion.30 = f32[1,16,14,2048]{3,1,2,0:T(8,128)S(1)} fusion(f32[1,16,16,2048]{3,1,2,0:T(8,128)S(1)} %convolution_bitcast_fusion.1, f32[14,2048]{1,0:T(8,128)S(1)} %slice_add_fusion.7, f32[14,2048]{1,0:T(8,128)S(1)} %bitcast.91), kind=kLoop, calls=%fused_computation.61 | loop fusion | flops 5963776 | bytes 9699328 | tf_op jit(solution)/shard_map/mul | solution.py:91
  47.7 1.6 %collective-permute-start.5 = (f32[1,2]{1,0:T(1,128)S(1)}, f32[1,2]{1,0:T(1,128)S(1)}, u32[]{:S(2)}, u32[]{:S(2)}) collective-permute-start(f32[1,2]{1,0:T(1,128)S(1)} %bitcast_add_fusion.2), channel_id=1, source_target_pairs={{0,2},{1,3},{2,0},{3,1},{4,6},{5,7},{6,4},{7,5},{8,10},{9,11},{10,... | collective-permute-start | bytes 32 | tf_op jit(solution)/shard_map/ppermute | solution.py:51
  49.3 2.5 %fusion.41 = f32[1,16,12,2048]{3,1,2,0:T(8,128)S(1)} fusion(f32[1,16,14,2048]{3,1,2,0:T(8,128)S(1)} %fusion.30, f32[12,2048]{1,0:T(8,128)S(1)} %slice_add_fusion.6, f32[12,2048]{1,0:T(8,128)S(1)} %bitcast.89), kind=kLoop, calls=%fused_computation.80 | loop fusion | flops 5111808 | bytes 8388608 | tf_op jit(solution)/shard_map/mul | solution.py:91
  51.9 2.1 %collective-permute-start.6 = (f32[1,2]{1,0:T(1,128)S(1)}, f32[1,2]{1,0:T(1,128)S(1)}, u32[]{:S(2)}, u32[]{:S(2)}) collective-permute-start(f32[1,2]{1,0:T(1,128)S(1)} %add.235), channel_id=1, source_target_pairs={{0,4},{1,5},{2,6},{3,7},{4,0},{5,1},{6,2},{7,3},{8,12},{9,13},{10,... | collective-permute-start | bytes 32 | tf_op jit(solution)/shard_map/ppermute | solution.py:51
  53.9 2.5 %collective-permute-done.6 = f32[1,2]{1,0:T(1,128)S(1)} collective-permute-done((f32[1,2]{1,0:T(1,128)S(1)}, f32[1,2]{1,0:T(1,128)S(1)}, u32[]{:S(2)}, u32[]{:S(2)}) %collective-permute-start.6) | collective-permute-done | bytes 40 | tf_op jit(solution)/shard_map/ppermute | solution.py:51
  58.3 4.1 %multiply_subtract_fusion = (f32[1,16,16,2048]{3,1,2,0:T(8,128)S(1)}, f32[1,16,16,2048]{3,1,2,0:T(8,128)S(1)}, f32[1,16,16,2048]{3,1,2,0:T(8,128)S(1)}) fusion(f32[]{:T(128)} %bitcast.17, f32[]{:T(128)} %bitcast.16, f32[1,16,20,2048]{3,1,2,0:T(8,128)S(1)} %broadcast_multiply_fusion, f32[1,16,18,2048]{3,1,2,0:T(8,128)S(1)} %fusion.7, ...), kind=kLoop, calls=%fused_computation.49 | loop fusion | flops 8912896 | bytes 17301512 | tf_op jit(solution)/shard_map/sub | solution.py:119
  65.1 2.1 %fusion.53 = f32[1,16,10,2048]{3,1,2,0:T(8,128)S(1)} fusion(f32[1,16,12,2048]{3,1,2,0:T(8,128)S(1)} %convolution_bitcast_fusion.2, f32[10,2048]{1,0:T(8,128)S(1)} %slice_add_fusion.5, f32[10,2048]{1,0:T(8,128)S(1)} %bitcast.90), kind=kLoop, calls=%fused_computation.100 | loop fusion | flops 4259840 | bytes 7077888 | tf_op jit(solution)/shard_map/mul | solution.py:91
  68.2 1.7 %fusion.70 = f32[1,16,8,2048]{3,1,2,0:T(8,128)S(1)} fusion(f32[1,16,10,2048]{3,1,2,0:T(8,128)S(1)} %fusion.53, f32[8,2048]{1,0:T(8,128)S(1)} %broadcast_add_fusion, f32[8,2048]{1,0:T(8,128)S(1)} %bitcast.92), kind=kLoop, calls=%fused_computation.127 | loop fusion | flops 3407872 | bytes 5636096 | tf_op jit(solution)/shard_map/mul | solution.py:91
  70.8 2.0 %collective-permute-start.9 = (f32[1,3]{1,0:T(1,128)S(1)}, f32[1,3]{1,0:T(1,128)S(1)}, u32[]{:S(2)}, u32[]{:S(2)}) collective-permute-start(f32[1,3]{1,0:T(1,128)S(1)} %add.251), channel_id=1, source_target_pairs={{0,4},{1,5},{2,6},{3,7},{4,0},{5,1},{6,2},{7,3},{8,12},{9,13},{10,... | collective-permute-start | bytes 44 | tf_op jit(solution)/shard_map/ppermute | solution.py:51
  72.8 2.5 %collective-permute-done.9 = f32[1,3]{1,0:T(1,128)S(1)} collective-permute-done((f32[1,3]{1,0:T(1,128)S(1)}, f32[1,3]{1,0:T(1,128)S(1)}, u32[]{:S(2)}, u32[]{:S(2)}) %collective-permute-start.9) | collective-permute-done | bytes 44 | tf_op jit(solution)/shard_map/ppermute | solution.py:51
  81.5 2.6 %collective-permute-done.11 = f32[1,3]{1,0:T(1,128)S(1)} collective-permute-done((f32[1,3]{1,0:T(1,128)S(1)}, f32[1,3]{1,0:T(1,128)S(1)}, u32[]{:S(2)}, u32[]{:S(2)}) %collective-permute-start.11) | collective-permute-done | bytes 44 | tf_op jit(solution)/shard_map/ppermute | solution.py:51
  84.1 2.0 %collective-permute-start.12 = (f32[1,3]{1,0:T(1,128)S(1)}, f32[1,3]{1,0:T(1,128)S(1)}, u32[]{:S(2)}, u32[]{:S(2)}) collective-permute-start(f32[1,3]{1,0:T(1,128)S(1)} %add.261), channel_id=1, source_target_pairs={{0,4},{1,5},{2,6},{3,7},{4,0},{5,1},{6,2},{7,3},{8,12},{9,13},{10,... | collective-permute-start | bytes 44 | tf_op jit(solution)/shard_map/ppermute | solution.py:51
  86.1 2.5 %collective-permute-done.12 = f32[1,3]{1,0:T(1,128)S(1)} collective-permute-done((f32[1,3]{1,0:T(1,128)S(1)}, f32[1,3]{1,0:T(1,128)S(1)}, u32[]{:S(2)}, u32[]{:S(2)}) %collective-permute-start.12) | collective-permute-done | bytes 44 | tf_op jit(solution)/shard_map/ppermute | solution.py:51
  92.1 1.6 %copy.15 = f32[1,16,8,2048]{3,2,0,1:T(8,128)} copy(f32[1,16,8,2048]{3,1,2,0:T(8,128)S(1)} %get-tuple-element.22) | data formatting | bytes 2097152 | tf_op jit(solution)/shard_map/sub | solution.py:134
  93.6 3.9 %all-to-all-start.1 = ((f32[1,16,8,2048]{3,2,0,1:T(8,128)}), f32[1,16,8,2048]{3,2,0,1:T(8,128)S(1)}, u32[]{:S(2)}, u32[]{:S(2)}) async-start(f32[1,16,8,2048]{3,2,0,1:T(8,128)} %copy.15), calls=%async_computation.1 | async-start | bytes 2097152 | tf_op jit(solution)/shard_map/all_to_all | solution.py:152
  101.3 2.6 %collective-permute-done.14 = f32[4,7]{1,0:T(4,128)S(1)} collective-permute-done((f32[4,7]{1,0:T(4,128)S(1)}, f32[4,7]{1,0:T(4,128)S(1)}, u32[]{:S(2)}, u32[]{:S(2)}) %collective-permute-start.14) | collective-permute-done | bytes 144 | tf_op jit(solution)/shard_map/ppermute | solution.py:51
  104.0 2.0 %collective-permute-start.15 = (f32[4,7]{1,0:T(4,128)S(1)}, f32[4,7]{1,0:T(4,128)S(1)}, u32[]{:S(2)}, u32[]{:S(2)}) collective-permute-start(f32[4,7]{1,0:T(4,128)S(1)} %add.266), channel_id=1, source_target_pairs={{0,4},{1,5},{2,6},{3,7},{4,0},{5,1},{6,2},{7,3},{8,12},{9,13},{10,... | collective-permute-start | bytes 344 | tf_op jit(solution)/shard_map/ppermute | solution.py:51
  105.9 2.5 %collective-permute-done.15 = f32[4,7]{1,0:T(4,128)S(1)} collective-permute-done((f32[4,7]{1,0:T(4,128)S(1)}, f32[4,7]{1,0:T(4,128)S(1)}, u32[]{:S(2)}, u32[]{:S(2)}) %collective-permute-start.15) | collective-permute-done | bytes 144 | tf_op jit(solution)/shard_map/ppermute | solution.py:51
  108.4 2.0 %collective-permute-start.16 = (f32[4,7]{1,0:T(4,128)S(1)}, f32[4,7]{1,0:T(4,128)S(1)}, u32[]{:S(2)}, u32[]{:S(2)}) collective-permute-start(f32[4,7]{1,0:T(4,128)S(1)} %add.267), channel_id=1, source_target_pairs={{0,8},{8,0},{16,24},{24,16},{1,9},{9,1},{17,25},{25,17},{2,10},{10... | collective-permute-start | bytes 344 | tf_op jit(solution)/shard_map/ppermute | solution.py:51
  110.5 1.6 %collective-permute-done.16 = f32[4,7]{1,0:T(4,128)S(1)} collective-permute-done((f32[4,7]{1,0:T(4,128)S(1)}, f32[4,7]{1,0:T(4,128)S(1)}, u32[]{:S(2)}, u32[]{:S(2)}) %collective-permute-start.16) | collective-permute-done | bytes 144 | tf_op jit(solution)/shard_map/ppermute | solution.py:51
  112.0 2.0 %collective-permute-start.17 = (f32[4,7]{1,0:T(4,128)S(1)}, f32[4,7]{1,0:T(4,128)S(1)}, u32[]{:S(2)}, u32[]{:S(2)}) collective-permute-start(f32[4,7]{1,0:T(4,128)S(1)} %add.268), channel_id=1, source_target_pairs={{0,16},{8,24},{16,0},{24,8},{1,17},{9,25},{17,1},{25,9},{2,18},{10... | collective-permute-start | bytes 344 | tf_op jit(solution)/shard_map/ppermute | solution.py:51
  (98 shorter events, 25.5 us)
Async XLA Ops:
  0.6 10.3 %copy-start = (f32[16,16]{1,0:T(8,128)S(1)}, f32[16,16]{1,0:T(8,128)}, u32[]{:S(2)}) copy-start(f32[16,16]{1,0:T(8,128)} %param.7) | copy-start | bytes 3076
  0.6 7.4 %copy-start.2 = (f32[8,2048]{1,0:T(8,128)S(1)}, f32[8,2048]{1,0:T(8,128)}, u32[]{:S(2)}) copy-start(f32[8,2048]{1,0:T(8,128)} %param.6) | copy-start | bytes 196612
  2.9 13.2 %all-to-all-start = ((bf16[4,4,8,2048]{3,2,1,0:T(8,128)(2,1)}), bf16[4,4,8,2048]{3,2,1,0:T(8,128)(2,1)S(1)}, u32[]{:S(2)}, u32[]{:S(2)}) async-start(bf16[4,4,8,2048]{3,2,1,0:T(8,128)(2,1)} %multiply_convert_fusion), calls=%async_computation | async-start | bytes 1048576 | tf_op jit(solution)/shard_map/all_to_all | solution.py:80
  8.1 3.5 %collective-permute-start.2 = (f32[6,2048]{1,0:T(8,128)S(1)}, f32[6,2048]{1,0:T(8,128)S(1)}, u32[]{:S(2)}, u32[]{:S(2)}) collective-permute-start(f32[6,2048]{1,0:T(8,128)S(1)} %get-tuple-element.38), channel_id=1, source_target_pairs={{0,1},{1,2},{2,3},{3,4},{4,5},{5,6},{6,7},{8,9},{9,10},{10,11},{11... | collective-permute-start | bytes 147464 | tf_op jit(solution)/shard_map/ppermute | solution.py:71
  9.6 4.8 %collective-permute-start.3 = (f32[6,2048]{1,0:T(8,128)S(1)}, f32[6,2048]{1,0:T(8,128)S(1)}, u32[]{:S(2)}, u32[]{:S(2)}) collective-permute-start(f32[6,2048]{1,0:T(8,128)S(1)} %get-tuple-element.39), channel_id=1, source_target_pairs={{1,0},{2,1},{3,2},{4,3},{5,4},{6,5},{7,6},{9,8},{10,9},{11,10},{12... | collective-permute-start | bytes 147464 | tf_op jit(solution)/shard_map/ppermute | solution.py:72
  16.5 4.9 %collective-permute-start = (bf16[1,16,6,2048]{3,1,2,0:T(8,128)(2,1)S(1)}, bf16[1,16,6,2048]{3,1,2,0:T(8,128)(2,1)S(1)}, u32[]{:S(2)}, u32[]{:S(2)}) collective-permute-start(bf16[1,16,6,2048]{3,1,2,0:T(8,128)(2,1)S(1)} %get-tuple-element.36), channel_id=1, source_target_pairs={{0,1},{1,2},{2,3},{3,4},{4,5},{5,6},{6,7},{8,9},{9,10},{10,11},{11... | collective-permute-start | bytes 1179656 | tf_op jit(solution)/shard_map/ppermute | solution.py:71
  19.8 3.6 %collective-permute-start.1 = (bf16[1,16,6,2048]{3,1,2,0:T(8,128)(2,1)S(1)}, bf16[1,16,6,2048]{3,1,2,0:T(8,128)(2,1)S(1)}, u32[]{:S(2)}, u32[]{:S(2)}) collective-permute-start(bf16[1,16,6,2048]{3,1,2,0:T(8,128)(2,1)S(1)} %get-tuple-element.37), channel_id=1, source_target_pairs={{1,0},{2,1},{3,2},{4,3},{5,4},{6,5},{7,6},{9,8},{10,9},{11,10},{12... | collective-permute-start | bytes 1179656 | tf_op jit(solution)/shard_map/ppermute | solution.py:72
  23.7 3.2 %copy-start.1 = (f32[1,1,20,2048]{3,1,2,0:T(1,128)}, f32[1,1,20,2048]{3,1,2,0:T(1,128)S(1)}, u32[]{:S(2)}) copy-start(f32[1,1,20,2048]{3,1,2,0:T(1,128)S(1)} %slice_multiply_fusion.9) | copy-start | bytes 491524
  37.8 6.2 %slice-start = ((f32[1,1,20,2048]{3,1,2,0:T(1,128)}), f32[1,1,14,2048]{3,1,2,0:T(1,128)S(1)}, s32[]{:S(2)}) async-start(f32[1,1,20,2048]{3,1,2,0:T(1,128)} %copy-done.1), calls=%async_computation.2 | async-start | bytes 229376 | tf_op jit(solution)/shard_map/slice | solution.py:91
  37.8 6.3 %slice-start.1 = ((f32[1,1,20,2048]{3,1,2,0:T(1,128)}), f32[1,1,12,2048]{3,1,2,0:T(1,128)S(1)}, s32[]{:S(2)}) async-start(f32[1,1,20,2048]{3,1,2,0:T(1,128)} %copy-done.1), calls=%async_computation.3 | async-start | bytes 196608 | tf_op jit(solution)/shard_map/slice | solution.py:91
  37.8 6.3 %slice-start.2 = ((f32[1,1,20,2048]{3,1,2,0:T(1,128)}), f32[1,1,10,2048]{3,1,2,0:T(1,128)S(1)}, s32[]{:S(2)}) async-start(f32[1,1,20,2048]{3,1,2,0:T(1,128)} %copy-done.1), calls=%async_computation.4 | async-start | bytes 163840 | tf_op jit(solution)/shard_map/slice | solution.py:91
  37.9 6.3 %slice-start.3 = ((f32[1,1,20,2048]{3,1,2,0:T(1,128)}), f32[1,1,8,2048]{3,1,2,0:T(1,128)S(1)}, s32[]{:S(2)}) async-start(f32[1,1,20,2048]{3,1,2,0:T(1,128)} %copy-done.1), calls=%async_computation.5 | async-start | bytes 131072 | tf_op jit(solution)/shard_map/slice | solution.py:91
  38.2 9.4 %collective-permute-start.4 = (f32[1,2]{1,0:T(1,128)S(1)}, f32[1,2]{1,0:T(1,128)S(1)}, u32[]{:S(2)}, u32[]{:S(2)}) collective-permute-start(f32[1,2]{1,0:T(1,128)S(1)} %bitcast.94), channel_id=1, source_target_pairs={{0,1},{1,0},{2,3},{3,2},{4,5},{5,4},{6,7},{7,6},{8,9},{9,8},{10,11... | collective-permute-start | bytes 32 | tf_op jit(solution)/shard_map/ppermute | solution.py:51
  47.7 4.2 %collective-permute-start.5 = (f32[1,2]{1,0:T(1,128)S(1)}, f32[1,2]{1,0:T(1,128)S(1)}, u32[]{:S(2)}, u32[]{:S(2)}) collective-permute-start(f32[1,2]{1,0:T(1,128)S(1)} %bitcast_add_fusion.2), channel_id=1, source_target_pairs={{0,2},{1,3},{2,0},{3,1},{4,6},{5,7},{6,4},{7,5},{8,10},{9,11},{10,... | collective-permute-start | bytes 32 | tf_op jit(solution)/shard_map/ppermute | solution.py:51
  51.9 4.5 %collective-permute-start.6 = (f32[1,2]{1,0:T(1,128)S(1)}, f32[1,2]{1,0:T(1,128)S(1)}, u32[]{:S(2)}, u32[]{:S(2)}) collective-permute-start(f32[1,2]{1,0:T(1,128)S(1)} %add.235), channel_id=1, source_target_pairs={{0,4},{1,5},{2,6},{3,7},{4,0},{5,1},{6,2},{7,3},{8,12},{9,13},{10,... | collective-permute-start | bytes 32 | tf_op jit(solution)/shard_map/ppermute | solution.py:51
  65.0 2.1 %collective-permute-start.7 = (f32[1,3]{1,0:T(1,128)S(1)}, f32[1,3]{1,0:T(1,128)S(1)}, u32[]{:S(2)}, u32[]{:S(2)}) collective-permute-start(f32[1,3]{1,0:T(1,128)S(1)} %bitcast.95), channel_id=1, source_target_pairs={{0,1},{1,0},{2,3},{3,2},{4,5},{5,4},{6,7},{7,6},{8,9},{9,8},{10,11... | collective-permute-start | bytes 44 | tf_op jit(solution)/shard_map/ppermute | solution.py:51
  67.2 3.6 %collective-permute-start.8 = (f32[1,3]{1,0:T(1,128)S(1)}, f32[1,3]{1,0:T(1,128)S(1)}, u32[]{:S(2)}, u32[]{:S(2)}) collective-permute-start(f32[1,3]{1,0:T(1,128)S(1)} %bitcast_add_fusion.1), channel_id=1, source_target_pairs={{0,2},{1,3},{2,0},{3,1},{4,6},{5,7},{6,4},{7,5},{8,10},{9,11},{10,... | collective-permute-start | bytes 44 | tf_op jit(solution)/shard_map/ppermute | solution.py:51
  70.8 4.5 %collective-permute-start.9 = (f32[1,3]{1,0:T(1,128)S(1)}, f32[1,3]{1,0:T(1,128)S(1)}, u32[]{:S(2)}, u32[]{:S(2)}) collective-permute-start(f32[1,3]{1,0:T(1,128)S(1)} %add.251), channel_id=1, source_target_pairs={{0,4},{1,5},{2,6},{3,7},{4,0},{5,1},{6,2},{7,3},{8,12},{9,13},{10,... | collective-permute-start | bytes 44 | tf_op jit(solution)/shard_map/ppermute | solution.py:51
  79.4 1.2 collective-permute-start.10
  80.6 3.6 %collective-permute-start.11 = (f32[1,3]{1,0:T(1,128)S(1)}, f32[1,3]{1,0:T(1,128)S(1)}, u32[]{:S(2)}, u32[]{:S(2)}) collective-permute-start(f32[1,3]{1,0:T(1,128)S(1)} %bitcast_add_fusion), channel_id=1, source_target_pairs={{0,2},{1,3},{2,0},{3,1},{4,6},{5,7},{6,4},{7,5},{8,10},{9,11},{10,... | collective-permute-start | bytes 44 | tf_op jit(solution)/shard_map/ppermute | solution.py:51
  84.1 4.5 %collective-permute-start.12 = (f32[1,3]{1,0:T(1,128)S(1)}, f32[1,3]{1,0:T(1,128)S(1)}, u32[]{:S(2)}, u32[]{:S(2)}) collective-permute-start(f32[1,3]{1,0:T(1,128)S(1)} %add.261), channel_id=1, source_target_pairs={{0,4},{1,5},{2,6},{3,7},{4,0},{5,1},{6,2},{7,3},{8,12},{9,13},{10,... | collective-permute-start | bytes 44 | tf_op jit(solution)/shard_map/ppermute | solution.py:51
  93.6 22.9 %all-to-all-start.1 = ((f32[1,16,8,2048]{3,2,0,1:T(8,128)}), f32[1,16,8,2048]{3,2,0,1:T(8,128)S(1)}, u32[]{:S(2)}, u32[]{:S(2)}) async-start(f32[1,16,8,2048]{3,2,0,1:T(8,128)} %copy.15), calls=%async_computation.1 | async-start | bytes 2097152 | tf_op jit(solution)/shard_map/all_to_all | solution.py:152
  98.3 1.2 %collective-permute-start.13 = (f32[4,7]{1,0:T(4,128)S(1)}, f32[4,7]{1,0:T(4,128)S(1)}, u32[]{:S(2)}, u32[]{:S(2)}) collective-permute-start(f32[4,7]{1,0:T(4,128)S(1)} %dynamic_update_slice.5), channel_id=1, source_target_pairs={{0,1},{1,0},{2,3},{3,2},{4,5},{5,4},{6,7},{7,6},{8,9},{9,8},{10,11... | collective-permute-start | bytes 344 | tf_op jit(solution)/shard_map/ppermute | solution.py:51
  100.3 3.6 %collective-permute-start.14 = (f32[4,7]{1,0:T(4,128)S(1)}, f32[4,7]{1,0:T(4,128)S(1)}, u32[]{:S(2)}, u32[]{:S(2)}) collective-permute-start(f32[4,7]{1,0:T(4,128)S(1)} %add.265), channel_id=1, source_target_pairs={{0,2},{1,3},{2,0},{3,1},{4,6},{5,7},{6,4},{7,5},{8,10},{9,11},{10,... | collective-permute-start | bytes 344 | tf_op jit(solution)/shard_map/ppermute | solution.py:51
  104.0 4.5 %collective-permute-start.15 = (f32[4,7]{1,0:T(4,128)S(1)}, f32[4,7]{1,0:T(4,128)S(1)}, u32[]{:S(2)}, u32[]{:S(2)}) collective-permute-start(f32[4,7]{1,0:T(4,128)S(1)} %add.266), channel_id=1, source_target_pairs={{0,4},{1,5},{2,6},{3,7},{4,0},{5,1},{6,2},{7,3},{8,12},{9,13},{10,... | collective-permute-start | bytes 344 | tf_op jit(solution)/shard_map/ppermute | solution.py:51
  108.4 3.6 %collective-permute-start.16 = (f32[4,7]{1,0:T(4,128)S(1)}, f32[4,7]{1,0:T(4,128)S(1)}, u32[]{:S(2)}, u32[]{:S(2)}) collective-permute-start(f32[4,7]{1,0:T(4,128)S(1)} %add.267), channel_id=1, source_target_pairs={{0,8},{8,0},{16,24},{24,16},{1,9},{9,1},{17,25},{25,17},{2,10},{10... | collective-permute-start | bytes 344 | tf_op jit(solution)/shard_map/ppermute | solution.py:51
  112.0 3.6 %collective-permute-start.17 = (f32[4,7]{1,0:T(4,128)S(1)}, f32[4,7]{1,0:T(4,128)S(1)}, u32[]{:S(2)}, u32[]{:S(2)}) collective-permute-start(f32[4,7]{1,0:T(4,128)S(1)} %add.268), channel_id=1, source_target_pairs={{0,16},{8,24},{16,0},{24,8},{1,17},{9,25},{17,1},{25,9},{2,18},{10... | collective-permute-start | bytes 344 | tf_op jit(solution)/shard_map/ppermute | solution.py:51
  115.6 2.2 %copy-start.3 = (f32[4,7]{1,0:T(4,128)}, f32[4,7]{1,0:T(4,128)S(1)}, u32[]{:S(2)}) copy-start(f32[4,7]{1,0:T(4,128)S(1)} %add.269) | copy-start | bytes 340

commit v8 on v7

--- a/solution.py
+++ b/solution.py
@@ -84,17 +84,18 @@
     variances = jnp.diagonal(trait_covariance)
     z = field_ext * variances[None, :, None, None]
 
-    def apply_half(x, off, mix):
+    def mix(x):
+        return jnp.einsum("ts,psrc->ptrc", trait_covariance, x, precision=lax.Precision.HIGHEST)
+
+    def stencil(x, off):
         r = x.shape[2]
-        if mix:
-            x = jnp.einsum("ts,psrc->ptrc", trait_covariance, x, precision=lax.Precision.HIGHEST)
         return land_ext[off + 1 : off + r - 1] * nine_valid(x, kappa_ext[off + 1 : off + r - 1])
 
     def apply_a(x, off):
-        return apply_half(apply_half(x, off, True), off + 1, False)
+        return mix(stencil(stencil(x, off), off + 1))
 
     def a_stages(x, off):
-        return (lambda _: apply_half(x, off, True), lambda first: apply_half(first, off + 1, False))
+        return (lambda _: stencil(x, off), lambda first: mix(stencil(first, off + 1)))
 
     def own(x, off):
         return x[:, :, h - off : h - off + rows]

time: 118 us -> 111 us (0.941)
  other arithmetic: 32.7 us -> 20.9 us
  matrix products: 6.47 us -> 12.4 us
  waiting for transfers between devices: 27.8 us -> 23 us
  starting transfers between devices: 39.1 us -> 42.2 us
    mul x6 -> x3, other arithmetic: 18.2 us -> 9.96 us  [stencil(): land_ext[off + 1:off + r - 1]]
    dot_general x3, matrix products: 6.47 us -> 12.4 us  [mix(): jnp.einsum('ts,psrc->ptrc', trait_covariance, x, precision=lax.Precision....]
    ppermute x2, waiting for transfers between devices: 4.76 us -> 0.01 us  [halo_rows(): lax.ppermute(lax.slice_in_dim(block, 0, width, axis=dim), 'tile', backward)]
    sub x1, other arithmetic: 4.13 us -> 0.58 us  [shards(): w = aq - alpha[:, None, None, None] * q]
    ppermute x14, waiting for transfers between devices: 21.4 us -> 18.9 us  [butterfly_sum(): got = lax.ppermute(v, axis, [(i, i ^ s) for i in range(n)])]
    ppermute x14, starting transfers between devices: 22.7 us -> 24.5 us  [butterfly_sum(): got = lax.ppermute(v, axis, [(i, i ^ s) for i in range(n)])]
    ppermute x2, waiting for transfers between devices: 0.01 us -> 1.44 us  [halo_rows(): lax.ppermute(lax.slice_in_dim(block, rows - width, rows, axis=dim), 'tile...]
    ppermute x2, starting transfers between devices: 4.75 us -> 6.09 us  [halo_rows(): lax.ppermute(lax.slice_in_dim(block, rows - width, rows, axis=dim), 'tile...]
  transfers between devices with their start and end apart: 20 -> 20, of which waited for: 14 -> 14; matrix products, arithmetic and copies ran while one was open for 11% -> 14% of each run, Pallas kernels for 0% -> 0%
where the time goes in v8:
time: 111 us; the launch traced here: 110 us
  starting transfers between devices  42.2 us (38%)
  waiting for transfers between devices  23 us (21%)
  other arithmetic  20.9 us (19%)
  matrix products  12.4 us (11%)
  between operations  6.34 us (6%)
  local copies, waits for them, and re-layouts  5.29 us (5%)
    ppermute x14, starting transfers between devices, butterfly_sum(): got = lax.ppermute(v, axis, [(i, i ^ s) for i in range(n)])  24.5 us
    ppermute x14, waiting for transfers between devices, butterfly_sum(): got = lax.ppermute(v, axis, [(i, i ^ s) for i in range(n)])  18.9 us
    dot_general x3, matrix products, mix(): jnp.einsum('ts,psrc->ptrc', trait_covariance, x, precision=lax.Precision....  12.4 us
    mul x3, other arithmetic, stencil(): land_ext[off + 1:off + r - 1]  9.96 us
    ppermute x2, starting transfers between devices, halo_rows(): lax.ppermute(lax.slice_in_dim(block, rows - width, rows, axis=dim), 'tile...  6.09 us
    all_to_all x1, starting transfers between devices, shards(): lax.all_to_all(signed, 'trait', split_axis=0, concat_axis=1, tiled=True)  5.19 us
    all_to_all x1, starting transfers between devices, shards(): lax.all_to_all(w_own, 'trait', split_axis=1, concat_axis=0, tiled=True)  3.86 us
    all_to_all x1, waiting for transfers between devices, shards(): lax.all_to_all(signed, 'trait', split_axis=0, concat_axis=1, tiled=True)  2.63 us
  transfers between devices with their start and end apart: 20, of which 14 were waited for; matrix products, arithmetic and copies ran while one was open for 14% of the time, Pallas kernels for 0%

profile of v8, /device:TPU:0, one launch (start us, length us, event | category | flops | bytes accessed | tf_op | source)
XLA Modules:
  0.0 110.1 jit_solution(15388917436219579329)
XLA Ops:
  0.7 2.2 %multiply_convert_fusion = bf16[4,4,8,2048]{3,2,1,0:T(8,128)(2,1)} fusion(s32[4,4,8,2048]{3,2,1,0:T(8,128)} %param.4, s32[8,2048]{1,0:T(8,128)} %param.5), kind=kLoop, calls=%fused_computation.163 | loop fusion | flops 1048576 | bytes 1638400 | tf_op jit(solution)/shard_map/convert_element_type | solution.py:79
  2.9 5.2 %all-to-all-start = ((bf16[4,4,8,2048]{3,2,1,0:T(8,128)(2,1)}), bf16[4,4,8,2048]{3,2,1,0:T(8,128)(2,1)S(1)}, u32[]{:S(2)}, u32[]{:S(2)}) async-start(bf16[4,4,8,2048]{3,2,1,0:T(8,128)(2,1)} %multiply_convert_fusion), calls=%async_computation | async-start | bytes 1048576 | tf_op jit(solution)/shard_map/all_to_all | solution.py:80
  8.1 1.3 %collective-permute-start.3 = (f32[6,2048]{1,0:T(8,128)S(1)}, f32[6,2048]{1,0:T(8,128)S(1)}, u32[]{:S(2)}, u32[]{:S(2)}) collective-permute-start(f32[6,2048]{1,0:T(8,128)S(1)} %get-tuple-element.39), channel_id=1, source_target_pairs={{1,0},{2,1},{3,2},{4,3},{5,4},{6,5},{7,6},{9,8},{10,9},{11,10},{12... | collective-permute-start | bytes 147464 | tf_op jit(solution)/shard_map/ppermute | solution.py:72
  9.4 3.0 %collective-permute-start.2 = (f32[6,2048]{1,0:T(8,128)S(1)}, f32[6,2048]{1,0:T(8,128)S(1)}, u32[]{:S(2)}, u32[]{:S(2)}) collective-permute-start(f32[6,2048]{1,0:T(8,128)S(1)} %get-tuple-element.38), channel_id=1, source_target_pairs={{0,1},{1,2},{2,3},{3,4},{4,5},{5,6},{6,7},{8,9},{9,10},{10,11},{11... | collective-permute-start | bytes 147464 | tf_op jit(solution)/shard_map/ppermute | solution.py:71
  13.5 2.6 %all-to-all-done = bf16[4,4,8,2048]{3,2,1,0:T(8,128)(2,1)S(1)} async-done(((bf16[4,4,8,2048]{3,2,1,0:T(8,128)(2,1)}), bf16[4,4,8,2048]{3,2,1,0:T(8,128)(2,1)S(1)}, u32[]{:S(2)}, u32[]{:S(2)}) %all-to-all-start) | async-done | bytes 524320 | tf_op jit(solution)/shard_map/all_to_all | solution.py:80
  16.5 1.3 %collective-permute-start.1 = (bf16[1,16,6,2048]{3,1,2,0:T(8,128)(2,1)S(1)}, bf16[1,16,6,2048]{3,1,2,0:T(8,128)(2,1)S(1)}, u32[]{:S(2)}, u32[]{:S(2)}) collective-permute-start(bf16[1,16,6,2048]{3,1,2,0:T(8,128)(2,1)S(1)} %get-tuple-element.37), channel_id=1, source_target_pairs={{1,0},{2,1},{3,2},{4,3},{5,4},{6,5},{7,6},{9,8},{10,9},{11,10},{12... | collective-permute-start | bytes 1179656 | tf_op jit(solution)/shard_map/ppermute | solution.py:72
  17.8 3.1 %collective-permute-start = (bf16[1,16,6,2048]{3,1,2,0:T(8,128)(2,1)S(1)}, bf16[1,16,6,2048]{3,1,2,0:T(8,128)(2,1)S(1)}, u32[]{:S(2)}, u32[]{:S(2)}) collective-permute-start(bf16[1,16,6,2048]{3,1,2,0:T(8,128)(2,1)S(1)} %get-tuple-element.36), channel_id=1, source_target_pairs={{0,1},{1,2},{2,3},{3,4},{4,5},{5,6},{6,7},{8,9},{9,10},{10,11},{11... | collective-permute-start | bytes 1179656 | tf_op jit(solution)/shard_map/ppermute | solution.py:71
  20.9 1.3 %collective-permute-done = bf16[1,16,6,2048]{3,1,2,0:T(8,128)(2,1)S(1)} collective-permute-done((bf16[1,16,6,2048]{3,1,2,0:T(8,128)(2,1)S(1)}, bf16[1,16,6,2048]{3,1,2,0:T(8,128)(2,1)S(1)}, u32[]{:S(2)}, u32[]{:S(2)}) %collective-permute-start) | collective-permute-done | bytes 393248 | tf_op jit(solution)/shard_map/ppermute | solution.py:71
  23.1 4.4 %fusion.5 = f32[1,16,18,2048]{3,1,2,0:T(8,128)S(1)} fusion(f32[1,16,20,2048]{3,1,2,0:T(8,128)S(1)} %broadcast_multiply_fusion, f32[18,2048]{1,0:T(8,128)S(1)} %slice_add_fusion.4, f32[18,2048]{1,0:T(8,128)S(1)} %bitcast.83), kind=kLoop, calls=%fused_computation.17 | loop fusion | flops 7667712 | bytes 12451840 | tf_op jit(solution)/shard_map/mul | solution.py:92
  27.5 5.6 %convolution_bitcast_fusion = f32[1,16,16,2048]{3,1,2,0:T(8,128)S(1)} fusion(f32[1,16,18,2048]{3,1,2,0:T(8,128)S(1)} %fusion.5, f32[16,2048]{1,0:T(8,128)S(1)} %slice_add_fusion.8, f32[16,2048]{1,0:T(8,128)S(1)} %bitcast.87, f32[16,16]{1,0:T(8,128)S(1)} %copy-done), kind=kOutput, calls=%fused_computation.3 | convolution fusion | flops 107479040 | bytes 11018240 | tf_op jit(solution)/shard_map/ts,psrc->ptrc/dot_general | solution.py:88
  33.7 4.6 %collective-permute-start.4 = (f32[1,2]{1,0:T(1,128)S(1)}, f32[1,2]{1,0:T(1,128)S(1)}, u32[]{:S(2)}, u32[]{:S(2)}) collective-permute-start(f32[1,2]{1,0:T(1,128)S(1)} %bitcast.90), channel_id=1, source_target_pairs={{0,1},{1,0},{2,3},{3,2},{4,5},{5,4},{6,7},{7,6},{8,9},{9,8},{10,11... | collective-permute-start | bytes 32 | tf_op jit(solution)/shard_map/ppermute | solution.py:51
  38.4 3.5 %fusion.33 = f32[1,16,14,2048]{3,1,2,0:T(8,128)S(1)} fusion(f32[1,16,16,2048]{3,1,2,0:T(8,128)S(1)} %convolution_bitcast_fusion, f32[14,2048]{1,0:T(8,128)S(1)} %slice_add_fusion.7, f32[14,2048]{1,0:T(8,128)S(1)} %bitcast.85), kind=kLoop, calls=%fused_computation.60 | loop fusion | flops 5963776 | bytes 9699328 | tf_op jit(solution)/shard_map/mul | solution.py:92
  42.0 2.9 %collective-permute-start.5 = (f32[1,2]{1,0:T(1,128)S(1)}, f32[1,2]{1,0:T(1,128)S(1)}, u32[]{:S(2)}, u32[]{:S(2)}) collective-permute-start(f32[1,2]{1,0:T(1,128)S(1)} %bitcast_add_fusion.2), channel_id=1, source_target_pairs={{0,2},{1,3},{2,0},{3,1},{4,6},{5,7},{6,4},{7,5},{8,10},{9,11},{10,... | collective-permute-start | bytes 32 | tf_op jit(solution)/shard_map/ppermute | solution.py:51
  44.9 4.3 %convolution_bitcast_fusion.1 = f32[1,16,12,2048]{3,1,2,0:T(8,128)S(1)} fusion(f32[1,16,14,2048]{3,1,2,0:T(8,128)S(1)} %fusion.33, f32[12,2048]{1,0:T(8,128)S(1)} %slice_add_fusion.6, f32[12,2048]{1,0:T(8,128)S(1)} %bitcast.86, f32[16,16]{1,0:T(8,128)S(1)} %copy-done), kind=kOutput, calls=%fused_computation.4 | convolution fusion | flops 80609280 | bytes 8396800 | tf_op jit(solution)/shard_map/ts,psrc->ptrc/dot_general | solution.py:88
  49.2 2.7 %collective-permute-start.6 = (f32[1,2]{1,0:T(1,128)S(1)}, f32[1,2]{1,0:T(1,128)S(1)}, u32[]{:S(2)}, u32[]{:S(2)}) collective-permute-start(f32[1,2]{1,0:T(1,128)S(1)} %add.235), channel_id=1, source_target_pairs={{0,4},{1,5},{2,6},{3,7},{4,0},{5,1},{6,2},{7,3},{8,12},{9,13},{10,... | collective-permute-start | bytes 32 | tf_op jit(solution)/shard_map/ppermute | solution.py:51
  51.9 1.9 %collective-permute-done.6 = f32[1,2]{1,0:T(1,128)S(1)} collective-permute-done((f32[1,2]{1,0:T(1,128)S(1)}, f32[1,2]{1,0:T(1,128)S(1)}, u32[]{:S(2)}, u32[]{:S(2)}) %collective-permute-start.6) | collective-permute-done | bytes 40 | tf_op jit(solution)/shard_map/ppermute | solution.py:51
  57.5 2.1 %fusion.65 = f32[1,16,10,2048]{3,1,2,0:T(8,128)S(1)} fusion(f32[1,16,12,2048]{3,1,2,0:T(8,128)S(1)} %fusion.53, f32[10,2048]{1,0:T(8,128)S(1)} %slice_add_fusion.5, f32[10,2048]{1,0:T(8,128)S(1)} %bitcast.84), kind=kLoop, calls=%fused_computation.105 | loop fusion | flops 4259840 | bytes 7077888 | tf_op jit(solution)/shard_map/mul | solution.py:92
  59.8 2.5 %convolution_bitcast_fusion.2 = f32[1,16,8,2048]{3,1,2,0:T(8,128)S(1)} fusion(f32[1,16,10,2048]{3,1,2,0:T(8,128)S(1)} %fusion.65, f32[8,2048]{1,0:T(8,128)S(1)} %broadcast_add_fusion, f32[8,2048]{1,0:T(8,128)S(1)} %bitcast.88, f32[16,16]{1,0:T(8,128)S(1)} %copy-done), kind=kOutput, calls=%fused_computation.5 | convolution fusion | flops 53739520 | bytes 5644288 | tf_op jit(solution)/shard_map/ts,psrc->ptrc/dot_general | solution.py:88
  63.2 2.6 %collective-permute-start.9 = (f32[1,3]{1,0:T(1,128)S(1)}, f32[1,3]{1,0:T(1,128)S(1)}, u32[]{:S(2)}, u32[]{:S(2)}) collective-permute-start(f32[1,3]{1,0:T(1,128)S(1)} %add.251), channel_id=1, source_target_pairs={{0,4},{1,5},{2,6},{3,7},{4,0},{5,1},{6,2},{7,3},{8,12},{9,13},{10,... | collective-permute-start | bytes 44 | tf_op jit(solution)/shard_map/ppermute | solution.py:51
  65.8 1.9 %collective-permute-done.9 = f32[1,3]{1,0:T(1,128)S(1)} collective-permute-done((f32[1,3]{1,0:T(1,128)S(1)}, f32[1,3]{1,0:T(1,128)S(1)}, u32[]{:S(2)}, u32[]{:S(2)}) %collective-permute-start.9) | collective-permute-done | bytes 44 | tf_op jit(solution)/shard_map/ppermute | solution.py:51
  74.0 2.5 %collective-permute-done.11 = f32[1,3]{1,0:T(1,128)S(1)} collective-permute-done((f32[1,3]{1,0:T(1,128)S(1)}, f32[1,3]{1,0:T(1,128)S(1)}, u32[]{:S(2)}, u32[]{:S(2)}) %collective-permute-start.11) | collective-permute-done | bytes 44 | tf_op jit(solution)/shard_map/ppermute | solution.py:51
  76.5 2.6 %collective-permute-start.12 = (f32[1,3]{1,0:T(1,128)S(1)}, f32[1,3]{1,0:T(1,128)S(1)}, u32[]{:S(2)}, u32[]{:S(2)}) collective-permute-start(f32[1,3]{1,0:T(1,128)S(1)} %add.261), channel_id=1, source_target_pairs={{0,4},{1,5},{2,6},{3,7},{4,0},{5,1},{6,2},{7,3},{8,12},{9,13},{10,... | collective-permute-start | bytes 44 | tf_op jit(solution)/shard_map/ppermute | solution.py:51
  79.1 1.9 %collective-permute-done.12 = f32[1,3]{1,0:T(1,128)S(1)} collective-permute-done((f32[1,3]{1,0:T(1,128)S(1)}, f32[1,3]{1,0:T(1,128)S(1)}, u32[]{:S(2)}, u32[]{:S(2)}) %collective-permute-start.12) | collective-permute-done | bytes 44 | tf_op jit(solution)/shard_map/ppermute | solution.py:51
  84.4 1.6 %copy.12 = f32[1,16,8,2048]{3,2,0,1:T(8,128)} copy(f32[1,16,8,2048]{3,1,2,0:T(8,128)S(1)} %get-tuple-element.22) | data formatting | bytes 2097152 | tf_op jit(solution)/shard_map/sub | solution.py:135
  86.0 3.9 %all-to-all-start.1 = ((f32[1,16,8,2048]{3,2,0,1:T(8,128)}), f32[1,16,8,2048]{3,2,0,1:T(8,128)S(1)}, u32[]{:S(2)}, u32[]{:S(2)}) async-start(f32[1,16,8,2048]{3,2,0,1:T(8,128)} %copy.12), calls=%async_computation.1 | async-start | bytes 2097152 | tf_op jit(solution)/shard_map/all_to_all | solution.py:153
  93.8 2.5 %collective-permute-done.14 = f32[4,7]{1,0:T(4,128)S(1)} collective-permute-done((f32[4,7]{1,0:T(4,128)S(1)}, f32[4,7]{1,0:T(4,128)S(1)}, u32[]{:S(2)}, u32[]{:S(2)}) %collective-permute-start.14) | collective-permute-done | bytes 144 | tf_op jit(solution)/shard_map/ppermute | solution.py:51
  96.3 2.6 %collective-permute-start.15 = (f32[4,7]{1,0:T(4,128)S(1)}, f32[4,7]{1,0:T(4,128)S(1)}, u32[]{:S(2)}, u32[]{:S(2)}) collective-permute-start(f32[4,7]{1,0:T(4,128)S(1)} %add.266), channel_id=1, source_target_pairs={{0,4},{1,5},{2,6},{3,7},{4,0},{5,1},{6,2},{7,3},{8,12},{9,13},{10,... | collective-permute-start | bytes 344 | tf_op jit(solution)/shard_map/ppermute | solution.py:51
  98.9 1.9 %collective-permute-done.15 = f32[4,7]{1,0:T(4,128)S(1)} collective-permute-done((f32[4,7]{1,0:T(4,128)S(1)}, f32[4,7]{1,0:T(4,128)S(1)}, u32[]{:S(2)}, u32[]{:S(2)}) %collective-permute-start.15) | collective-permute-done | bytes 144 | tf_op jit(solution)/shard_map/ppermute | solution.py:51
  100.8 2.0 %collective-permute-start.16 = (f32[4,7]{1,0:T(4,128)S(1)}, f32[4,7]{1,0:T(4,128)S(1)}, u32[]{:S(2)}, u32[]{:S(2)}) collective-permute-start(f32[4,7]{1,0:T(4,128)S(1)} %add.267), channel_id=1, source_target_pairs={{0,8},{8,0},{16,24},{24,16},{1,9},{9,1},{17,25},{25,17},{2,10},{10... | collective-permute-start | bytes 344 | tf_op jit(solution)/shard_map/ppermute | solution.py:51
  102.8 1.6 %collective-permute-done.16 = f32[4,7]{1,0:T(4,128)S(1)} collective-permute-done((f32[4,7]{1,0:T(4,128)S(1)}, f32[4,7]{1,0:T(4,128)S(1)}, u32[]{:S(2)}, u32[]{:S(2)}) %collective-permute-start.16) | collective-permute-done | bytes 144 | tf_op jit(solution)/shard_map/ppermute | solution.py:51
  104.4 2.0 %collective-permute-start.17 = (f32[4,7]{1,0:T(4,128)S(1)}, f32[4,7]{1,0:T(4,128)S(1)}, u32[]{:S(2)}, u32[]{:S(2)}) collective-permute-start(f32[4,7]{1,0:T(4,128)S(1)} %add.268), channel_id=1, source_target_pairs={{0,16},{8,24},{16,0},{24,8},{1,17},{9,25},{17,1},{25,9},{2,18},{10... | collective-permute-start | bytes 344 | tf_op jit(solution)/shard_map/ppermute | solution.py:51
  106.4 1.6 %collective-permute-done.17 = f32[4,7]{1,0:T(4,128)S(1)} collective-permute-done((f32[4,7]{1,0:T(4,128)S(1)}, f32[4,7]{1,0:T(4,128)S(1)}, u32[]{:S(2)}, u32[]{:S(2)}) %collective-permute-start.17) | collective-permute-done | bytes 144 | tf_op jit(solution)/shard_map/ppermute | solution.py:51
  (94 shorter events, 18.4 us)
Async XLA Ops:
  0.6 11.8 %copy-start = (f32[16,16]{1,0:T(8,128)S(1)}, f32[16,16]{1,0:T(8,128)}, u32[]{:S(2)}) copy-start(f32[16,16]{1,0:T(8,128)} %param.7) | copy-start | bytes 3076
  0.6 7.4 %copy-start.2 = (f32[8,2048]{1,0:T(8,128)S(1)}, f32[8,2048]{1,0:T(8,128)}, u32[]{:S(2)}) copy-start(f32[8,2048]{1,0:T(8,128)} %param.6) | copy-start | bytes 196612
  2.9 13.2 %all-to-all-start = ((bf16[4,4,8,2048]{3,2,1,0:T(8,128)(2,1)}), bf16[4,4,8,2048]{3,2,1,0:T(8,128)(2,1)S(1)}, u32[]{:S(2)}, u32[]{:S(2)}) async-start(bf16[4,4,8,2048]{3,2,1,0:T(8,128)(2,1)} %multiply_convert_fusion), calls=%async_computation | async-start | bytes 1048576 | tf_op jit(solution)/shard_map/all_to_all | solution.py:80
  8.1 5.0 %collective-permute-start.3 = (f32[6,2048]{1,0:T(8,128)S(1)}, f32[6,2048]{1,0:T(8,128)S(1)}, u32[]{:S(2)}, u32[]{:S(2)}) collective-permute-start(f32[6,2048]{1,0:T(8,128)S(1)} %get-tuple-element.39), channel_id=1, source_target_pairs={{1,0},{2,1},{3,2},{4,3},{5,4},{6,5},{7,6},{9,8},{10,9},{11,10},{12... | collective-permute-start | bytes 147464 | tf_op jit(solution)/shard_map/ppermute | solution.py:72
  9.4 3.9 %collective-permute-start.2 = (f32[6,2048]{1,0:T(8,128)S(1)}, f32[6,2048]{1,0:T(8,128)S(1)}, u32[]{:S(2)}, u32[]{:S(2)}) collective-permute-start(f32[6,2048]{1,0:T(8,128)S(1)} %get-tuple-element.38), channel_id=1, source_target_pairs={{0,1},{1,2},{2,3},{3,4},{4,5},{5,6},{6,7},{8,9},{9,10},{10,11},{11... | collective-permute-start | bytes 147464 | tf_op jit(solution)/shard_map/ppermute | solution.py:71
  16.5 4.4 %collective-permute-start.1 = (bf16[1,16,6,2048]{3,1,2,0:T(8,128)(2,1)S(1)}, bf16[1,16,6,2048]{3,1,2,0:T(8,128)(2,1)S(1)}, u32[]{:S(2)}, u32[]{:S(2)}) collective-permute-start(bf16[1,16,6,2048]{3,1,2,0:T(8,128)(2,1)S(1)} %get-tuple-element.37), channel_id=1, source_target_pairs={{1,0},{2,1},{3,2},{4,3},{5,4},{6,5},{7,6},{9,8},{10,9},{11,10},{12... | collective-permute-start | bytes 1179656 | tf_op jit(solution)/shard_map/ppermute | solution.py:72
  17.8 4.4 %collective-permute-start = (bf16[1,16,6,2048]{3,1,2,0:T(8,128)(2,1)S(1)}, bf16[1,16,6,2048]{3,1,2,0:T(8,128)(2,1)S(1)}, u32[]{:S(2)}, u32[]{:S(2)}) collective-permute-start(bf16[1,16,6,2048]{3,1,2,0:T(8,128)(2,1)S(1)} %get-tuple-element.36), channel_id=1, source_target_pairs={{0,1},{1,2},{2,3},{3,4},{4,5},{5,6},{6,7},{8,9},{9,10},{10,11},{11... | collective-permute-start | bytes 1179656 | tf_op jit(solution)/shard_map/ppermute | solution.py:71
  22.4 0.7 copy-start.1
  33.3 5.0 %slice-start = ((f32[1,1,20,2048]{3,1,2,0:T(1,128)}), f32[1,1,14,2048]{3,1,2,0:T(1,128)S(1)}, s32[]{:S(2)}) async-start(f32[1,1,20,2048]{3,1,2,0:T(1,128)} %copy-done.1), calls=%async_computation.2 | async-start | bytes 229376 | tf_op jit(solution)/shard_map/slice | solution.py:92
  33.3 5.0 %slice-start.1 = ((f32[1,1,20,2048]{3,1,2,0:T(1,128)}), f32[1,1,12,2048]{3,1,2,0:T(1,128)S(1)}, s32[]{:S(2)}) async-start(f32[1,1,20,2048]{3,1,2,0:T(1,128)} %copy-done.1), calls=%async_computation.3 | async-start | bytes 196608 | tf_op jit(solution)/shard_map/slice | solution.py:92
  33.3 5.1 %slice-start.2 = ((f32[1,1,20,2048]{3,1,2,0:T(1,128)}), f32[1,1,10,2048]{3,1,2,0:T(1,128)S(1)}, s32[]{:S(2)}) async-start(f32[1,1,20,2048]{3,1,2,0:T(1,128)} %copy-done.1), calls=%async_computation.4 | async-start | bytes 163840 | tf_op jit(solution)/shard_map/slice | solution.py:92
  33.3 5.1 %slice-start.3 = ((f32[1,1,20,2048]{3,1,2,0:T(1,128)}), f32[1,1,8,2048]{3,1,2,0:T(1,128)S(1)}, s32[]{:S(2)}) async-start(f32[1,1,20,2048]{3,1,2,0:T(1,128)} %copy-done.1), calls=%async_computation.5 | async-start | bytes 131072 | tf_op jit(solution)/shard_map/slice | solution.py:92
  33.7 8.3 %collective-permute-start.4 = (f32[1,2]{1,0:T(1,128)S(1)}, f32[1,2]{1,0:T(1,128)S(1)}, u32[]{:S(2)}, u32[]{:S(2)}) collective-permute-start(f32[1,2]{1,0:T(1,128)S(1)} %bitcast.90), channel_id=1, source_target_pairs={{0,1},{1,0},{2,3},{3,2},{4,5},{5,4},{6,7},{7,6},{8,9},{9,8},{10,11... | collective-permute-start | bytes 32 | tf_op jit(solution)/shard_map/ppermute | solution.py:51
  42.0 7.2 %collective-permute-start.5 = (f32[1,2]{1,0:T(1,128)S(1)}, f32[1,2]{1,0:T(1,128)S(1)}, u32[]{:S(2)}, u32[]{:S(2)}) collective-permute-start(f32[1,2]{1,0:T(1,128)S(1)} %bitcast_add_fusion.2), channel_id=1, source_target_pairs={{0,2},{1,3},{2,0},{3,1},{4,6},{5,7},{6,4},{7,5},{8,10},{9,11},{10,... | collective-permute-start | bytes 32 | tf_op jit(solution)/shard_map/ppermute | solution.py:51
  49.2 4.5 %collective-permute-start.6 = (f32[1,2]{1,0:T(1,128)S(1)}, f32[1,2]{1,0:T(1,128)S(1)}, u32[]{:S(2)}, u32[]{:S(2)}) collective-permute-start(f32[1,2]{1,0:T(1,128)S(1)} %add.235), channel_id=1, source_target_pairs={{0,4},{1,5},{2,6},{3,7},{4,0},{5,1},{6,2},{7,3},{8,12},{9,13},{10,... | collective-permute-start | bytes 32 | tf_op jit(solution)/shard_map/ppermute | solution.py:51
  57.4 2.1 %collective-permute-start.7 = (f32[1,3]{1,0:T(1,128)S(1)}, f32[1,3]{1,0:T(1,128)S(1)}, u32[]{:S(2)}, u32[]{:S(2)}) collective-permute-start(f32[1,3]{1,0:T(1,128)S(1)} %bitcast.91), channel_id=1, source_target_pairs={{0,1},{1,0},{2,3},{3,2},{4,5},{5,4},{6,7},{7,6},{8,9},{9,8},{10,11... | collective-permute-start | bytes 44 | tf_op jit(solution)/shard_map/ppermute | solution.py:51
  59.6 3.6 %collective-permute-start.8 = (f32[1,3]{1,0:T(1,128)S(1)}, f32[1,3]{1,0:T(1,128)S(1)}, u32[]{:S(2)}, u32[]{:S(2)}) collective-permute-start(f32[1,3]{1,0:T(1,128)S(1)} %bitcast_add_fusion.1), channel_id=1, source_target_pairs={{0,2},{1,3},{2,0},{3,1},{4,6},{5,7},{6,4},{7,5},{8,10},{9,11},{10,... | collective-permute-start | bytes 44 | tf_op jit(solution)/shard_map/ppermute | solution.py:51
  63.2 4.5 %collective-permute-start.9 = (f32[1,3]{1,0:T(1,128)S(1)}, f32[1,3]{1,0:T(1,128)S(1)}, u32[]{:S(2)}, u32[]{:S(2)}) collective-permute-start(f32[1,3]{1,0:T(1,128)S(1)} %add.251), channel_id=1, source_target_pairs={{0,4},{1,5},{2,6},{3,7},{4,0},{5,1},{6,2},{7,3},{8,12},{9,13},{10,... | collective-permute-start | bytes 44 | tf_op jit(solution)/shard_map/ppermute | solution.py:51
  71.7 1.2 %collective-permute-start.10 = (f32[1,3]{1,0:T(1,128)S(1)}, f32[1,3]{1,0:T(1,128)S(1)}, u32[]{:S(2)}, u32[]{:S(2)}) collective-permute-start(f32[1,3]{1,0:T(1,128)S(1)} %bitcast.92), channel_id=1, source_target_pairs={{0,1},{1,0},{2,3},{3,2},{4,5},{5,4},{6,7},{7,6},{8,9},{9,8},{10,11... | collective-permute-start | bytes 44 | tf_op jit(solution)/shard_map/ppermute | solution.py:51
  72.9 3.6 %collective-permute-start.11 = (f32[1,3]{1,0:T(1,128)S(1)}, f32[1,3]{1,0:T(1,128)S(1)}, u32[]{:S(2)}, u32[]{:S(2)}) collective-permute-start(f32[1,3]{1,0:T(1,128)S(1)} %bitcast_add_fusion), channel_id=1, source_target_pairs={{0,2},{1,3},{2,0},{3,1},{4,6},{5,7},{6,4},{7,5},{8,10},{9,11},{10,... | collective-permute-start | bytes 44 | tf_op jit(solution)/shard_map/ppermute | solution.py:51
  76.5 4.5 %collective-permute-start.12 = (f32[1,3]{1,0:T(1,128)S(1)}, f32[1,3]{1,0:T(1,128)S(1)}, u32[]{:S(2)}, u32[]{:S(2)}) collective-permute-start(f32[1,3]{1,0:T(1,128)S(1)} %add.261), channel_id=1, source_target_pairs={{0,4},{1,5},{2,6},{3,7},{4,0},{5,1},{6,2},{7,3},{8,12},{9,13},{10,... | collective-permute-start | bytes 44 | tf_op jit(solution)/shard_map/ppermute | solution.py:51
  86.0 22.9 %all-to-all-start.1 = ((f32[1,16,8,2048]{3,2,0,1:T(8,128)}), f32[1,16,8,2048]{3,2,0,1:T(8,128)S(1)}, u32[]{:S(2)}, u32[]{:S(2)}) async-start(f32[1,16,8,2048]{3,2,0,1:T(8,128)} %copy.12), calls=%async_computation.1 | async-start | bytes 2097152 | tf_op jit(solution)/shard_map/all_to_all | solution.py:153
  90.7 1.2 %collective-permute-start.13 = (f32[4,7]{1,0:T(4,128)S(1)}, f32[4,7]{1,0:T(4,128)S(1)}, u32[]{:S(2)}, u32[]{:S(2)}) collective-permute-start(f32[4,7]{1,0:T(4,128)S(1)} %dynamic_update_slice.5), channel_id=1, source_target_pairs={{0,1},{1,0},{2,3},{3,2},{4,5},{5,4},{6,7},{7,6},{8,9},{9,8},{10,11... | collective-permute-start | bytes 344 | tf_op jit(solution)/shard_map/ppermute | solution.py:51
  92.7 3.6 %collective-permute-start.14 = (f32[4,7]{1,0:T(4,128)S(1)}, f32[4,7]{1,0:T(4,128)S(1)}, u32[]{:S(2)}, u32[]{:S(2)}) collective-permute-start(f32[4,7]{1,0:T(4,128)S(1)} %add.265), channel_id=1, source_target_pairs={{0,2},{1,3},{2,0},{3,1},{4,6},{5,7},{6,4},{7,5},{8,10},{9,11},{10,... | collective-permute-start | bytes 344 | tf_op jit(solution)/shard_map/ppermute | solution.py:51
  96.3 4.5 %collective-permute-start.15 = (f32[4,7]{1,0:T(4,128)S(1)}, f32[4,7]{1,0:T(4,128)S(1)}, u32[]{:S(2)}, u32[]{:S(2)}) collective-permute-start(f32[4,7]{1,0:T(4,128)S(1)} %add.266), channel_id=1, source_target_pairs={{0,4},{1,5},{2,6},{3,7},{4,0},{5,1},{6,2},{7,3},{8,12},{9,13},{10,... | collective-permute-start | bytes 344 | tf_op jit(solution)/shard_map/ppermute | solution.py:51
  100.8 3.6 %collective-permute-start.16 = (f32[4,7]{1,0:T(4,128)S(1)}, f32[4,7]{1,0:T(4,128)S(1)}, u32[]{:S(2)}, u32[]{:S(2)}) collective-permute-start(f32[4,7]{1,0:T(4,128)S(1)} %add.267), channel_id=1, source_target_pairs={{0,8},{8,0},{16,24},{24,16},{1,9},{9,1},{17,25},{25,17},{2,10},{10... | collective-permute-start | bytes 344 | tf_op jit(solution)/shard_map/ppermute | solution.py:51
  104.4 3.6 %collective-permute-start.17 = (f32[4,7]{1,0:T(4,128)S(1)}, f32[4,7]{1,0:T(4,128)S(1)}, u32[]{:S(2)}, u32[]{:S(2)}) collective-permute-start(f32[4,7]{1,0:T(4,128)S(1)} %add.268), channel_id=1, source_target_pairs={{0,16},{8,24},{16,0},{24,8},{1,17},{9,25},{17,1},{25,9},{2,18},{10... | collective-permute-start | bytes 344 | tf_op jit(solution)/shard_map/ppermute | solution.py:51
  108.0 2.2 %copy-start.3 = (f32[4,7]{1,0:T(4,128)}, f32[4,7]{1,0:T(4,128)S(1)}, u32[]{:S(2)}) copy-start(f32[4,7]{1,0:T(4,128)S(1)} %add.269) | copy-start | bytes 340

commit v9 on v8

--- a/solution.py
+++ b/solution.py
@@ -9,7 +9,7 @@
 cross_term = 0.1
 epsilon = 1e-06
 
-HALO = 6
+HALO = 2
 
 
 def nine_valid(x, kappa_rows):
@@ -94,41 +94,35 @@
     def apply_a(x, off):
         return mix(stencil(stencil(x, off), off + 1))
 
-    def a_stages(x, off):
-        return (lambda _: stencil(x, off), lambda first: mix(stencil(first, off + 1)))
+    def own(x):
+        return x[:, :, h : h + rows]
 
-    def own(x, off):
-        return x[:, :, h - off : h - off + rows]
-
-    def dot(a, b, off):
-        return jnp.sum(own(a, off) * own(b, off), axis=(1, 2, 3))
-
-    def crop(x, k):
-        return x[:, :, k : x.shape[2] - k]
-
-    def reduce_tile(pairs, off, work=()):
-        prods = jnp.stack([own(a, off) * own(b, off) for a, b in pairs], axis=-1)
+    def reduce_tile(pairs, work=()):
+        prods = jnp.stack([a * b for a, b in pairs], axis=-1)
         return butterfly_sum(jnp.sum(prods, axis=(1, 2, 3)), "tile", work)
 
+    def a_stages(x):
+        return (
+            lambda _: halo_rows(x, h),
+            lambda ext: stencil(ext, 0),
+            lambda first: mix(stencil(first, 1)),
+        )
+
     az = apply_a(z, 0)
-    z2 = crop(z, 2)
-    sums, aaz = reduce_tile([(z2, z2), (az, z2)], 2, a_stages(az, 2))
+    z = own(z)
+    sums, aaz = reduce_tile([(z, z), (az, z)], a_stages(az))
     norm = jnp.sqrt(sums[:, 0] + epsilon)
     alpha = sums[:, 1] / (norm * norm)
-    q = z2 / norm[:, None, None, None]
+    q = z / norm[:, None, None, None]
     aq = az / norm[:, None, None, None]
     w = aq - alpha[:, None, None, None] * q
-    aw = aaz / norm[:, None, None, None] - alpha[:, None, None, None] * crop(aq, 2)
-    aq = crop(aq, 2)
-    q = crop(q, 2)
-    w = crop(w, 2)
-    off = 4
+    aw = aaz / norm[:, None, None, None] - alpha[:, None, None, None] * aq
     alphas = [alpha]
     betas = []
     iters = 3
     for step in range(1, iters):
         last_step = step == iters - 1
-        sums, aaw = reduce_tile([(w, w), (aw, w), (q, w)], off, () if last_step else a_stages(aw, off))
+        sums, aaw = reduce_tile([(w, w), (aw, w), (q, w)], () if last_step else a_stages(aw))
         beta = jnp.sqrt(sums[:, 0] + epsilon)
         alpha = sums[:, 1] / (beta * beta) - sums[:, 2]
         q_next = w / beta[:, None, None, None]
@@ -136,20 +130,16 @@
         if not last_step:
             aw_next = (
                 aaw / beta[:, None, None, None]
-                - beta[:, None, None, None] * crop(aq, 2)
-                - alpha[:, None, None, None] * crop(aw, 2) / beta[:, None, None, None]
+                - beta[:, None, None, None] * aq
+                - alpha[:, None, None, None] * aw / beta[:, None, None, None]
             )
-            aq = crop(aw, 2) / beta[:, None, None, None]
-            q = crop(q_next, 2)
-            w = crop(w_next, 2)
+            aq = aw / beta[:, None, None, None]
             aw = aw_next
-            off += 2
-        else:
-            q = q_next
-            w = w_next
+        q = q_next
+        w = w_next
         betas.append(beta)
         alphas.append(alpha)
-    w_own = own(w, off)
+    w_own = w
     w_back = lax.all_to_all(w_own, "trait", split_axis=1, concat_axis=0, tiled=True)
     partial = jnp.sum(w_own * w_own, axis=(1, 2, 3))[:, None]
     first = (lax.axis_index("tile") == 0).astype(jnp.float32)

time: 111 us -> 127 us (1.14)
  starting transfers between devices: 42.2 us -> 58 us
  waiting for transfers between devices: 23 us -> 31.8 us
  matrix products: 12.4 us -> 7.57 us
  other arithmetic: 20.9 us -> 16.7 us
    ppermute x14, starting transfers between devices: 24.5 us -> 31.6 us  [butterfly_sum(): got = lax.ppermute(v, axis, [(i, i ^ s) for i in range(n)])]
    ppermute x2 -> x4, starting transfers between devices: 6.09 us -> 12.6 us  [halo_rows(): lax.ppermute(lax.slice_in_dim(block, rows - width, rows, axis=dim), 'tile...]
    dot_general x3, matrix products: 12.4 us -> 7.57 us  [mix(): jnp.einsum('ts,psrc->ptrc', trait_covariance, x, precision=lax.Precision....]
    all_to_all x1, waiting for transfers between devices: 2.63 us -> 7.44 us  [shards(): lax.all_to_all(signed, 'trait', split_axis=0, concat_axis=1, tiled=True)]
    ppermute x2 -> x4, waiting for transfers between devices: 0.01 us -> 4.53 us  [halo_rows(): lax.ppermute(lax.slice_in_dim(block, 0, width, axis=dim), 'tile', backward)]
    mul x3, other arithmetic: 9.96 us -> 6.28 us  [stencil(): land_ext[off + 1:off + r - 1]]
    ppermute x2 -> x4, starting transfers between devices: 2.58 us -> 5.7 us  [halo_rows(): lax.ppermute(lax.slice_in_dim(block, 0, width, axis=dim), 'tile', backward)]
    ppermute x2 -> x4, waiting for transfers between devices: 1.44 us -> 0.01 us  [halo_rows(): lax.ppermute(lax.slice_in_dim(block, rows - width, rows, axis=dim), 'tile...]
  transfers between devices with their start and end apart: 20 -> 24, of which waited for: 14 -> 16; matrix products, arithmetic and copies ran while one was open for 14% -> 5% of each run, Pallas kernels for 0% -> 0%
where the time goes in v9:
time: 127 us; the launch traced here: 126 us
  starting transfers between devices  58 us (46%)
  waiting for transfers between devices  31.8 us (25%)
  other arithmetic  16.7 us (13%)
  matrix products  7.57 us (6%)
  between operations  6.35 us (5%)
  local copies, waits for them, and re-layouts  5.74 us (5%)
    ppermute x14, starting transfers between devices, butterfly_sum(): got = lax.ppermute(v, axis, [(i, i ^ s) for i in range(n)])  31.6 us
    ppermute x14, waiting for transfers between devices, butterfly_sum(): got = lax.ppermute(v, axis, [(i, i ^ s) for i in range(n)])  19.8 us
    ppermute x4, starting transfers between devices, halo_rows(): lax.ppermute(lax.slice_in_dim(block, rows - width, rows, axis=dim), 'tile...  12.6 us
    dot_general x3, matrix products, mix(): jnp.einsum('ts,psrc->ptrc', trait_covariance, x, precision=lax.Precision....  7.57 us
    all_to_all x1, waiting for transfers between devices, shards(): lax.all_to_all(signed, 'trait', split_axis=0, concat_axis=1, tiled=True)  7.44 us
    mul x3, other arithmetic, stencil(): land_ext[off + 1:off + r - 1]  6.28 us
    ppermute x4, starting transfers between devices, halo_rows(): lax.ppermute(lax.slice_in_dim(block, 0, width, axis=dim), 'tile', backward)  5.7 us
    ppermute x4, waiting for transfers between devices, halo_rows(): lax.ppermute(lax.slice_in_dim(block, 0, width, axis=dim), 'tile', backward)  4.53 us
  transfers between devices with their start and end apart: 24, of which 16 were waited for; matrix products, arithmetic and copies ran while one was open for 5% of the time, Pallas kernels for 0%

profile of v9, /device:TPU:0, one launch (start us, length us, event | category | flops | bytes accessed | tf_op | source)
XLA Modules:
  0.0 126.1 jit_solution(17374204902915264034)
XLA Ops:
  1.6 2.4 %collective-permute-start.2 = (f32[2,2048]{1,0:T(2,128)S(1)}, f32[2,2048]{1,0:T(2,128)S(1)}, u32[]{:S(2)}, u32[]{:S(2)}) collective-permute-start(f32[2,2048]{1,0:T(2,128)S(1)} %get-tuple-element.49), channel_id=1, source_target_pairs={{0,1},{1,2},{2,3},{3,4},{4,5},{5,6},{6,7},{8,9},{9,10},{10,11},{11... | collective-permute-start | bytes 49160 | tf_op jit(solution)/shard_map/ppermute | solution.py:71
  5.4 2.2 %multiply_convert_fusion = bf16[4,4,8,2048]{3,2,1,0:T(8,128)(2,1)} fusion(s32[4,4,8,2048]{3,2,1,0:T(8,128)} %param.4, s32[8,2048]{1,0:T(8,128)} %param.5), kind=kLoop, calls=%fused_computation.142 | loop fusion | flops 1048576 | bytes 1638400 | tf_op jit(solution)/shard_map/convert_element_type | solution.py:79
  7.6 4.5 %all-to-all-start = ((bf16[4,4,8,2048]{3,2,1,0:T(8,128)(2,1)}), bf16[4,4,8,2048]{3,2,1,0:T(8,128)(2,1)S(1)}, u32[]{:S(2)}, u32[]{:S(2)}) async-start(bf16[4,4,8,2048]{3,2,1,0:T(8,128)(2,1)} %multiply_convert_fusion), calls=%async_computation | async-start | bytes 1048576 | tf_op jit(solution)/shard_map/all_to_all | solution.py:80
  12.9 7.4 %all-to-all-done = bf16[4,4,8,2048]{3,2,1,0:T(8,128)(2,1)S(1)} async-done(((bf16[4,4,8,2048]{3,2,1,0:T(8,128)(2,1)}), bf16[4,4,8,2048]{3,2,1,0:T(8,128)(2,1)S(1)}, u32[]{:S(2)}, u32[]{:S(2)}) %all-to-all-start) | async-done | bytes 524320 | tf_op jit(solution)/shard_map/all_to_all | solution.py:80
  20.6 3.0 %collective-permute-start = (bf16[1,16,2,2048]{3,1,2,0:T(8,128)(2,1)S(1)}, bf16[1,16,2,2048]{3,1,2,0:T(8,128)(2,1)S(1)}, u32[]{:S(2)}, u32[]{:S(2)}) collective-permute-start(bf16[1,16,2,2048]{3,1,2,0:T(8,128)(2,1)S(1)} %get-tuple-element.47), channel_id=1, source_target_pairs={{0,1},{1,2},{2,3},{3,4},{4,5},{5,6},{6,7},{8,9},{9,10},{10,11},{11... | collective-permute-start | bytes 393224 | tf_op jit(solution)/shard_map/ppermute | solution.py:71
  25.0 4.5 %collective-permute-done.1 = bf16[1,16,2,2048]{3,1,2,0:T(8,128)(2,1)S(1)} collective-permute-done((bf16[1,16,2,2048]{3,1,2,0:T(8,128)(2,1)S(1)}, bf16[1,16,2,2048]{3,1,2,0:T(8,128)(2,1)S(1)}, u32[]{:S(2)}, u32[]{:S(2)}) %collective-permute-start.1) | collective-permute-done | bytes 131104 | tf_op jit(solution)/shard_map/ppermute | solution.py:72
  30.0 2.1 %fusion.5 = f32[1,16,10,2048]{3,1,2,0:T(8,128)S(1)} fusion(f32[1,16,12,2048]{3,1,2,0:T(8,128)S(1)} %broadcast_multiply_fusion, f32[10,2048]{1,0:T(8,128)S(1)} %fusion.103, f32[10,2048]{1,0:T(8,128)S(1)} %bitcast.70), kind=kLoop, calls=%fused_computation.32 | loop fusion | flops 4259840 | bytes 7077888 | tf_op jit(solution)/shard_map/mul | solution.py:92
  32.1 2.5 %convolution_bitcast_fusion.2 = f32[1,16,8,2048]{3,1,2,0:T(8,128)S(1)} fusion(f32[1,16,10,2048]{3,1,2,0:T(8,128)S(1)} %fusion.5, f32[8,2048]{1,0:T(8,128)S(1)} %broadcast_add_fusion, f32[8,2048]{1,0:T(8,128)S(1)} %bitcast.74, f32[16,16]{1,0:T(8,128)S(1)} %copy-done), kind=kOutput, calls=%fused_computation.5 | convolution fusion | flops 53739520 | bytes 5644288 | tf_op jit(solution)/shard_map/ts,psrc->ptrc/dot_general | solution.py:88
  34.9 5.5 %collective-permute-start.5 = (f32[1,16,2,2048]{3,1,2,0:T(8,128)S(1)}, f32[1,16,2,2048]{3,1,2,0:T(8,128)S(1)}, u32[]{:S(2)}, u32[]{:S(2)}) collective-permute-start(f32[1,16,2,2048]{3,1,2,0:T(8,128)S(1)} %get-tuple-element.45), channel_id=1, source_target_pairs={{0,1},{1,2},{2,3},{3,4},{4,5},{5,6},{6,7},{8,9},{9,10},{10,11},{11... | collective-permute-start | bytes 786440 | tf_op jit(solution)/shard_map/ppermute | solution.py:71
  44.3 2.1 %fusion.15 = f32[1,16,10,2048]{3,1,2,0:T(8,128)S(1)} fusion(f32[1,16,12,2048]{3,1,2,0:T(8,128)S(1)} %pad_maximum_fusion, f32[10,2048]{1,0:T(8,128)S(1)} %fusion.103, f32[10,2048]{1,0:T(8,128)S(1)} %bitcast.71), kind=kLoop, calls=%fused_computation.42 | loop fusion | flops 4259840 | bytes 7077888 | tf_op jit(solution)/shard_map/mul | solution.py:92
  46.4 3.7 %collective-permute-start.7 = (f32[1,2]{1,0:T(1,128)S(1)}, f32[1,2]{1,0:T(1,128)S(1)}, u32[]{:S(2)}, u32[]{:S(2)}) collective-permute-start(f32[1,2]{1,0:T(1,128)S(1)} %bitcast_add_fusion.2), channel_id=1, source_target_pairs={{0,2},{1,3},{2,0},{3,1},{4,6},{5,7},{6,4},{7,5},{8,10},{9,11},{10,... | collective-permute-start | bytes 32 | tf_op jit(solution)/shard_map/ppermute | solution.py:51
  51.7 2.5 %convolution_bitcast_fusion.1 = f32[1,16,8,2048]{3,1,2,0:T(8,128)S(1)} fusion(f32[1,16,10,2048]{3,1,2,0:T(8,128)S(1)} %fusion.15, f32[8,2048]{1,0:T(8,128)S(1)} %broadcast_add_fusion, f32[8,2048]{1,0:T(8,128)S(1)} %bitcast.75, f32[16,16]{1,0:T(8,128)S(1)} %copy-done), kind=kOutput, calls=%fused_computation.4 | convolution fusion | flops 53739520 | bytes 5644288 | tf_op jit(solution)/shard_map/ts,psrc->ptrc/dot_general | solution.py:88
  54.2 3.1 %collective-permute-start.8 = (f32[1,2]{1,0:T(1,128)S(1)}, f32[1,2]{1,0:T(1,128)S(1)}, u32[]{:S(2)}, u32[]{:S(2)}) collective-permute-start(f32[1,2]{1,0:T(1,128)S(1)} %add.193), channel_id=1, source_target_pairs={{0,4},{1,5},{2,6},{3,7},{4,0},{5,1},{6,2},{7,3},{8,12},{9,13},{10,... | collective-permute-start | bytes 32 | tf_op jit(solution)/shard_map/ppermute | solution.py:51
  61.6 1.8 %collective-permute-start.10 = (f32[1,16,2,2048]{3,1,2,0:T(8,128)S(1)}, f32[1,16,2,2048]{3,1,2,0:T(8,128)S(1)}, u32[]{:S(2)}, u32[]{:S(2)}) collective-permute-start(f32[1,16,2,2048]{3,1,2,0:T(8,128)S(1)} %get-tuple-element.42), channel_id=1, source_target_pairs={{0,1},{1,2},{2,3},{3,4},{4,5},{5,6},{6,7},{8,9},{9,10},{10,11},{11... | collective-permute-start | bytes 786440 | tf_op jit(solution)/shard_map/ppermute | solution.py:71
  65.3 2.8 %collective-permute-start.9 = (f32[1,3]{1,0:T(1,128)S(1)}, f32[1,3]{1,0:T(1,128)S(1)}, u32[]{:S(2)}, u32[]{:S(2)}) collective-permute-start(f32[1,3]{1,0:T(1,128)S(1)} %bitcast.79), channel_id=1, source_target_pairs={{0,1},{1,0},{2,3},{3,2},{4,5},{5,4},{6,7},{7,6},{8,9},{9,8},{10,11... | collective-permute-start | bytes 44 | tf_op jit(solution)/shard_map/ppermute | solution.py:51
  69.1 2.1 %fusion.25 = f32[1,16,10,2048]{3,1,2,0:T(8,128)S(1)} fusion(f32[1,16,12,2048]{3,1,2,0:T(8,128)S(1)} %pad_maximum_fusion.1, f32[10,2048]{1,0:T(8,128)S(1)} %fusion.103, f32[10,2048]{1,0:T(8,128)S(1)} %bitcast.72), kind=kLoop, calls=%fused_computation.52 | loop fusion | flops 4259840 | bytes 7077888 | tf_op jit(solution)/shard_map/mul | solution.py:92
  71.2 4.1 %collective-permute-start.12 = (f32[1,3]{1,0:T(1,128)S(1)}, f32[1,3]{1,0:T(1,128)S(1)}, u32[]{:S(2)}, u32[]{:S(2)}) collective-permute-start(f32[1,3]{1,0:T(1,128)S(1)} %bitcast_add_fusion.1), channel_id=1, source_target_pairs={{0,2},{1,3},{2,0},{3,1},{4,6},{5,7},{6,4},{7,5},{8,10},{9,11},{10,... | collective-permute-start | bytes 44 | tf_op jit(solution)/shard_map/ppermute | solution.py:51
  76.8 2.5 %convolution_bitcast_fusion = f32[1,16,8,2048]{3,1,2,0:T(8,128)S(1)} fusion(f32[1,16,10,2048]{3,1,2,0:T(8,128)S(1)} %fusion.25, f32[8,2048]{1,0:T(8,128)S(1)} %broadcast_add_fusion, f32[8,2048]{1,0:T(8,128)S(1)} %bitcast.76, f32[16,16]{1,0:T(8,128)S(1)} %copy-done), kind=kOutput, calls=%fused_computation.3 | convolution fusion | flops 53739520 | bytes 5644288 | tf_op jit(solution)/shard_map/ts,psrc->ptrc/dot_general | solution.py:88
  79.3 3.1 %collective-permute-start.13 = (f32[1,3]{1,0:T(1,128)S(1)}, f32[1,3]{1,0:T(1,128)S(1)}, u32[]{:S(2)}, u32[]{:S(2)}) collective-permute-start(f32[1,3]{1,0:T(1,128)S(1)} %add.205), channel_id=1, source_target_pairs={{0,4},{1,5},{2,6},{3,7},{4,0},{5,1},{6,2},{7,3},{8,12},{9,13},{10,... | collective-permute-start | bytes 44 | tf_op jit(solution)/shard_map/ppermute | solution.py:51
  89.2 1.9 %collective-permute-start.15 = (f32[1,3]{1,0:T(1,128)S(1)}, f32[1,3]{1,0:T(1,128)S(1)}, u32[]{:S(2)}, u32[]{:S(2)}) collective-permute-start(f32[1,3]{1,0:T(1,128)S(1)} %bitcast_add_fusion), channel_id=1, source_target_pairs={{0,2},{1,3},{2,0},{3,1},{4,6},{5,7},{6,4},{7,5},{8,10},{9,11},{10,... | collective-permute-start | bytes 44 | tf_op jit(solution)/shard_map/ppermute | solution.py:51
  91.1 1.7 %collective-permute-done.15 = f32[1,3]{1,0:T(1,128)S(1)} collective-permute-done((f32[1,3]{1,0:T(1,128)S(1)}, f32[1,3]{1,0:T(1,128)S(1)}, u32[]{:S(2)}, u32[]{:S(2)}) %collective-permute-start.15) | collective-permute-done | bytes 44 | tf_op jit(solution)/shard_map/ppermute | solution.py:51
  92.7 2.9 %collective-permute-start.16 = (f32[1,3]{1,0:T(1,128)S(1)}, f32[1,3]{1,0:T(1,128)S(1)}, u32[]{:S(2)}, u32[]{:S(2)}) collective-permute-start(f32[1,3]{1,0:T(1,128)S(1)} %add.217), channel_id=1, source_target_pairs={{0,4},{1,5},{2,6},{3,7},{4,0},{5,1},{6,2},{7,3},{8,12},{9,13},{10,... | collective-permute-start | bytes 44 | tf_op jit(solution)/shard_map/ppermute | solution.py:51
  100.7 1.6 %copy.12 = f32[1,16,8,2048]{3,2,0,1:T(8,128)} copy(f32[1,16,8,2048]{3,1,2,0:T(8,128)S(1)} %get-tuple-element.30) | data formatting | bytes 2097152 | tf_op jit(solution)/shard_map/sub | solution.py:129
  102.3 3.5 %all-to-all-start.1 = ((f32[1,16,8,2048]{3,2,0,1:T(8,128)}), f32[1,16,8,2048]{3,2,0,1:T(8,128)S(1)}, u32[]{:S(2)}, u32[]{:S(2)}) async-start(f32[1,16,8,2048]{3,2,0,1:T(8,128)} %copy.12), calls=%async_computation.1 | async-start | bytes 2097152 | tf_op jit(solution)/shard_map/all_to_all | solution.py:143
  108.6 2.0 %collective-permute-start.18 = (f32[4,7]{1,0:T(4,128)S(1)}, f32[4,7]{1,0:T(4,128)S(1)}, u32[]{:S(2)}, u32[]{:S(2)}) collective-permute-start(f32[4,7]{1,0:T(4,128)S(1)} %add.221), channel_id=1, source_target_pairs={{0,2},{1,3},{2,0},{3,1},{4,6},{5,7},{6,4},{7,5},{8,10},{9,11},{10,... | collective-permute-start | bytes 344 | tf_op jit(solution)/shard_map/ppermute | solution.py:51
  110.6 1.7 %collective-permute-done.18 = f32[4,7]{1,0:T(4,128)S(1)} collective-permute-done((f32[4,7]{1,0:T(4,128)S(1)}, f32[4,7]{1,0:T(4,128)S(1)}, u32[]{:S(2)}, u32[]{:S(2)}) %collective-permute-start.18) | collective-permute-done | bytes 144 | tf_op jit(solution)/shard_map/ppermute | solution.py:51
  112.3 2.9 %collective-permute-start.19 = (f32[4,7]{1,0:T(4,128)S(1)}, f32[4,7]{1,0:T(4,128)S(1)}, u32[]{:S(2)}, u32[]{:S(2)}) collective-permute-start(f32[4,7]{1,0:T(4,128)S(1)} %add.222), channel_id=1, source_target_pairs={{0,4},{1,5},{2,6},{3,7},{4,0},{5,1},{6,2},{7,3},{8,12},{9,13},{10,... | collective-permute-start | bytes 344 | tf_op jit(solution)/shard_map/ppermute | solution.py:51
  115.2 1.6 %collective-permute-done.19 = f32[4,7]{1,0:T(4,128)S(1)} collective-permute-done((f32[4,7]{1,0:T(4,128)S(1)}, f32[4,7]{1,0:T(4,128)S(1)}, u32[]{:S(2)}, u32[]{:S(2)}) %collective-permute-start.19) | collective-permute-done | bytes 144 | tf_op jit(solution)/shard_map/ppermute | solution.py:51
  116.7 2.0 %collective-permute-start.20 = (f32[4,7]{1,0:T(4,128)S(1)}, f32[4,7]{1,0:T(4,128)S(1)}, u32[]{:S(2)}, u32[]{:S(2)}) collective-permute-start(f32[4,7]{1,0:T(4,128)S(1)} %add.223), channel_id=1, source_target_pairs={{0,8},{8,0},{16,24},{24,16},{1,9},{9,1},{17,25},{25,17},{2,10},{10... | collective-permute-start | bytes 344 | tf_op jit(solution)/shard_map/ppermute | solution.py:51
  118.7 1.6 %collective-permute-done.20 = f32[4,7]{1,0:T(4,128)S(1)} collective-permute-done((f32[4,7]{1,0:T(4,128)S(1)}, f32[4,7]{1,0:T(4,128)S(1)}, u32[]{:S(2)}, u32[]{:S(2)}) %collective-permute-start.20) | collective-permute-done | bytes 144 | tf_op jit(solution)/shard_map/ppermute | solution.py:51
  120.3 2.0 %collective-permute-start.21 = (f32[4,7]{1,0:T(4,128)S(1)}, f32[4,7]{1,0:T(4,128)S(1)}, u32[]{:S(2)}, u32[]{:S(2)}) collective-permute-start(f32[4,7]{1,0:T(4,128)S(1)} %add.224), channel_id=1, source_target_pairs={{0,16},{8,24},{16,0},{24,8},{1,17},{9,25},{17,1},{25,9},{2,18},{10... | collective-permute-start | bytes 344 | tf_op jit(solution)/shard_map/ppermute | solution.py:51
  122.3 1.6 %collective-permute-done.21 = f32[4,7]{1,0:T(4,128)S(1)} collective-permute-done((f32[4,7]{1,0:T(4,128)S(1)}, f32[4,7]{1,0:T(4,128)S(1)}, u32[]{:S(2)}, u32[]{:S(2)}) %collective-permute-start.21) | collective-permute-done | bytes 144 | tf_op jit(solution)/shard_map/ppermute | solution.py:51
  (84 shorter events, 31.0 us)
Async XLA Ops:
  0.6 11.5 %copy-start = (f32[16,16]{1,0:T(8,128)S(1)}, f32[16,16]{1,0:T(8,128)}, u32[]{:S(2)}) copy-start(f32[16,16]{1,0:T(8,128)} %param.7) | copy-start | bytes 3076
  1.6 23.3 %collective-permute-start.2 = (f32[2,2048]{1,0:T(2,128)S(1)}, f32[2,2048]{1,0:T(2,128)S(1)}, u32[]{:S(2)}, u32[]{:S(2)}) collective-permute-start(f32[2,2048]{1,0:T(2,128)S(1)} %get-tuple-element.49), channel_id=1, source_target_pairs={{0,1},{1,2},{2,3},{3,4},{4,5},{5,6},{6,7},{8,9},{9,10},{10,11},{11... | collective-permute-start | bytes 49160 | tf_op jit(solution)/shard_map/ppermute | solution.py:71
  4.0 8.9 %copy-start.1 = (f32[8,2048]{1,0:T(8,128)S(1)}, f32[8,2048]{1,0:T(8,128)}, u32[]{:S(2)}) copy-start(f32[8,2048]{1,0:T(8,128)} %param.6) | copy-start | bytes 196612
  4.0 20.9 %collective-permute-start.3 = (f32[2,2048]{1,0:T(2,128)S(1)}, f32[2,2048]{1,0:T(2,128)S(1)}, u32[]{:S(2)}, u32[]{:S(2)}) collective-permute-start(f32[2,2048]{1,0:T(2,128)S(1)} %get-tuple-element.50), channel_id=1, source_target_pairs={{1,0},{2,1},{3,2},{4,3},{5,4},{6,5},{7,6},{9,8},{10,9},{11,10},{12... | collective-permute-start | bytes 49160 | tf_op jit(solution)/shard_map/ppermute | solution.py:72
  7.6 12.7 %all-to-all-start = ((bf16[4,4,8,2048]{3,2,1,0:T(8,128)(2,1)}), bf16[4,4,8,2048]{3,2,1,0:T(8,128)(2,1)S(1)}, u32[]{:S(2)}, u32[]{:S(2)}) async-start(bf16[4,4,8,2048]{3,2,1,0:T(8,128)(2,1)} %multiply_convert_fusion), calls=%async_computation | async-start | bytes 1048576 | tf_op jit(solution)/shard_map/all_to_all | solution.py:80
  20.6 4.4 %collective-permute-start = (bf16[1,16,2,2048]{3,1,2,0:T(8,128)(2,1)S(1)}, bf16[1,16,2,2048]{3,1,2,0:T(8,128)(2,1)S(1)}, u32[]{:S(2)}, u32[]{:S(2)}) collective-permute-start(bf16[1,16,2,2048]{3,1,2,0:T(8,128)(2,1)S(1)} %get-tuple-element.47), channel_id=1, source_target_pairs={{0,1},{1,2},{2,3},{3,4},{4,5},{5,6},{6,7},{8,9},{9,10},{10,11},{11... | collective-permute-start | bytes 393224 | tf_op jit(solution)/shard_map/ppermute | solution.py:71
  23.6 5.9 %collective-permute-start.1 = (bf16[1,16,2,2048]{3,1,2,0:T(8,128)(2,1)S(1)}, bf16[1,16,2,2048]{3,1,2,0:T(8,128)(2,1)S(1)}, u32[]{:S(2)}, u32[]{:S(2)}) collective-permute-start(bf16[1,16,2,2048]{3,1,2,0:T(8,128)(2,1)S(1)} %get-tuple-element.48), channel_id=1, source_target_pairs={{1,0},{2,1},{3,2},{4,3},{5,4},{6,5},{7,6},{9,8},{10,9},{11,10},{12... | collective-permute-start | bytes 393224 | tf_op jit(solution)/shard_map/ppermute | solution.py:72
  34.9 9.3 %collective-permute-start.5 = (f32[1,16,2,2048]{3,1,2,0:T(8,128)S(1)}, f32[1,16,2,2048]{3,1,2,0:T(8,128)S(1)}, u32[]{:S(2)}, u32[]{:S(2)}) collective-permute-start(f32[1,16,2,2048]{3,1,2,0:T(8,128)S(1)} %get-tuple-element.45), channel_id=1, source_target_pairs={{0,1},{1,2},{2,3},{3,4},{4,5},{5,6},{6,7},{8,9},{9,10},{10,11},{11... | collective-permute-start | bytes 786440 | tf_op jit(solution)/shard_map/ppermute | solution.py:71
  40.4 3.8 %collective-permute-start.6 = (f32[1,16,2,2048]{3,1,2,0:T(8,128)S(1)}, f32[1,16,2,2048]{3,1,2,0:T(8,128)S(1)}, u32[]{:S(2)}, u32[]{:S(2)}) collective-permute-start(f32[1,16,2,2048]{3,1,2,0:T(8,128)S(1)} %get-tuple-element.46), channel_id=1, source_target_pairs={{1,0},{2,1},{3,2},{4,3},{5,4},{6,5},{7,6},{9,8},{10,9},{11,10},{12... | collective-permute-start | bytes 786440 | tf_op jit(solution)/shard_map/ppermute | solution.py:72
  42.2 1.9 %collective-permute-start.4 = (f32[1,2]{1,0:T(1,128)S(1)}, f32[1,2]{1,0:T(1,128)S(1)}, u32[]{:S(2)}, u32[]{:S(2)}) collective-permute-start(f32[1,2]{1,0:T(1,128)S(1)} %bitcast.78), channel_id=1, source_target_pairs={{0,1},{1,0},{2,3},{3,2},{4,5},{5,4},{6,7},{7,6},{8,9},{9,8},{10,11... | collective-permute-start | bytes 32 | tf_op jit(solution)/shard_map/ppermute | solution.py:51
  46.4 5.2 %collective-permute-start.7 = (f32[1,2]{1,0:T(1,128)S(1)}, f32[1,2]{1,0:T(1,128)S(1)}, u32[]{:S(2)}, u32[]{:S(2)}) collective-permute-start(f32[1,2]{1,0:T(1,128)S(1)} %bitcast_add_fusion.2), channel_id=1, source_target_pairs={{0,2},{1,3},{2,0},{3,1},{4,6},{5,7},{6,4},{7,5},{8,10},{9,11},{10,... | collective-permute-start | bytes 32 | tf_op jit(solution)/shard_map/ppermute | solution.py:51
  54.2 4.6 %collective-permute-start.8 = (f32[1,2]{1,0:T(1,128)S(1)}, f32[1,2]{1,0:T(1,128)S(1)}, u32[]{:S(2)}, u32[]{:S(2)}) collective-permute-start(f32[1,2]{1,0:T(1,128)S(1)} %add.193), channel_id=1, source_target_pairs={{0,4},{1,5},{2,6},{3,7},{4,0},{5,1},{6,2},{7,3},{8,12},{9,13},{10,... | collective-permute-start | bytes 32 | tf_op jit(solution)/shard_map/ppermute | solution.py:51
  61.6 7.3 %collective-permute-start.10 = (f32[1,16,2,2048]{3,1,2,0:T(8,128)S(1)}, f32[1,16,2,2048]{3,1,2,0:T(8,128)S(1)}, u32[]{:S(2)}, u32[]{:S(2)}) collective-permute-start(f32[1,16,2,2048]{3,1,2,0:T(8,128)S(1)} %get-tuple-element.42), channel_id=1, source_target_pairs={{0,1},{1,2},{2,3},{3,4},{4,5},{5,6},{6,7},{8,9},{9,10},{10,11},{11... | collective-permute-start | bytes 786440 | tf_op jit(solution)/shard_map/ppermute | solution.py:71
  63.4 5.5 %collective-permute-start.11 = (f32[1,16,2,2048]{3,1,2,0:T(8,128)S(1)}, f32[1,16,2,2048]{3,1,2,0:T(8,128)S(1)}, u32[]{:S(2)}, u32[]{:S(2)}) collective-permute-start(f32[1,16,2,2048]{3,1,2,0:T(8,128)S(1)} %get-tuple-element.43), channel_id=1, source_target_pairs={{1,0},{2,1},{3,2},{4,3},{5,4},{6,5},{7,6},{9,8},{10,9},{11,10},{12... | collective-permute-start | bytes 786440 | tf_op jit(solution)/shard_map/ppermute | solution.py:72
  65.3 3.6 %collective-permute-start.9 = (f32[1,3]{1,0:T(1,128)S(1)}, f32[1,3]{1,0:T(1,128)S(1)}, u32[]{:S(2)}, u32[]{:S(2)}) collective-permute-start(f32[1,3]{1,0:T(1,128)S(1)} %bitcast.79), channel_id=1, source_target_pairs={{0,1},{1,0},{2,3},{3,2},{4,5},{5,4},{6,7},{7,6},{8,9},{9,8},{10,11... | collective-permute-start | bytes 44 | tf_op jit(solution)/shard_map/ppermute | solution.py:51
  71.2 5.6 %collective-permute-start.12 = (f32[1,3]{1,0:T(1,128)S(1)}, f32[1,3]{1,0:T(1,128)S(1)}, u32[]{:S(2)}, u32[]{:S(2)}) collective-permute-start(f32[1,3]{1,0:T(1,128)S(1)} %bitcast_add_fusion.1), channel_id=1, source_target_pairs={{0,2},{1,3},{2,0},{3,1},{4,6},{5,7},{6,4},{7,5},{8,10},{9,11},{10,... | collective-permute-start | bytes 44 | tf_op jit(solution)/shard_map/ppermute | solution.py:51
  79.3 4.7 %collective-permute-start.13 = (f32[1,3]{1,0:T(1,128)S(1)}, f32[1,3]{1,0:T(1,128)S(1)}, u32[]{:S(2)}, u32[]{:S(2)}) collective-permute-start(f32[1,3]{1,0:T(1,128)S(1)} %add.205), channel_id=1, source_target_pairs={{0,4},{1,5},{2,6},{3,7},{4,0},{5,1},{6,2},{7,3},{8,12},{9,13},{10,... | collective-permute-start | bytes 44 | tf_op jit(solution)/shard_map/ppermute | solution.py:51
  88.0 1.2 collective-permute-start.14
  89.2 3.6 %collective-permute-start.15 = (f32[1,3]{1,0:T(1,128)S(1)}, f32[1,3]{1,0:T(1,128)S(1)}, u32[]{:S(2)}, u32[]{:S(2)}) collective-permute-start(f32[1,3]{1,0:T(1,128)S(1)} %bitcast_add_fusion), channel_id=1, source_target_pairs={{0,2},{1,3},{2,0},{3,1},{4,6},{5,7},{6,4},{7,5},{8,10},{9,11},{10,... | collective-permute-start | bytes 44 | tf_op jit(solution)/shard_map/ppermute | solution.py:51
  92.7 4.5 %collective-permute-start.16 = (f32[1,3]{1,0:T(1,128)S(1)}, f32[1,3]{1,0:T(1,128)S(1)}, u32[]{:S(2)}, u32[]{:S(2)}) collective-permute-start(f32[1,3]{1,0:T(1,128)S(1)} %add.217), channel_id=1, source_target_pairs={{0,4},{1,5},{2,6},{3,7},{4,0},{5,1},{6,2},{7,3},{8,12},{9,13},{10,... | collective-permute-start | bytes 44 | tf_op jit(solution)/shard_map/ppermute | solution.py:51
  102.3 22.6 %all-to-all-start.1 = ((f32[1,16,8,2048]{3,2,0,1:T(8,128)}), f32[1,16,8,2048]{3,2,0,1:T(8,128)S(1)}, u32[]{:S(2)}, u32[]{:S(2)}) async-start(f32[1,16,8,2048]{3,2,0,1:T(8,128)} %copy.12), calls=%async_computation.1 | async-start | bytes 2097152 | tf_op jit(solution)/shard_map/all_to_all | solution.py:143
  106.7 1.2 collective-permute-start.17
  108.6 3.6 %collective-permute-start.18 = (f32[4,7]{1,0:T(4,128)S(1)}, f32[4,7]{1,0:T(4,128)S(1)}, u32[]{:S(2)}, u32[]{:S(2)}) collective-permute-start(f32[4,7]{1,0:T(4,128)S(1)} %add.221), channel_id=1, source_target_pairs={{0,2},{1,3},{2,0},{3,1},{4,6},{5,7},{6,4},{7,5},{8,10},{9,11},{10,... | collective-permute-start | bytes 344 | tf_op jit(solution)/shard_map/ppermute | solution.py:51
  112.3 4.5 %collective-permute-start.19 = (f32[4,7]{1,0:T(4,128)S(1)}, f32[4,7]{1,0:T(4,128)S(1)}, u32[]{:S(2)}, u32[]{:S(2)}) collective-permute-start(f32[4,7]{1,0:T(4,128)S(1)} %add.222), channel_id=1, source_target_pairs={{0,4},{1,5},{2,6},{3,7},{4,0},{5,1},{6,2},{7,3},{8,12},{9,13},{10,... | collective-permute-start | bytes 344 | tf_op jit(solution)/shard_map/ppermute | solution.py:51
  116.7 3.6 %collective-permute-start.20 = (f32[4,7]{1,0:T(4,128)S(1)}, f32[4,7]{1,0:T(4,128)S(1)}, u32[]{:S(2)}, u32[]{:S(2)}) collective-permute-start(f32[4,7]{1,0:T(4,128)S(1)} %add.223), channel_id=1, source_target_pairs={{0,8},{8,0},{16,24},{24,16},{1,9},{9,1},{17,25},{25,17},{2,10},{10... | collective-permute-start | bytes 344 | tf_op jit(solution)/shard_map/ppermute | solution.py:51
  120.3 3.6 %collective-permute-start.21 = (f32[4,7]{1,0:T(4,128)S(1)}, f32[4,7]{1,0:T(4,128)S(1)}, u32[]{:S(2)}, u32[]{:S(2)}) collective-permute-start(f32[4,7]{1,0:T(4,128)S(1)} %add.224), channel_id=1, source_target_pairs={{0,16},{8,24},{16,0},{24,8},{1,17},{9,25},{17,1},{25,9},{2,18},{10... | collective-permute-start | bytes 344 | tf_op jit(solution)/shard_map/ppermute | solution.py:51
  123.9 2.2 %copy-start.2 = (f32[4,7]{1,0:T(4,128)}, f32[4,7]{1,0:T(4,128)S(1)}, u32[]{:S(2)}) copy-start(f32[4,7]{1,0:T(4,128)S(1)} %add.225) | copy-start | bytes 340
